TPU v7x, 256 devices: a whole 4x4x8 slice. The times are simulated.
256 devices in a mesh: bus: 16 (over y, z_hi), line: 16 (over z_lo, x, core).
Axes of the slice: x: 4, y: 4, z: 8 (z_hi: 4, z_lo: 2; z = z_hi * 2 + z_lo), core: 2. Of those that a mesh axis runs over, the one named last changes fastest.
Arguments:
- generation: bfloat16 [1024, 16384], P(None, 'bus'), may hold values from -6 to 6
- profiles: float32 [24, 16384], P(None, 'bus'), may hold values from -5 to 5
- scen_profile: int32 [1024], replicated, may hold values from 0 to 23
- ptdf: bfloat16 [16384, 16384], P('line', 'bus'), may hold values from -0.046875 to 0.046875
- lodf: float32 [6144, 512], P('line'), may hold values from -1 to 1
- limits: float32 [6144], P('line'), may hold values from 0.5 to 2
- monitored: int32 [6144], P('line'), may hold values from 0 to 16383, as said below
- outages: int32 [512], replicated, may hold values from 0 to 16383, as said below
- cost_quad: float32 [16384], P('bus'), may hold values from 0.5 to 2
Outputs:
- gradient: bfloat16 [1024, 16384], P('line', 'bus')
- outage_flow: float32 [1024, 512], P('bus')
- outage_sens: float32 [1024, 512], P('bus')
Inputs may be any that keep to these rules, and one draw needn't show every extreme that they name: `monitored`: the entries with positions k * 384 to (k + 1) * 384 - 1 are distinct line ids of the k-th block of 1024 lines (ids k * 1024 to (k + 1) * 1024 - 1). `outages`: distinct line ids; how many fall in each block of 1024 lines varies from block to block.
All inputs are finite; a program needn't handle non-finite values.
Results may differ from a plain program's by a relative error of at most 0.0029.
Values may be sent and summed in bfloat16 or wider, within the bound.
No kernel may reach another device: no remote copies, remote signals or barrier semaphores. Data moves between devices by JAX's collectives and lax.ppermute only.
A program may use at most 64 MiB of HBM per device.

v0:
```python
import math

import jax
import jax.numpy as jnp
from jax import lax
from jax.sharding import PartitionSpec as P

sharpness = 4.0


def contingency(pieces, lodf, limits, outage_total):
    base_block, outage_block = pieces
    post_flow = base_block[:, :, None] + lodf[None, :, :] * outage_block[:, None, :]
    bounds = limits[None, :, None]
    raw_slope = jax.nn.sigmoid(sharpness * (post_flow - bounds)) - jax.nn.sigmoid(
        sharpness * (-post_flow - bounds)
    )
    direct = jnp.sum(raw_slope, axis=2) / outage_total
    sens_part = jnp.einsum("smk,mk->sk", raw_slope, lodf, precision=lax.Precision.HIGHEST)
    return (direct, sens_part)


def on_device(
    generation, profiles, scen_profile, ptdf, lodf, limits, monitored, outages, cost_quad
):
    profile_count = profiles.shape[0]
    profile_pick = (
        scen_profile[:, None] == jnp.arange(profile_count, dtype=jnp.int32)[None, :]
    ).astype(jnp.float32)
    loads = jnp.dot(profile_pick, profiles, precision=lax.Precision.HIGHEST)
    injection = (generation.astype(jnp.float32) - loads).astype(jnp.bfloat16)
    scen_rows = injection.shape[0] // lax.axis_size("bus")
    line_rows = ptdf.shape[0]
    first_line = lax.axis_index("line") * line_rows
    local_monitored = monitored - first_line
    positions = jnp.arange(line_rows, dtype=jnp.int32)
    picker = ((outages - first_line)[None, :] == positions[:, None]).astype(jnp.float32)
    monitor_count = monitored.shape[0]
    inputs = injection
    flow_field = lax.psum_scatter(
        lax.dot_general(inputs, ptdf, (((1,), (1,)), ((), ())), preferred_element_type=jnp.float32),
        "bus",
        scatter_dimension=0,
        tiled=True,
    )
    base = jnp.take(flow_field, local_monitored, axis=1)
    entire_flows = lax.all_gather(flow_field, "line", axis=1, tiled=True)
    outflow = jnp.take(entire_flows, outages, axis=1)
    outage_total = outages.shape[0]
    monitored_total = monitor_count * lax.axis_size("line")
    block_size = math.gcd(scen_rows, 4)
    base_blocks = base.reshape(scen_rows // block_size, block_size, monitor_count)
    outage_blocks = outflow.reshape(scen_rows // block_size, block_size, outage_total)
    direct, sens_part = lax.map(
        lambda pieces: contingency(pieces, lodf, limits, outage_total), (base_blocks, outage_blocks)
    )
    direct = direct.reshape(scen_rows, monitor_count)
    sens_part = sens_part.reshape(scen_rows, outage_total)
    sens_total = lax.psum(sens_part, "line")
    backward = sens_total / outage_total
    outage_sens = sens_total / math.sqrt(monitored_total)
    adjoint = jnp.zeros((scen_rows, line_rows), jnp.float32).at[:, local_monitored].add(direct)
    adjoint = adjoint + jnp.dot(backward, picker.T, precision=lax.Precision.HIGHEST)
    adjoint_half = adjoint.astype(jnp.bfloat16)
    all_adjoint = lax.all_gather(adjoint_half, "bus", axis=0, tiled=True)
    grad_rows = all_adjoint.shape[0] // lax.axis_size("line")
    inputs = all_adjoint
    pushed = lax.psum_scatter(
        jnp.dot(inputs, ptdf, preferred_element_type=jnp.float32),
        "line",
        scatter_dimension=0,
        tiled=True,
    )
    own_generation = lax.dynamic_slice_in_dim(
        generation, lax.axis_index("line") * grad_rows, grad_rows, 0
    ).astype(jnp.float32)
    gradient = (cost_quad[None, :] * own_generation + pushed).astype(jnp.bfloat16)
    return (gradient, outflow, outage_sens)


def solution(mesh):
    placed = (
        P(None, "bus"),
        P(None, "bus"),
        P(),
        P("line", "bus"),
        P("line", None),
        P("line"),
        P("line"),
        P(),
        P("bus"),
    )
    return jax.shard_map(
        on_device,
        mesh=mesh,
        in_specs=placed,
        out_specs=(P("line", "bus"), P("bus", None), P("bus", None)),
        check_vma=False,
    )
```

profile of v0, /device:TPU:7, one launch (start us, length us, event | category | flops | bytes accessed | tf_op | source)
XLA Modules:
  0.0 544.0 jit_solution(11208969200925676231)
XLA Ops:
  7.2 0.0 reduce-scatter.3.cloned.1.call-start
  7.2 3.7 subtract_convert_fusion
  11.0 4.4 fusion.9
  15.3 0.0 reduce-scatter.3.cloned.1.call-update
  15.4 0.0 all-gather.3.cloned.1.call-start
  15.4 98.2 %reduce-scatter.3.cloned.1.call-done = f32[64,1024]{1,0:T(8,128)} async-done(((f32[1024,1024]{1,0:T(8,128)}), f32[64,1024]{1,0:T(8,128)}) %reduce-scatter.3.cloned.1.call-update) | async-done | bytes 262160 | tf_op jit(solution)/shard_map/reduce_scatter | solution.py:40
  113.6 0.0 all-gather.3.cloned.1.call-update
  113.6 0.0 all-reduce.2.cloned.1.call-start
  113.8 1.1 copy.40
  114.9 1.1 gather_fusion
  116.1 0.1 copy.41
  116.3 37.8 %all-gather.3.cloned.1.call-done = f32[64,16384]{1,0:T(8,128)} async-done(((f32[64,1024]{1,0:T(8,128)}), f32[64,16384]{1,0:T(8,128)}) %all-gather.3.cloned.1.call-update) | async-done | bytes 4194320 | tf_op jit(solution)/shard_map/all_gather | solution.py:47
  154.0 6.9 %copy.42 = f32[64,16384]{0,1:T(8,128)} copy(f32[64,16384]{1,0:T(8,128)} %all-gather.3.cloned.1.call-done) | data formatting | bytes 8388608 | tf_op jit(solution)/shard_map/all_gather | solution.py:47
  160.9 4.4 gather_fusion.1
  165.4 0.1 copy.43
  165.6 108.0 %while.12 = (s32[]{:T(128)}, f32[16,4,384]{2,1,0:T(4,128)S(1)}, f32[16,4,512]{2,1,0:T(4,128)S(1)}, f32[16,4,384]{2,1,0:T(4,128)S(1)}, f32[384,512]{1,0:T(8,128)}...) while((s32[]{:T(128)}, f32[16,4,384]{2,1,0:T(4,128)S(1)}, f32[16,4,512]{2,1,0:T(4,128)S(1)}, ...), condition=%wide.region_3.4_spmd, body=%wide.region_1.0_spmd.sunk | while | flops 24377344 | bytes 2462821 | solution.py:54
  165.6 3.3 multiply_reduce_fusion.2
  169.0 3.3 fusion.17
  172.4 3.3 multiply_reduce_fusion.2
  175.7 3.3 fusion.17
  179.1 3.3 multiply_reduce_fusion.2
  182.5 3.3 fusion.17
  185.9 3.3 multiply_reduce_fusion.2
  189.2 3.3 fusion.17
  192.6 3.3 multiply_reduce_fusion.2
  195.9 3.3 fusion.17
  199.4 3.3 multiply_reduce_fusion.2
  202.7 3.3 fusion.17
  206.1 3.3 multiply_reduce_fusion.2
  209.4 3.3 fusion.17
  212.9 3.3 multiply_reduce_fusion.2
  216.2 3.3 fusion.17
  219.6 3.3 multiply_reduce_fusion.2
  222.9 3.3 fusion.17
  226.4 3.3 multiply_reduce_fusion.2
  229.7 3.3 fusion.17
  233.1 3.3 multiply_reduce_fusion.2
  236.4 3.3 fusion.17
  239.9 3.3 multiply_reduce_fusion.2
  243.2 3.3 fusion.17
  246.6 3.3 multiply_reduce_fusion.2
  249.9 3.3 fusion.17
  253.4 3.3 multiply_reduce_fusion.2
  256.7 3.3 fusion.17
  260.1 3.3 multiply_reduce_fusion.2
  263.4 3.3 fusion.17
  266.8 3.3 multiply_reduce_fusion.2
  270.2 3.3 fusion.17
  273.6 0.7 reshape.54
  274.3 0.0 all-reduce.2.cloned.1.call-update
  274.3 0.0 all-gather.5.cloned.1.call-start
  274.4 0.1 copy.44
  274.5 123.4 %all-reduce.2.cloned.1.call-done = f32[64,512]{1,0:T(8,128)} async-done(((f32[64,512]{1,0:T(8,128)}), f32[64,512]{1,0:T(8,128)}) %all-reduce.2.cloned.1.call-update) | async-done | bytes 131088 | tf_op jit(solution)/shard_map/psum | solution.py:59
  397.9 1.9 fusion.1
  399.8 2.8 scatter_custom_fusion
  402.7 0.8 copy.46
  403.5 0.0 reduce-scatter.5.cloned.1.call-start
  403.5 58.9 %all-gather.5.cloned.1.call-done = bf16[1024,1024]{1,0:T(8,128)(2,1)} async-done(((bf16[64,1024]{1,0:T(8,128)(2,1)}), bf16[1024,1024]{1,0:T(8,128)(2,1)}) %all-gather.5.cloned.1.call-update) | async-done | bytes 2097168 | tf_op jit(solution)/shard_map/all_gather | solution.py:65
  462.4 5.9 %fusion.10 = f32[1024,1024]{1,0:T(8,128)} fusion(bf16[1024,1024]{1,0:T(8,128)(2,1)} %all-gather.5.cloned.1.call-done, bf16[1024,1024]{1,0:T(8,128)(2,1)S(1)} %copy-done), kind=kOutput, calls=%fused_computation.34 | convolution fusion | flops 2147483648 | bytes 8388608 | tf_op jit(solution)/shard_map/dot_general | solution.py:69
  468.3 0.1 broadcast_select_fusion
  468.4 0.8 copy.47
  469.2 0.7 broadcast_multiply_fusion
  469.9 66.0 %reduce-scatter.5.cloned.1.call-done = f32[64,1024]{1,0:T(8,128)} async-done(((f32[1024,1024]{1,0:T(8,128)}), f32[64,1024]{1,0:T(8,128)}) %reduce-scatter.5.cloned.1.call-update) | async-done | bytes 262160 | tf_op jit(solution)/shard_map/reduce_scatter | solution.py:68
  535.8 1.7 add_convert_fusion
  (90 shorter events, 1.0 us)
Async XLA Ops:
  7.2 3.8 copy-start
  7.2 106.4 %reduce-scatter.3.cloned.1.call-start = ((), (), s32[]{:S(2)}) async-start(), calls=%async_computation.2 | async-start | bytes 4456448 | tf_op jit(solution)/shard_map/reduce_scatter | solution.py:40
  15.3 98.4 %copy-start.4 = (s32[384]{0:T(512)S(1)}, s32[384]{0:T(512)}, u32[]{:S(2)}) copy-start(s32[384]{0:T(512)} %param.17) | copy-start | bytes 4612
  15.3 98.4 %copy-start.2 = (s32[512]{0:T(512)S(1)}, s32[512]{0:T(512)}, u32[]{:S(2)}) copy-start(s32[512]{0:T(512)} %param.18) | copy-start | bytes 6148
  15.4 138.7 %all-gather.3.cloned.1.call-start = ((), (), s32[]{:S(2)}) async-start(), calls=%async_computation.3 | async-start | bytes 4456448 | tf_op jit(solution)/shard_map/all_gather | solution.py:47
  113.6 284.3 %all-reduce.2.cloned.1.call-start = ((), (), s32[]{:S(2)}) async-start(), calls=%async_computation.4 | async-start | bytes 262144 | tf_op jit(solution)/shard_map/psum | solution.py:59
  116.3 49.3 %copy-start.5 = (f32[384]{0:T(512)S(1)}, f32[384]{0:T(512)}, u32[]{:S(2)}) copy-start(f32[384]{0:T(512)} %param.16) | copy-start | bytes 4612
  274.3 188.1 %all-gather.5.cloned.1.call-start = ((), (), s32[]{:S(2)}) async-start(), calls=%async_computation.5 | async-start | bytes 2228224 | tf_op jit(solution)/shard_map/all_gather | solution.py:65
  403.5 132.4 %reduce-scatter.5.cloned.1.call-start = ((), (), s32[]{:S(2)}) async-start(), calls=%async_computation.6 | async-start | bytes 4456448 | tf_op jit(solution)/shard_map/reduce_scatter | solution.py:68
  468.2 1.0 copy-start.1
  468.2 67.6 %copy-start.3 = (f32[1024]{0:T(1024)S(1)}, f32[1024]{0:T(1024)}, u32[]{:S(2)}) copy-start(f32[1024]{0:T(1024)} %param.19) | copy-start | bytes 12292
Sparse Core Ops, SparseCore 0:
  15.5 98.0 reduce-scatter.2
  115.4 38.5 all-gather.2
  274.4 123.4 all-reduce.1
  403.6 58.7 all-gather.4
  468.4 67.3 reduce-scatter.4
where the time goes:
time: 547 us; the launch traced here: 544 us
  waiting for transfers between devices  384 us (70%)
  other arithmetic  112 us (20%)
  local copies, waits for them, and re-layouts  16.8 us (3%)
  matrix products  15.9 us (3%)
  between operations  14 us (3%)
    psum x1, waiting for transfers between devices, on_device(): sens_total = lax.psum(sens_part, 'line')  123 us
    reduce_scatter x1, waiting for transfers between devices, on_device(): lax.psum_scatter(lax.dot_general(inputs, ptdf, (((1,), (1,)), ((), ())),...  98.2 us
    reduce_scatter x1, waiting for transfers between devices, on_device(): lax.psum_scatter(jnp.dot(inputs, ptdf, preferred_element_type=jnp.float32...  66 us
    all_gather x1, waiting for transfers between devices, on_device(): all_adjoint = lax.all_gather(adjoint_half, 'bus', axis=0, tiled=True)  58.9 us
    reduce_sum x16, other arithmetic, contingency(): direct = jnp.sum(raw_slope, axis=2) / outage_total  53.5 us
    dot_general x16, other arithmetic, contingency(): jnp.einsum('smk,mk->sk', raw_slope, lodf, precision=lax.Precision.HIGHEST)  53.1 us
    all_gather x1, waiting for transfers between devices, on_device(): entire_flows = lax.all_gather(flow_field, 'line', axis=1, tiled=True)  37.8 us
  transfers between devices with their start and end apart: 5, of which 5 were waited for; matrix products, arithmetic and copies ran while one was open for 1% of the time, Pallas kernels for 0%

commit v1 on v0

--- a/solution.py
+++ b/solution.py
@@ -23,6 +23,7 @@
 def on_device(
     generation, profiles, scen_profile, ptdf, lodf, limits, monitored, outages, cost_quad
 ):
+    line_count = lax.axis_size("line")
     profile_count = profiles.shape[0]
     profile_pick = (
         scen_profile[:, None] == jnp.arange(profile_count, dtype=jnp.int32)[None, :]
@@ -33,21 +34,28 @@
     line_rows = ptdf.shape[0]
     first_line = lax.axis_index("line") * line_rows
     local_monitored = monitored - first_line
-    positions = jnp.arange(line_rows, dtype=jnp.int32)
-    picker = ((outages - first_line)[None, :] == positions[:, None]).astype(jnp.float32)
     monitor_count = monitored.shape[0]
-    inputs = injection
-    flow_field = lax.psum_scatter(
-        lax.dot_general(inputs, ptdf, (((1,), (1,)), ((), ())), preferred_element_type=jnp.float32),
-        "bus",
-        scatter_dimension=0,
-        tiled=True,
+    outage_total = outages.shape[0]
+    monitored_total = monitor_count * line_count
+
+    rel_outages = outages - first_line
+    in_block = (rel_outages >= 0) & (rel_outages < line_rows)
+    outage_rows = jnp.where(
+        in_block[:, None],
+        jnp.take(ptdf, jnp.clip(rel_outages, 0, line_rows - 1), axis=0),
+        jnp.zeros((), ptdf.dtype),
     )
-    base = jnp.take(flow_field, local_monitored, axis=1)
-    entire_flows = lax.all_gather(flow_field, "line", axis=1, tiled=True)
-    outflow = jnp.take(entire_flows, outages, axis=1)
-    outage_total = outages.shape[0]
-    monitored_total = monitor_count * lax.axis_size("line")
+    my_outage_rows = lax.psum_scatter(outage_rows, "line", scatter_dimension=0, tiled=True)
+    monitored_rows = jnp.take(ptdf, local_monitored, axis=0)
+    rows = jnp.concatenate([monitored_rows, my_outage_rows], axis=0)
+
+    flow_part = lax.dot_general(
+        injection, rows, (((1,), (1,)), ((), ())), preferred_element_type=jnp.float32
+    )
+    flow_field = lax.psum_scatter(flow_part, "bus", scatter_dimension=0, tiled=True)
+    base = flow_field[:, :monitor_count]
+    outflow = lax.all_gather(flow_field[:, monitor_count:], "line", axis=1, tiled=True)
+
     block_size = math.gcd(scen_rows, 4)
     base_blocks = base.reshape(scen_rows // block_size, block_size, monitor_count)
     outage_blocks = outflow.reshape(scen_rows // block_size, block_size, outage_total)
@@ -56,17 +64,30 @@
     )
     direct = direct.reshape(scen_rows, monitor_count)
     sens_part = sens_part.reshape(scen_rows, outage_total)
-    sens_total = lax.psum(sens_part, "line")
+
+    matches = (outages[:, None] == monitored[None, :]).astype(jnp.float32)
+    flag_part = jnp.sum(matches, axis=1)
+    extended = jnp.concatenate(
+        [sens_part, flag_part[None, :], jnp.zeros((7, outage_total), jnp.float32)], axis=0
+    )
+    mine = lax.psum_scatter(extended, "line", scatter_dimension=1, tiled=True)
+    sens_mine = mine[:scen_rows]
+    flag_mine = mine[scen_rows]
+    sens_total = lax.all_gather(sens_mine, "line", axis=1, tiled=True)
     backward = sens_total / outage_total
     outage_sens = sens_total / math.sqrt(monitored_total)
-    adjoint = jnp.zeros((scen_rows, line_rows), jnp.float32).at[:, local_monitored].add(direct)
-    adjoint = adjoint + jnp.dot(backward, picker.T, precision=lax.Precision.HIGHEST)
-    adjoint_half = adjoint.astype(jnp.bfloat16)
-    all_adjoint = lax.all_gather(adjoint_half, "bus", axis=0, tiled=True)
-    grad_rows = all_adjoint.shape[0] // lax.axis_size("line")
-    inputs = all_adjoint
+
+    adjoint_monitored = (
+        direct + jnp.dot(backward, matches, precision=lax.Precision.HIGHEST)
+    ).astype(jnp.bfloat16)
+    adjoint_outage = jnp.where(
+        flag_mine[None, :] > 0.5, 0.0, sens_mine / outage_total
+    ).astype(jnp.bfloat16)
+    piece = jnp.concatenate([adjoint_monitored, adjoint_outage], axis=1)
+    all_piece = lax.all_gather(piece, "bus", axis=0, tiled=True)
+    grad_rows = all_piece.shape[0] // line_count
     pushed = lax.psum_scatter(
-        jnp.dot(inputs, ptdf, preferred_element_type=jnp.float32),
+        jnp.dot(all_piece, rows, preferred_element_type=jnp.float32),
         "line",
         scatter_dimension=0,
         tiled=True,

time: 547 us -> 534 us (0.976)
  waiting for transfers between devices: 384 us -> 276 us
  blocking collectives: 0 us -> 81.6 us
  other arithmetic: 112 us -> 124 us
    psum x1 -> x0, waiting for transfers between devices: 123 us -> none  [on_device(): sens_total = lax.psum(sens_part, 'line')]
    all_gather x2 -> x0, waiting for transfers between devices: 96.6 us -> none  [the longest x1 58.9 us: on_device(): all_adjoint = lax.all_gather(adjoint_half, 'bus', axis=0, tiled=True)]
    all_gather x0 -> x3, blocking collectives: none -> 81.6 us  [the longest x1 45.9 us: on_device(): all_piece = lax.all_gather(piece, 'bus', axis=0, tiled=True)]
    unnamed x5, waiting for transfers between devices: 0.08 us -> 59.5 us
    reduce_scatter x2 -> x3, waiting for transfers between devices: 164 us -> 217 us  [the longest x1 87.4 us: on_device(): lax.psum_scatter(flow_part, 'bus', scatter_dimension=0, tiled=True)]
    dynamic_update_slice x16, local copies, waits for them, and re-layouts: 0.19 us -> 9.57 us  [on_device(): lax.map(lambda pieces: contingency(pieces, lodf, limits, outage_total), (...]
    dynamic_update_slice x16, other arithmetic: 0.24 us -> 9.61 us  [on_device(): lax.map(lambda pieces: contingency(pieces, lodf, limits, outage_total), (...]
    all_gather x1, local copies, waits for them, and re-layouts: 6.9 us -> 0.11 us  [on_device(): lax.all_gather(flow_field[:, monitor_count:], 'line', axis=1, tiled=True)]
  transfers between devices with their start and end apart: 5 -> 4, of which waited for: 5 -> 4; matrix products, arithmetic and copies ran while one was open for 1% -> 2% of each run, Pallas kernels for 0% -> 0%
where the time goes in v1:
time: 534 us; the launch traced here: 530 us
  waiting for transfers between devices  276 us (52%)
  other arithmetic  124 us (23%)
  blocking collectives  81.6 us (15%)
  local copies, waits for them, and re-layouts  21.5 us (4%)
  between operations  13.9 us (3%)
  matrix products  12.8 us (2%)
    reduce_scatter x1, waiting for transfers between devices, on_device(): lax.psum_scatter(flow_part, 'bus', scatter_dimension=0, tiled=True)  87.4 us
    reduce_scatter x1, waiting for transfers between devices, on_device(): lax.psum_scatter(jnp.dot(all_piece, rows, preferred_element_type=jnp.floa...  71.2 us
    unnamed x5, waiting for transfers between devices  59.5 us
    reduce_scatter x1, waiting for transfers between devices, on_device(): lax.psum_scatter(outage_rows, 'line', scatter_dimension=0, tiled=True)  58 us
    dot_general x16, other arithmetic, contingency(): jnp.einsum('smk,mk->sk', raw_slope, lodf, precision=lax.Precision.HIGHEST)  55.3 us
    reduce_sum x16, other arithmetic, contingency(): direct = jnp.sum(raw_slope, axis=2) / outage_total  53.3 us
    all_gather x1, blocking collectives, on_device(): all_piece = lax.all_gather(piece, 'bus', axis=0, tiled=True)  45.9 us
    all_gather x1, blocking collectives, on_device(): lax.all_gather(flow_field[:, monitor_count:], 'line', axis=1, tiled=True)  18.4 us
  transfers between devices with their start and end apart: 4, of which 4 were waited for; matrix products, arithmetic and copies ran while one was open for 2% of the time, Pallas kernels for 0%

profile of v1, /device:TPU:7, one launch (start us, length us, event | category | flops | bytes accessed | tf_op | source)
XLA Modules:
  0.0 530.5 jit_solution(728160581816020870)
XLA Ops:
  7.2 0.8 compare_and_fusion
  8.1 0.7 copy-done
  8.8 2.0 gather_fusion.1
  10.8 1.2 select_select_fusion
  12.2 2.1 gather_fusion
  14.3 1.0 broadcast_select_fusion
  15.3 4.9 subtract_convert_fusion
  20.2 58.0 %reduce-scatter.7.cloned.1.call-done = bf16[32,1024]{1,0:T(8,128)(2,1)} async-done(((bf16[512,1024]{1,0:T(8,128)(2,1)}), bf16[32,1024]{1,0:T(8,128)(2,1)}) %reduce-scatter.7.cloned.1.call-update) | async-done | bytes 65552 | tf_op jit(solution)/shard_map/reduce_scatter | solution.py:48
  78.3 4.2 fusion.5
  82.9 87.4 %reduce-scatter.9.cloned.1.call-done = f32[64,416]{1,0:T(8,128)} async-done(((f32[1024,416]{1,0:T(8,128)}), f32[64,416]{1,0:T(8,128)}) %reduce-scatter.9.cloned.1.call-update) | async-done | bytes 106512 | tf_op jit(solution)/shard_map/reduce_scatter | solution.py:55
  170.3 0.8 slice.21
  171.1 0.9 slice.20
  172.1 18.4 %all_gather.9 = f32[64,512]{0,1:T(8,128)S(1)} all-gather(f32[64,32]{0,1:T(8,128)S(1)} %copy.22), channel_id=1, replica_groups=mesh['bus'=16,'line'=16] {'line'}, dimensions={1}, use_global_device_ids=true | all-gather | bytes 139264 | tf_op jit(solution)/shard_map/all_gather | solution.py:57
  191.3 128.0 %while.12 = (s32[]{:T(128)}, f32[16,4,384]{2,1,0:T(4,128)}, f32[16,4,512]{2,1,0:T(4,128)}, f32[16,4,384]{2,1,0:T(4,128)S(1)}, f32[384,512]{1,0:T(8,128)}, /*inde...) while((s32[]{:T(128)}, f32[16,4,384]{2,1,0:T(4,128)}, f32[16,4,512]{2,1,0:T(4,128)}, ...), condition=%wide.region_4.5_spmd, body=%wide.region_2.4_spmd.sunk | while | flops 24377344 | bytes 2462829 | solution.py:62
  191.3 3.3 fusion.18
  194.6 3.5 multiply_reduce_fusion.2
  198.1 0.6 bitcast_dynamic-update-slice_fusion.4
  199.3 3.3 fusion.18
  202.6 3.5 multiply_reduce_fusion.2
  206.1 0.6 bitcast_dynamic-update-slice_fusion.4
  207.3 3.3 fusion.18
  210.6 3.5 multiply_reduce_fusion.2
  215.3 3.3 fusion.18
  218.6 3.5 multiply_reduce_fusion.2
  223.3 3.3 fusion.18
  226.6 3.5 multiply_reduce_fusion.2
  230.1 0.6 bitcast_dynamic-update-slice_fusion.4
  231.3 3.3 fusion.18
  234.6 3.5 multiply_reduce_fusion.2
  239.3 3.3 fusion.18
  242.6 3.5 multiply_reduce_fusion.2
  247.3 3.3 fusion.18
  250.6 3.5 multiply_reduce_fusion.2
  254.1 0.6 bitcast_dynamic-update-slice_fusion.4
  255.3 3.3 fusion.18
  258.6 3.5 multiply_reduce_fusion.2
  263.3 3.3 fusion.18
  266.6 3.5 multiply_reduce_fusion.2
  271.3 3.3 fusion.18
  274.6 3.5 multiply_reduce_fusion.2
  279.3 3.3 fusion.18
  282.6 3.5 multiply_reduce_fusion.2
  287.3 3.3 fusion.18
  290.6 3.5 multiply_reduce_fusion.2
  294.1 0.6 bitcast_dynamic-update-slice_fusion.4
  295.3 3.3 fusion.18
  298.6 3.5 multiply_reduce_fusion.2
  303.3 3.3 fusion.18
  306.6 3.5 multiply_reduce_fusion.2
  311.3 3.3 fusion.18
  314.6 3.5 multiply_reduce_fusion.2
  318.1 0.6 bitcast_dynamic-update-slice_fusion.4
  319.3 1.0 reshape.51
  320.3 0.8 copy.33
  321.2 0.9 reshape.50
  322.2 59.4 %reduce-scatter.13.cloned.1.call-done = f32[32,72]{1,0:T(8,128)} async-done(((f32[512,72]{1,0:T(8,128)}), f32[32,72]{1,0:T(8,128)}) %reduce-scatter.13.cloned.1.call-update) | async-done | bytes 9232
  381.6 0.8 slice_compare_fusion
  382.4 0.8 copy.36
  383.2 17.3 %all_gather.10 = f32[64,512]{0,1:T(8,128)S(1)} all-gather(f32[64,32]{0,1:T(8,128)} %bitcast.36), channel_id=1, replica_groups=mesh['bus'=16,'line'=16] {'line'}, dimensions={1}, use_global_device_ids=true | all-gather | bytes 139264 | tf_op jit(solution)/shard_map/all_gather | solution.py:76
  401.2 45.9 %all_gather.11 = bf16[1024,416]{1,0:T(8,128)(2,1)S(1)} all-gather(bf16[64,416]{1,0:T(8,128)(2,1)S(1)} %pad_maximum_fusion.3), channel_id=1, replica_groups=mesh['bus'=16,'line'=16] {'bus'}, dimensions={0}, use_global_device_ids=true | all-gather | bytes 905216 | tf_op jit(solution)/shard_map/all_gather | solution.py:87
  447.0 3.2 fusion.4
  450.3 0.8 copy.26
  451.1 71.2 %reduce-scatter.11.cloned.1.call-done = f32[64,1024]{1,0:T(8,128)} async-done(((f32[1024,1024]{1,0:T(8,128)}), f32[64,1024]{1,0:T(8,128)}) %reduce-scatter.11.cloned.1.call-update) | async-done | bytes 262160 | tf_op jit(solution)/shard_map/reduce_scatter | solution.py:89
  522.3 1.7 add_convert_fusion
  (103 shorter events, 17.8 us)
Async XLA Ops:
  7.2 1.6 copy-start
  7.2 71.1 %reduce-scatter.7.cloned.1.call-start = ((), (), s32[]{:S(2)}) async-start(), calls=%async_computation.4 | async-start | bytes 1114112 | tf_op jit(solution)/shard_map/reduce_scatter | solution.py:48
  10.8 1.3 copy-start.4
  12.1 158.2 %reduce-scatter.9.cloned.1.call-start = ((), (), s32[]{:S(2)}) async-start(), calls=%async_computation.5 | async-start | bytes 2228224 | tf_op jit(solution)/shard_map/reduce_scatter | solution.py:55
  12.2 3.1 copy-start.3
  12.2 3.1 copy-start.6
  15.3 63.0 %copy-start.1 = (bf16[384,1024]{1,0:T(8,128)(2,1)S(1)}, bf16[384,1024]{1,0:T(8,128)(2,1)}, u32[]{:S(2)}) copy-start(bf16[384,1024]{1,0:T(8,128)(2,1)} %broadcast_select_fusion) | copy-start | bytes 2359300
  20.2 62.4 %copy-start.5 = (s32[512]{0:T(512)S(1)}, s32[512]{0:T(512)}, u32[]{:S(2)}) copy-start(s32[512]{0:T(512)} %param.18) | copy-start | bytes 6148
  82.4 108.2 %copy-start.9 = (f32[384]{0:T(512)S(1)}, f32[384]{0:T(512)}, u32[]{:S(2)}) copy-start(f32[384]{0:T(512)} %param.16) | copy-start | bytes 4612
  82.5 299.1 %reduce-scatter.13.cloned.1.call-start = ((), (), s32[]{:S(2)}) async-start(), calls=%async_computation.7 | async-start | bytes 278528
  190.6 0.7 copy-start.2
  319.3 127.8 %copy-start.8 = (bf16[32,1024]{1,0:T(8,128)(2,1)S(1)}, bf16[32,1024]{1,0:T(8,128)(2,1)}, u32[]{:S(2)}) copy-start(bf16[32,1024]{1,0:T(8,128)(2,1)} %reduce-scatter.7.cloned.1.call-done) | copy-start | bytes 196612
  321.2 201.1 %reduce-scatter.11.cloned.1.call-start = ((), (), s32[]{:S(2)}) async-start(), calls=%async_computation.6 | async-start | bytes 4456448 | tf_op jit(solution)/shard_map/reduce_scatter | solution.py:89
  450.2 72.0 %copy-start.7 = (f32[1024]{0:T(1024)S(1)}, f32[1024]{0:T(1024)}, u32[]{:S(2)}) copy-start(f32[1024]{0:T(1024)} %param.19) | copy-start | bytes 12292
Sparse Core Ops, SparseCore 0:
  12.2 66.0 reduce-scatter.6
  82.6 87.6 reduce-scatter.8
  321.3 60.2 reduce-scatter.12
  450.4 71.8 reduce-scatter.10

commit v2 on v1

--- a/solution.py
+++ b/solution.py
@@ -18,6 +18,11 @@
     direct = jnp.sum(raw_slope, axis=2) / outage_total
     sens_part = jnp.einsum("smk,mk->sk", raw_slope, lodf, precision=lax.Precision.HIGHEST)
     return (direct, sens_part)
+
+
+def exchange_sum(values, axis, count):
+    blocks = values.reshape((count, values.shape[0] // count) + values.shape[1:])
+    return jnp.sum(lax.all_to_all(blocks, axis, 0, 0, tiled=False), axis=0)
 
 
 def on_device(
@@ -45,14 +50,14 @@
         jnp.take(ptdf, jnp.clip(rel_outages, 0, line_rows - 1), axis=0),
         jnp.zeros((), ptdf.dtype),
     )
-    my_outage_rows = lax.psum_scatter(outage_rows, "line", scatter_dimension=0, tiled=True)
+    my_outage_rows = exchange_sum(outage_rows, "line", line_count)
     monitored_rows = jnp.take(ptdf, local_monitored, axis=0)
     rows = jnp.concatenate([monitored_rows, my_outage_rows], axis=0)
 
     flow_part = lax.dot_general(
         injection, rows, (((1,), (1,)), ((), ())), preferred_element_type=jnp.float32
     )
-    flow_field = lax.psum_scatter(flow_part, "bus", scatter_dimension=0, tiled=True)
+    flow_field = exchange_sum(flow_part, "bus", lax.axis_size("bus"))
     base = flow_field[:, :monitor_count]
     outflow = lax.all_gather(flow_field[:, monitor_count:], "line", axis=1, tiled=True)
 
@@ -70,10 +75,12 @@
     extended = jnp.concatenate(
         [sens_part, flag_part[None, :], jnp.zeros((7, outage_total), jnp.float32)], axis=0
     )
-    mine = lax.psum_scatter(extended, "line", scatter_dimension=1, tiled=True)
-    sens_mine = mine[:scen_rows]
-    flag_mine = mine[scen_rows]
-    sens_total = lax.all_gather(sens_mine, "line", axis=1, tiled=True)
+    summed = jnp.sum(lax.all_gather(extended, "line", axis=0, tiled=False), axis=0)
+    sens_total = summed[:scen_rows]
+    out_share = outage_total // line_count
+    share_start = lax.axis_index("line") * out_share
+    sens_mine = lax.dynamic_slice_in_dim(sens_total, share_start, out_share, 1)
+    flag_mine = lax.dynamic_slice_in_dim(summed[scen_rows], share_start, out_share, 0)
     backward = sens_total / outage_total
     outage_sens = sens_total / math.sqrt(monitored_total)
 
@@ -84,13 +91,13 @@
         flag_mine[None, :] > 0.5, 0.0, sens_mine / outage_total
     ).astype(jnp.bfloat16)
     piece = jnp.concatenate([adjoint_monitored, adjoint_outage], axis=1)
-    all_piece = lax.all_gather(piece, "bus", axis=0, tiled=True)
+    bus_count = lax.axis_size("bus")
+    all_piece = lax.all_to_all(
+        jnp.broadcast_to(piece[None], (bus_count,) + piece.shape), "bus", 0, 0, tiled=False
+    ).reshape(bus_count * piece.shape[0], piece.shape[1])
     grad_rows = all_piece.shape[0] // line_count
-    pushed = lax.psum_scatter(
-        jnp.dot(all_piece, rows, preferred_element_type=jnp.float32),
-        "line",
-        scatter_dimension=0,
-        tiled=True,
+    pushed = exchange_sum(
+        jnp.dot(all_piece, rows, preferred_element_type=jnp.float32), "line", line_count
     )
     own_generation = lax.dynamic_slice_in_dim(
         generation, lax.axis_index("line") * grad_rows, grad_rows, 0

time: 534 us -> 391 us (0.73)
  waiting for transfers between devices: 276 us -> 152 us
  blocking collectives: 81.6 us -> 53.5 us
  starting transfers between devices: 0.16 us -> 25.8 us
  local copies, waits for them, and re-layouts: 21.5 us -> 7.12 us
    reduce_scatter x3 -> x0, waiting for transfers between devices: 217 us -> none  [the longest x1 87.4 us: on_device(): lax.psum_scatter(flow_part, 'bus', scatter_dimension=0, tiled=True)]
    all_to_all x0 -> x3, waiting for transfers between devices: none -> 117 us  [exchange_sum(): return jnp.sum(lax.all_to_all(blocks, axis, 0, 0, tiled=False), axis=0)]
    all_gather x2 -> x0, blocking collectives: 63.2 us -> none  [the longest x1 45.9 us: on_device(): all_piece = lax.all_gather(piece, 'bus', axis=0, tiled=True)]
    unnamed x5 -> x1, waiting for transfers between devices: 59.5 us -> 0.02 us
    all_to_all x0 -> x1, blocking collectives: none -> 36 us  [on_device(): lax.all_to_all(jnp.broadcast_to(piece[None], (bus_count,) + piece.shape),...]
    all_gather x0 -> x1, waiting for transfers between devices: none -> 35.3 us  [on_device(): lax.all_gather(extended, 'line', axis=0, tiled=False)]
    all_to_all x0 -> x3, starting transfers between devices: none -> 25.7 us  [exchange_sum(): return jnp.sum(lax.all_to_all(blocks, axis, 0, 0, tiled=False), axis=0)]
    dynamic_update_slice x16, other arithmetic: 9.61 us -> 0.22 us  [on_device(): lax.map(lambda pieces: contingency(pieces, lodf, limits, outage_total), (...]
  transfers between devices with their start and end apart: 4 -> 4, of which waited for: 4 -> 4; matrix products, arithmetic and copies ran while one was open for 2% -> 3% of each run, Pallas kernels for 0% -> 0%
where the time goes in v2:
time: 391 us; the launch traced here: 389 us
  waiting for transfers between devices  152 us (39%)
  other arithmetic  123 us (31%)
  blocking collectives  53.5 us (14%)
  starting transfers between devices  25.8 us (7%)
  between operations  14.3 us (4%)
  matrix products  12.9 us (3%)
  local copies, waits for them, and re-layouts  7.12 us (2%)
    all_to_all x3, waiting for transfers between devices, exchange_sum(): return jnp.sum(lax.all_to_all(blocks, axis, 0, 0, tiled=False), axis=0)  117 us
    dot_general x16, other arithmetic, contingency(): jnp.einsum('smk,mk->sk', raw_slope, lodf, precision=lax.Precision.HIGHEST)  55.2 us
    reduce_sum x16, other arithmetic, contingency(): direct = jnp.sum(raw_slope, axis=2) / outage_total  53.6 us
    all_to_all x1, blocking collectives, on_device(): lax.all_to_all(jnp.broadcast_to(piece[None], (bus_count,) + piece.shape),...  36 us
    all_gather x1, waiting for transfers between devices, on_device(): lax.all_gather(extended, 'line', axis=0, tiled=False)  35.3 us
    all_to_all x3, starting transfers between devices, exchange_sum(): return jnp.sum(lax.all_to_all(blocks, axis, 0, 0, tiled=False), axis=0)  25.7 us
    all_gather x1, blocking collectives, on_device(): lax.all_gather(flow_field[:, monitor_count:], 'line', axis=1, tiled=True)  17.5 us
  transfers between devices with their start and end apart: 4, of which 4 were waited for; matrix products, arithmetic and copies ran while one was open for 3% of the time, Pallas kernels for 0%

profile of v2, /device:TPU:7, one launch (start us, length us, event | category | flops | bytes accessed | tf_op | source)
XLA Modules:
  0.0 389.4 jit_solution(15673685653698346759)
XLA Ops:
  7.2 0.8 compare_and_fusion
  8.0 0.1 broadcast_in_dim.96
  8.2 0.6 copy-done
  8.8 2.0 gather_fusion.1
  10.8 1.2 select_select_fusion
  12.1 6.4 %all-to-all-start = ((bf16[16,32,1024]{2,1,0:T(8,128)(2,1)}), bf16[16,32,1024]{2,1,0:T(8,128)(2,1)S(1)}, u32[]{:S(2)}, u32[]{:S(2)}) async-start(bf16[16,32,1024]{2,1,0:T(8,128)(2,1)} %select_select_fusion), calls=%async_computation | async-start | bytes 2097152 | tf_op jit(solution)/shard_map/all_to_all | solution.py:25
  18.6 2.7 gather_fusion
  21.2 2.2 broadcast_select_fusion
  23.4 4.9 %subtract_convert_fusion = bf16[1024,1024]{1,0:T(8,128)(2,1)} fusion(bf16[1024,1024]{1,0:T(8,128)(2,1)} %param.11, f32[24,1024]{1,0:T(8,128)S(1)} %copy-done.3, s32[1024]{0:T(1024)S(1)} %copy-done.6), kind=kOutput, calls=%fused_computation.9 | convolution fusion | flops 305160192 | bytes 4296704 | tf_op jit(solution)/shard_map/dot_general | solution.py:36
  28.3 5.2 %all-to-all-done = bf16[16,32,1024]{2,1,0:T(8,128)(2,1)S(1)} async-done(((bf16[16,32,1024]{2,1,0:T(8,128)(2,1)}), bf16[16,32,1024]{2,1,0:T(8,128)(2,1)S(1)}, u32[]{:S(2)}, u32[]{:S(2)}) %all-to-all-start) | async-done | bytes 1048608 | tf_op jit(solution)/shard_map/all_to_all | solution.py:25
  33.4 0.2 reduce_sum.57
  33.6 4.3 %fusion.6 = f32[1024,416]{1,0:T(8,128)} fusion(bf16[1024,1024]{1,0:T(8,128)(2,1)} %subtract_convert_fusion, bf16[32,1024]{1,0:T(8,128)(2,1)S(1)} %reduce_sum.57, bf16[384,1024]{1,0:T(8,128)(2,1)} %broadcast_select_fusion), kind=kOutput, calls=%fused_computation.20 | convolution fusion | flops 874119168 | bytes 4653056 | tf_op jit(solution)/shard_map/dot_general | solution.py:57
  38.0 10.2 %all-to-all-start.1 = ((f32[16,64,416]{2,1,0:T(8,128)}), f32[16,64,416]{2,1,0:T(8,128)}, u32[]{:S(2)}, u32[]{:S(2)}) async-start(f32[16,64,416]{2,1,0:T(8,128)} %bitcast.39), calls=%async_computation.1 | async-start | bytes 4194304 | tf_op jit(solution)/shard_map/all_to_all | solution.py:25
  48.3 0.2 fusion.5
  48.6 50.3 %all-to-all-done.1 = f32[16,64,416]{2,1,0:T(8,128)} async-done(((f32[16,64,416]{2,1,0:T(8,128)}), f32[16,64,416]{2,1,0:T(8,128)}, u32[]{:S(2)}, u32[]{:S(2)}) %all-to-all-start.1) | async-done | bytes 1703968 | tf_op jit(solution)/shard_map/all_to_all | solution.py:25
  98.9 1.8 reduce_sum.58
  100.8 17.5 %all_gather.9 = f32[64,512]{0,1:T(8,128)S(1)} all-gather(f32[64,32]{0,1:T(8,128)S(1)} %copy.26), channel_id=1, replica_groups=mesh['bus'=16,'line'=16] {'line'}, dimensions={1}, use_global_device_ids=true | all-gather | bytes 139264 | tf_op jit(solution)/shard_map/all_gather | solution.py:62
  118.3 0.1 copy.27
  118.5 0.6 copy-done.2
  119.1 110.2 %while.12 = (s32[]{:T(128)}, f32[16,4,384]{2,1,0:T(4,128)S(1)}, f32[16,4,512]{2,1,0:T(4,128)S(1)}, f32[16,4,384]{2,1,0:T(4,128)S(1)}, f32[384,512]{1,0:T(8,128)}...) while((s32[]{:T(128)}, f32[16,4,384]{2,1,0:T(4,128)S(1)}, f32[16,4,512]{2,1,0:T(4,128)S(1)}, ...), condition=%wide.region_4.5_spmd, body=%wide.region_2.4_spmd.sunk | while | flops 24377344 | bytes 2462829 | solution.py:67
  119.1 3.3 fusion.20
  122.4 3.5 multiply_reduce_fusion.2
  125.9 3.3 fusion.20
  129.3 3.5 multiply_reduce_fusion.2
  132.8 3.3 fusion.20
  136.2 3.5 multiply_reduce_fusion.2
  139.7 3.3 fusion.20
  143.1 3.5 multiply_reduce_fusion.2
  146.6 3.3 fusion.20
  150.0 3.5 multiply_reduce_fusion.2
  153.5 3.3 fusion.20
  156.9 3.5 multiply_reduce_fusion.2
  160.4 3.3 fusion.20
  163.7 3.5 multiply_reduce_fusion.2
  167.3 3.3 fusion.20
  170.6 3.5 multiply_reduce_fusion.2
  174.2 3.3 fusion.20
  177.5 3.5 multiply_reduce_fusion.2
  181.1 3.3 fusion.20
  184.4 3.5 multiply_reduce_fusion.2
  188.0 3.3 fusion.20
  191.3 3.5 multiply_reduce_fusion.2
  194.8 3.3 fusion.20
  198.2 3.5 multiply_reduce_fusion.2
  201.7 3.3 fusion.20
  205.1 3.5 multiply_reduce_fusion.2
  208.6 3.3 fusion.20
  212.0 3.5 multiply_reduce_fusion.2
  215.5 3.3 fusion.20
  218.9 3.5 multiply_reduce_fusion.2
  222.4 3.3 fusion.20
  225.8 3.5 multiply_reduce_fusion.2
  229.3 0.7 maximum_maximum_fusion
  230.1 35.3 %all-gather.3.cloned.1.call-done = f32[1152,512]{1,0:T(8,128)} async-done(((f32[72,512]{1,0:T(8,128)}), f32[1152,512]{1,0:T(8,128)}) %all-gather.3.cloned.1.call-update) | async-done | bytes 2359312 | tf_op jit(solution)/shard_map/all_gather | solution.py:78
  265.4 1.9 reduce_sum.60
  267.4 0.7 broadcast_multiply_fusion
  268.0 0.4 fusion.1
  268.7 0.1 broadcast_in_dim.106
  268.8 36.0 %all_to_all.20 = bf16[16,64,416]{2,1,0:T(8,128)(2,1)S(1)} all-to-all(bf16[16,64,416]{2,1,0:T(8,128)(2,1)S(1)} %broadcast_in_dim.106), channel_id=1, replica_groups=mesh['bus'=16,'line'=16] {'bus'}, dimensions={0} | all-to-all | bytes 1703936 | tf_op jit(solution)/shard_map/all_to_all | solution.py:95
  304.8 3.2 fusion.3
  308.0 9.1 %all-to-all-start.3 = ((f32[16,64,1024]{2,1,0:T(8,128)}), f32[16,64,1024]{2,1,0:T(8,128)}, u32[]{:S(2)}, u32[]{:S(2)}) async-start(f32[16,64,1024]{2,1,0:T(8,128)} %fusion.3), calls=%async_computation.3 | async-start | bytes 8388608 | tf_op jit(solution)/shard_map/all_to_all | solution.py:25
  317.2 61.3 %all-to-all-done.3 = f32[16,64,1024]{2,1,0:T(8,128)} async-done(((f32[16,64,1024]{2,1,0:T(8,128)}), f32[16,64,1024]{2,1,0:T(8,128)}, u32[]{:S(2)}, u32[]{:S(2)}) %all-to-all-start.3) | async-done | bytes 4194336 | tf_op jit(solution)/shard_map/all_to_all | solution.py:25
  378.5 2.5 reduce_sum.61
  381.0 1.6 add_convert_fusion
  (101 shorter events, 1.4 us)
Async XLA Ops:
  7.2 1.6 copy-start
  10.8 7.7 %copy-start.4 = (s32[384]{0:T(512)S(1)}, s32[384]{0:T(512)}, u32[]{:S(2)}) copy-start(s32[384]{0:T(512)} %param.17) | copy-start | bytes 4612
  12.1 21.4 %all-to-all-start = ((bf16[16,32,1024]{2,1,0:T(8,128)(2,1)}), bf16[16,32,1024]{2,1,0:T(8,128)(2,1)S(1)}, u32[]{:S(2)}, u32[]{:S(2)}) async-start(bf16[16,32,1024]{2,1,0:T(8,128)(2,1)} %select_select_fusion), calls=%async_computation | async-start | bytes 2097152 | tf_op jit(solution)/shard_map/all_to_all | solution.py:25
  18.5 4.9 %copy-start.3 = (f32[24,1024]{1,0:T(8,128)S(1)}, f32[24,1024]{1,0:T(8,128)}, u32[]{:S(2)}) copy-start(f32[24,1024]{1,0:T(8,128)} %param.12) | copy-start | bytes 294916
  18.5 4.9 %copy-start.6 = (s32[1024]{0:T(1024)S(1)}, s32[1024]{0:T(1024)}, u32[]{:S(2)}) copy-start(s32[1024]{0:T(1024)} %param.13) | copy-start | bytes 12292
  38.0 10.4 %copy-start.5 = (s32[512]{0:T(512)S(1)}, s32[512]{0:T(512)}, u32[]{:S(2)}) copy-start(s32[512]{0:T(512)} %param.18) | copy-start | bytes 6148
  38.0 80.5 %copy-start.8 = (f32[384]{0:T(512)S(1)}, f32[384]{0:T(512)}, u32[]{:S(2)}) copy-start(f32[384]{0:T(512)} %param.16) | copy-start | bytes 4612
  38.0 60.9 %all-to-all-start.1 = ((f32[16,64,416]{2,1,0:T(8,128)}), f32[16,64,416]{2,1,0:T(8,128)}, u32[]{:S(2)}, u32[]{:S(2)}) async-start(f32[16,64,416]{2,1,0:T(8,128)} %bitcast.39), calls=%async_computation.1 | async-start | bytes 4194304 | tf_op jit(solution)/shard_map/all_to_all | solution.py:25
  48.2 217.2 %all-gather.3.cloned.1.call-start = ((), (), s32[]{:S(2)}) async-start(), calls=%async_computation.4 | async-start | bytes 2506752 | tf_op jit(solution)/shard_map/all_gather | solution.py:78
  118.4 0.7 copy-start.2
  265.4 39.4 %copy-start.1 = (bf16[384,1024]{1,0:T(8,128)(2,1)S(1)}, bf16[384,1024]{1,0:T(8,128)(2,1)}, u32[]{:S(2)}) copy-start(bf16[384,1024]{1,0:T(8,128)(2,1)} %broadcast_select_fusion) | copy-start | bytes 2359300
  308.0 70.4 %all-to-all-start.3 = ((f32[16,64,1024]{2,1,0:T(8,128)}), f32[16,64,1024]{2,1,0:T(8,128)}, u32[]{:S(2)}, u32[]{:S(2)}) async-start(f32[16,64,1024]{2,1,0:T(8,128)} %fusion.3), calls=%async_computation.3 | async-start | bytes 8388608 | tf_op jit(solution)/shard_map/all_to_all | solution.py:25
  317.1 63.8 %copy-start.7 = (f32[1024]{0:T(1024)S(1)}, f32[1024]{0:T(1024)}, u32[]{:S(2)}) copy-start(f32[1024]{0:T(1024)} %param.19) | copy-start | bytes 12292
Sparse Core Ops, SparseCore 0:
  230.2 35.1 all-gather.2

commit v3 on v2

--- a/solution.py
+++ b/solution.py
@@ -3,22 +3,60 @@
 import jax
 import jax.numpy as jnp
 from jax import lax
+from jax.experimental import pallas as pl
 from jax.sharding import PartitionSpec as P
 
 sharpness = 4.0
 
 
-def contingency(pieces, lodf, limits, outage_total):
-    base_block, outage_block = pieces
-    post_flow = base_block[:, :, None] + lodf[None, :, :] * outage_block[:, None, :]
-    bounds = limits[None, :, None]
-    raw_slope = jax.nn.sigmoid(sharpness * (post_flow - bounds)) - jax.nn.sigmoid(
-        sharpness * (-post_flow - bounds)
-    )
-    direct = jnp.sum(raw_slope, axis=2) / outage_total
-    sens_part = jnp.einsum("smk,mk->sk", raw_slope, lodf, precision=lax.Precision.HIGHEST)
-    return (direct, sens_part)
+def penalty_slopes(base, outflow, lodf, limits):
+    scen_rows, monitor_count = base.shape
+    outage_total = outflow.shape[1]
+    sb = 8
+    ch = 16
+    blocks = scen_rows // sb
+    half = sharpness / 2
+    base3 = (half * base).reshape(blocks, sb, monitor_count).transpose(0, 2, 1)
+    lodf2 = half * lodf
+    lim2 = (half * limits).reshape(monitor_count, 1)
 
+    def kernel(base_ref, out_ref, lodf_ref, lim_ref, direct_ref, sens_ref):
+        for i in range(sb):
+            flow_row = out_ref[i:i + 1, :]
+
+            def body(c, acc):
+                r = pl.multiple_of(c * ch, ch)
+                weight = lodf_ref[pl.ds(r, ch), :]
+                bound = lim_ref[pl.ds(r, ch), :]
+                post = base_ref[pl.ds(r, ch), i:i + 1] + weight * flow_row
+                slope = jnp.tanh(post - bound) + jnp.tanh(post + bound)
+                direct_ref[pl.ds(r, ch), i:i + 1] = jnp.sum(slope, axis=1, keepdims=True)
+                return acc + weight * slope
+
+            acc = lax.fori_loop(0, monitor_count // ch, body,
+                                jnp.zeros((ch, outage_total), jnp.float32))
+            sens_ref[i:i + 1, :] = jnp.sum(acc, axis=0, keepdims=True)
+
+    direct3, sens = pl.pallas_call(
+        kernel,
+        grid=(blocks,),
+        in_specs=[
+            pl.BlockSpec((None, monitor_count, sb), lambda g: (g, 0, 0)),
+            pl.BlockSpec((sb, outage_total), lambda g: (g, 0)),
+            pl.BlockSpec((monitor_count, outage_total), lambda g: (0, 0)),
+            pl.BlockSpec((monitor_count, 1), lambda g: (0, 0)),
+        ],
+        out_specs=[
+            pl.BlockSpec((None, monitor_count, sb), lambda g: (g, 0, 0)),
+            pl.BlockSpec((sb, outage_total), lambda g: (g, 0)),
+        ],
+        out_shape=[
+            jax.ShapeDtypeStruct((blocks, monitor_count, sb), jnp.float32),
+            jax.ShapeDtypeStruct((scen_rows, outage_total), jnp.float32),
+        ],
+    )(base3, outflow, lodf2, lim2)
+    direct = direct3.transpose(0, 2, 1).reshape(scen_rows, monitor_count) / (2.0 * outage_total)
+    return direct, sens / (2.0 * half)
 
 def exchange_sum(values, axis, count):
     blocks = values.reshape((count, values.shape[0] // count) + values.shape[1:])
@@ -61,26 +99,19 @@
     base = flow_field[:, :monitor_count]
     outflow = lax.all_gather(flow_field[:, monitor_count:], "line", axis=1, tiled=True)
 
-    block_size = math.gcd(scen_rows, 4)
-    base_blocks = base.reshape(scen_rows // block_size, block_size, monitor_count)
-    outage_blocks = outflow.reshape(scen_rows // block_size, block_size, outage_total)
-    direct, sens_part = lax.map(
-        lambda pieces: contingency(pieces, lodf, limits, outage_total), (base_blocks, outage_blocks)
-    )
-    direct = direct.reshape(scen_rows, monitor_count)
-    sens_part = sens_part.reshape(scen_rows, outage_total)
+    direct, sens_part = penalty_slopes(base, outflow, lodf, limits)
 
     matches = (outages[:, None] == monitored[None, :]).astype(jnp.float32)
     flag_part = jnp.sum(matches, axis=1)
     extended = jnp.concatenate(
         [sens_part, flag_part[None, :], jnp.zeros((7, outage_total), jnp.float32)], axis=0
     )
-    summed = jnp.sum(lax.all_gather(extended, "line", axis=0, tiled=False), axis=0)
-    sens_total = summed[:scen_rows]
     out_share = outage_total // line_count
-    share_start = lax.axis_index("line") * out_share
-    sens_mine = lax.dynamic_slice_in_dim(sens_total, share_start, out_share, 1)
-    flag_mine = lax.dynamic_slice_in_dim(summed[scen_rows], share_start, out_share, 0)
+    shares = extended.reshape(extended.shape[0], line_count, out_share).transpose(1, 0, 2)
+    mine = jnp.sum(lax.all_to_all(shares, "line", 0, 0, tiled=False), axis=0)
+    sens_mine = mine[:scen_rows]
+    flag_mine = mine[scen_rows]
+    sens_total = lax.all_gather(sens_mine, "line", axis=1, tiled=True)
     backward = sens_total / outage_total
     outage_sens = sens_total / math.sqrt(monitored_total)
 

time: 391 us -> 510 us (1.30)
  Pallas kernels: 0 us -> 253 us
  other arithmetic: 123 us -> 16.2 us
  waiting for transfers between devices: 152 us -> 114 us
  between operations: 14.3 us -> 0.83 us
  blocking collectives: 53.5 us -> 64.1 us
  starting transfers between devices: 25.8 us -> 34.3 us
    pallas_call x0 -> x1, Pallas kernels: none -> 253 us  [penalty_slopes(): pl.pallas_call(kernel, grid=(blocks,), in_specs=[pl.BlockSpec((None, moni...]
    reduce_sum x17 -> x1, other arithmetic: 55.5 us -> 0.03 us  [on_device(): mine = jnp.sum(lax.all_to_all(shares, 'line', 0, 0, tiled=False), axis=0)]
    dot_general x16 -> x0, other arithmetic: 55.2 us -> none  [contingency(): jnp.einsum('smk,mk->sk', raw_slope, lodf, precision=lax.Precision.HIGHEST)]
    all_gather x1 -> x0, waiting for transfers between devices: 35.3 us -> none  [on_device(): lax.all_gather(extended, 'line', axis=0, tiled=False)]
    all_gather x0 -> x1, blocking collectives: none -> 16.9 us  [on_device(): sens_total = lax.all_gather(sens_mine, 'line', axis=1, tiled=True)]
    all_to_all x0 -> x1, starting transfers between devices: none -> 6.77 us  [on_device(): mine = jnp.sum(lax.all_to_all(shares, 'line', 0, 0, tiled=False), axis=0)]
    all_to_all x1, blocking collectives: 36 us -> 30.1 us  [on_device(): lax.all_to_all(jnp.broadcast_to(piece[None], (bus_count,) + piece.shape),...]
where the time goes in v3:
time: 510 us; the launch traced here: 507 us
  Pallas kernels  253 us (50%)
  waiting for transfers between devices  114 us (22%)
  blocking collectives  64.1 us (13%)
  starting transfers between devices  34.3 us (7%)
  other arithmetic  16.2 us (3%)
  matrix products  13 us (3%)
  local copies, waits for them, and re-layouts  12 us (2%)
    pallas_call x1, Pallas kernels, penalty_slopes(): pl.pallas_call(kernel, grid=(blocks,), in_specs=[pl.BlockSpec((None, moni...  253 us
    all_to_all x3, waiting for transfers between devices, exchange_sum(): return jnp.sum(lax.all_to_all(blocks, axis, 0, 0, tiled=False), axis=0)  112 us
    all_to_all x1, blocking collectives, on_device(): lax.all_to_all(jnp.broadcast_to(piece[None], (bus_count,) + piece.shape),...  30.1 us
    all_to_all x3, starting transfers between devices, exchange_sum(): return jnp.sum(lax.all_to_all(blocks, axis, 0, 0, tiled=False), axis=0)  27.5 us
    all_gather x1, blocking collectives, on_device(): lax.all_gather(flow_field[:, monitor_count:], 'line', axis=1, tiled=True)  17.2 us
    all_gather x1, blocking collectives, on_device(): sens_total = lax.all_gather(sens_mine, 'line', axis=1, tiled=True)  16.9 us
  transfers between devices with their start and end apart: 4, of which 4 were waited for; matrix products, arithmetic and copies ran while one was open for 3% of the time, Pallas kernels for 0%

profile of v3, /device:TPU:7, one launch (start us, length us, event | category | flops | bytes accessed | tf_op | source)
XLA Modules:
  0.0 506.9 jit_solution(5148152522045850759)
XLA Ops:
  0.6 0.0 copy-start
  0.6 0.8 compare_and_fusion
  1.5 0.1 broadcast_in_dim.75
  1.6 0.1 broadcast_in_dim.73
  1.7 0.6 copy-done
  2.2 2.0 gather_fusion.1
  4.3 0.0 copy-start.4
  4.3 1.2 select_select_fusion
  5.5 6.4 %all-to-all-start = ((bf16[16,32,1024]{2,1,0:T(8,128)(2,1)}), bf16[16,32,1024]{2,1,0:T(8,128)(2,1)S(1)}, u32[]{:S(2)}, u32[]{:S(2)}) async-start(bf16[16,32,1024]{2,1,0:T(8,128)(2,1)} %select_select_fusion), calls=%async_computation | async-start | bytes 2097152 | tf_op jit(solution)/shard_map/all_to_all | solution.py:63
  11.9 0.0 copy-done.4
  12.0 0.0 copy-start.3
  12.0 0.0 copy-start.6
  12.0 2.7 gather_fusion
  14.7 2.2 broadcast_select_fusion
  16.9 0.0 copy-done.3
  16.9 0.0 copy-done.6
  16.9 4.8 subtract_convert_fusion
  21.8 5.1 %all-to-all-done = bf16[16,32,1024]{2,1,0:T(8,128)(2,1)S(1)} async-done(((bf16[16,32,1024]{2,1,0:T(8,128)(2,1)}), bf16[16,32,1024]{2,1,0:T(8,128)(2,1)S(1)}, u32[]{:S(2)}, u32[]{:S(2)}) %all-to-all-start) | async-done | bytes 1048608 | tf_op jit(solution)/shard_map/all_to_all | solution.py:63
  26.9 0.2 reduce_sum.48
  27.1 4.4 fusion.5
  31.5 0.0 copy-start.8
  31.5 0.0 copy-start.5
  31.5 0.0 copy-start.2
  31.5 10.2 %all-to-all-start.1 = ((f32[16,64,416]{2,1,0:T(8,128)}), f32[16,64,416]{2,1,0:T(8,128)}, u32[]{:S(2)}, u32[]{:S(2)}) async-start(f32[16,64,416]{2,1,0:T(8,128)} %bitcast.21), calls=%async_computation.1 | async-start | bytes 4194304 | tf_op jit(solution)/shard_map/all_to_all | solution.py:63
  41.7 0.0 copy-done.8
  41.7 0.8 reshape.77.lim_ref
  42.5 0.0 copy-done.5
  42.5 0.2 fusion.4
  42.7 0.2 concatenate.19
  43.0 0.1 pad.4.clone
  43.0 0.0 copy-done.2
  43.0 1.0 broadcast_multiply_fusion.lodf_ref
  44.0 48.8 %all-to-all-done.1 = f32[16,64,416]{2,1,0:T(8,128)} async-done(((f32[16,64,416]{2,1,0:T(8,128)}), f32[16,64,416]{2,1,0:T(8,128)}, u32[]{:S(2)}, u32[]{:S(2)}) %all-to-all-start.1) | async-done | bytes 1703968 | tf_op jit(solution)/shard_map/all_to_all | solution.py:63
  92.8 1.8 reduce_sum.49
  94.6 0.1 copy.48
  94.6 17.2 %all_gather.6 = f32[64,512]{0,1:T(8,128)S(1)} all-gather(f32[64,32]{0,1:T(8,128)S(1)} %copy.48), channel_id=1, replica_groups=mesh['bus'=16,'line'=16] {'line'}, dimensions={1}, use_global_device_ids=true | all-gather | bytes 139264 | tf_op jit(solution)/shard_map/all_gather | solution.py:100
  111.8 0.8 copy.49.out_ref
  112.6 1.6 copy.47
  114.2 252.6 %shard_map.112 = (f32[8,384,8]{2,1,0:T(8,128)}, f32[64,512]{1,0:T(8,128)}) custom-call(f32[8,384,8]{2,1,0:T(8,128)} %bitcast.19, f32[64,512]{1,0:T(8,128)} %copy.49.out_ref, f32[384,512]{1,0:T(8,128)} %broadcast_multiply_fusion.lodf_ref, f32[384,1]{1,0:T(8,128)} %reshape.77.lim_ref), custom_call_target="tpu_custom_call" | custom-call | tf_op jit(solution)/shard_map/pallas_call | solution.py:40
  366.9 0.9 broadcast_multiply_fusion.2
  367.8 0.1 copy.52
  367.9 0.8 maximum_bitcast_fusion
  368.8 6.8 %all-to-all-start.2 = ((f32[16,72,32]{1,2,0:T(8,128)}), f32[16,72,32]{1,2,0:T(8,128)S(1)}, u32[]{:S(2)}, u32[]{:S(2)}) async-start(f32[16,72,32]{1,2,0:T(8,128)} %maximum_bitcast_fusion), calls=%async_computation.2 | async-start | bytes 524288 | tf_op jit(solution)/shard_map/all_to_all | solution.py:111
  375.5 2.7 multiply_bitcast_fusion
  378.2 1.8 copy.51
  380.0 1.6 all-to-all-done.2
  381.6 0.0 copy-start.1
  381.6 0.2 fusion.12
  381.8 0.1 copy.59
  381.9 16.9 %all_gather.7 = f32[64,512]{0,1:T(8,128)S(1)} all-gather(f32[64,32]{0,1:T(8,128)S(1)} %bitcast.24), channel_id=1, replica_groups=mesh['bus'=16,'line'=16] {'line'}, dimensions={1}, use_global_device_ids=true | all-gather | bytes 139264 | tf_op jit(solution)/shard_map/all_gather | solution.py:114
  398.8 0.5 fusion
  399.3 0.1 broadcast_in_dim.84
  399.4 30.1 %all_to_all.25 = bf16[16,64,416]{2,1,0:T(8,128)(2,1)S(1)} all-to-all(bf16[16,64,416]{2,1,0:T(8,128)(2,1)S(1)} %broadcast_in_dim.84), channel_id=1, replica_groups=mesh['bus'=16,'line'=16] {'bus'}, dimensions={0} | all-to-all | bytes 1703936 | tf_op jit(solution)/shard_map/all_to_all | solution.py:126
  429.5 0.0 copy-done.1
  429.5 3.2 fusion.2
  432.8 10.9 %all-to-all-start.4 = ((f32[16,64,1024]{2,1,0:T(8,128)}), f32[16,64,1024]{2,1,0:T(8,128)}, u32[]{:S(2)}, u32[]{:S(2)}) async-start(f32[16,64,1024]{2,1,0:T(8,128)} %fusion.2), calls=%async_computation.4 | async-start | bytes 8388608 | tf_op jit(solution)/shard_map/all_to_all | solution.py:63
  443.7 0.8 copy.57
  444.5 0.0 copy-start.7
  444.5 58.3 %all-to-all-done.4 = f32[16,64,1024]{2,1,0:T(8,128)} async-done(((f32[16,64,1024]{2,1,0:T(8,128)}), f32[16,64,1024]{2,1,0:T(8,128)}, u32[]{:S(2)}, u32[]{:S(2)}) %all-to-all-start.4) | async-done | bytes 4194336 | tf_op jit(solution)/shard_map/all_to_all | solution.py:63
  502.8 2.5 reduce_sum.52
  505.3 0.0 copy-done.7
  505.3 1.6 add_convert_fusion
  (11 shorter events, 0.1 us)
Async XLA Ops:
  0.6 1.6 copy-start
  4.3 7.6 %copy-start.4 = (s32[384]{0:T(512)S(1)}, s32[384]{0:T(512)}, u32[]{:S(2)}) copy-start(s32[384]{0:T(512)} %param.15) | copy-start | bytes 4612
  5.5 21.4 %all-to-all-start = ((bf16[16,32,1024]{2,1,0:T(8,128)(2,1)}), bf16[16,32,1024]{2,1,0:T(8,128)(2,1)S(1)}, u32[]{:S(2)}, u32[]{:S(2)}) async-start(bf16[16,32,1024]{2,1,0:T(8,128)(2,1)} %select_select_fusion), calls=%async_computation | async-start | bytes 2097152 | tf_op jit(solution)/shard_map/all_to_all | solution.py:63
  12.0 4.9 copy-start.3
  12.0 4.9 copy-start.6
  31.5 10.2 %copy-start.8 = (f32[384]{0:T(512)S(1)}, f32[384]{0:T(512)}, u32[]{:S(2)}) copy-start(f32[384]{0:T(512)} %param.14) | copy-start | bytes 4612
  31.5 11.0 %copy-start.5 = (s32[512]{0:T(512)S(1)}, s32[512]{0:T(512)}, u32[]{:S(2)}) copy-start(s32[512]{0:T(512)} %param.16) | copy-start | bytes 6148
  31.5 11.6 %copy-start.2 = (f32[384,512]{1,0:T(8,128)S(1)}, f32[384,512]{1,0:T(8,128)}, u32[]{:S(2)}) copy-start(f32[384,512]{1,0:T(8,128)} %param.13) | copy-start | bytes 2359300
  31.5 61.3 %all-to-all-start.1 = ((f32[16,64,416]{2,1,0:T(8,128)}), f32[16,64,416]{2,1,0:T(8,128)}, u32[]{:S(2)}, u32[]{:S(2)}) async-start(f32[16,64,416]{2,1,0:T(8,128)} %bitcast.21), calls=%async_computation.1 | async-start | bytes 4194304 | tf_op jit(solution)/shard_map/all_to_all | solution.py:63
  368.8 12.8 %all-to-all-start.2 = ((f32[16,72,32]{1,2,0:T(8,128)}), f32[16,72,32]{1,2,0:T(8,128)S(1)}, u32[]{:S(2)}, u32[]{:S(2)}) async-start(f32[16,72,32]{1,2,0:T(8,128)} %maximum_bitcast_fusion), calls=%async_computation.2 | async-start | bytes 524288 | tf_op jit(solution)/shard_map/all_to_all | solution.py:111
  381.6 47.9 %copy-start.1 = (bf16[384,1024]{1,0:T(8,128)(2,1)S(1)}, bf16[384,1024]{1,0:T(8,128)(2,1)}, u32[]{:S(2)}) copy-start(bf16[384,1024]{1,0:T(8,128)(2,1)} %broadcast_select_fusion) | copy-start | bytes 2359300
  432.8 70.0 %all-to-all-start.4 = ((f32[16,64,1024]{2,1,0:T(8,128)}), f32[16,64,1024]{2,1,0:T(8,128)}, u32[]{:S(2)}, u32[]{:S(2)}) async-start(f32[16,64,1024]{2,1,0:T(8,128)} %fusion.2), calls=%async_computation.4 | async-start | bytes 8388608 | tf_op jit(solution)/shard_map/all_to_all | solution.py:63
  444.5 60.8 %copy-start.7 = (f32[1024]{0:T(1024)S(1)}, f32[1024]{0:T(1024)}, u32[]{:S(2)}) copy-start(f32[1024]{0:T(1024)} %param.17) | copy-start | bytes 12292

commit v4 on v3

--- a/solution.py
+++ b/solution.py
@@ -14,6 +14,7 @@
     outage_total = outflow.shape[1]
     sb = 8
     ch = 16
+    lanes = 128
     blocks = scen_rows // sb
     half = sharpness / 2
     base3 = (half * base).reshape(blocks, sb, monitor_count).transpose(0, 2, 1)
@@ -30,14 +31,18 @@
                 bound = lim_ref[pl.ds(r, ch), :]
                 post = base_ref[pl.ds(r, ch), i:i + 1] + weight * flow_row
                 slope = jnp.tanh(post - bound) + jnp.tanh(post + bound)
-                direct_ref[pl.ds(r, ch), i:i + 1] = jnp.sum(slope, axis=1, keepdims=True)
+                folded = slope[:, 0:lanes]
+                for q in range(1, outage_total // lanes):
+                    folded = folded + slope[:, q * lanes:(q + 1) * lanes]
+                direct_ref[i, pl.ds(r, ch), :] = folded
                 return acc + weight * slope
 
             acc = lax.fori_loop(0, monitor_count // ch, body,
-                                jnp.zeros((ch, outage_total), jnp.float32))
+                                jnp.zeros((ch, outage_total), jnp.float32),
+                                unroll=monitor_count // ch)
             sens_ref[i:i + 1, :] = jnp.sum(acc, axis=0, keepdims=True)
 
-    direct3, sens = pl.pallas_call(
+    direct_lanes, sens = pl.pallas_call(
         kernel,
         grid=(blocks,),
         in_specs=[
@@ -47,16 +52,17 @@
             pl.BlockSpec((monitor_count, 1), lambda g: (0, 0)),
         ],
         out_specs=[
-            pl.BlockSpec((None, monitor_count, sb), lambda g: (g, 0, 0)),
+            pl.BlockSpec((sb, monitor_count, lanes), lambda g: (g, 0, 0)),
             pl.BlockSpec((sb, outage_total), lambda g: (g, 0)),
         ],
         out_shape=[
-            jax.ShapeDtypeStruct((blocks, monitor_count, sb), jnp.float32),
+            jax.ShapeDtypeStruct((scen_rows, monitor_count, lanes), jnp.float32),
             jax.ShapeDtypeStruct((scen_rows, outage_total), jnp.float32),
         ],
     )(base3, outflow, lodf2, lim2)
-    direct = direct3.transpose(0, 2, 1).reshape(scen_rows, monitor_count) / (2.0 * outage_total)
+    direct = jnp.sum(direct_lanes, axis=2) / (2.0 * outage_total)
     return direct, sens / (2.0 * half)
+
 
 def exchange_sum(values, axis, count):
     blocks = values.reshape((count, values.shape[0] // count) + values.shape[1:])

time: 510 us -> 282 us (0.55)
  Pallas kernels: 253 us -> 19.6 us
  other arithmetic: 16.2 us -> 21.4 us
    pallas_call x1, Pallas kernels: 253 us -> 19.6 us  [penalty_slopes(): pl.pallas_call(kernel, grid=(blocks,), in_specs=[pl.BlockSpec((None, moni...]
    reduce_sum x0 -> x1, other arithmetic: none -> 7.89 us  [penalty_slopes(): direct = jnp.sum(direct_lanes, axis=2) / (2.0 * outage_total)]
  transfers between devices with their start and end apart: 4 -> 4, of which waited for: 4 -> 3; matrix products, arithmetic and copies ran while one was open for 3% -> 7% of each run, Pallas kernels for 0% -> 0%
where the time goes in v4:
time: 282 us; the launch traced here: 281 us
  waiting for transfers between devices  115 us (41%)
  blocking collectives  67.9 us (24%)
  starting transfers between devices  33.6 us (12%)
  other arithmetic  21.4 us (8%)
  Pallas kernels  19.6 us (7%)
  matrix products  13 us (5%)
  local copies, waits for them, and re-layouts  10.2 us (4%)
    all_to_all x3, waiting for transfers between devices, exchange_sum(): return jnp.sum(lax.all_to_all(blocks, axis, 0, 0, tiled=False), axis=0)  115 us
    all_to_all x1, blocking collectives, on_device(): lax.all_to_all(jnp.broadcast_to(piece[None], (bus_count,) + piece.shape),...  34.3 us
    all_to_all x3, starting transfers between devices, exchange_sum(): return jnp.sum(lax.all_to_all(blocks, axis, 0, 0, tiled=False), axis=0)  26.8 us
    pallas_call x1, Pallas kernels, penalty_slopes(): pl.pallas_call(kernel, grid=(blocks,), in_specs=[pl.BlockSpec((None, moni...  19.6 us
    all_gather x1, blocking collectives, on_device(): lax.all_gather(flow_field[:, monitor_count:], 'line', axis=1, tiled=True)  17.2 us
    all_gather x1, blocking collectives, on_device(): sens_total = lax.all_gather(sens_mine, 'line', axis=1, tiled=True)  16.5 us
    reduce_sum x1, other arithmetic, penalty_slopes(): direct = jnp.sum(direct_lanes, axis=2) / (2.0 * outage_total)  7.89 us
    all_to_all x1, starting transfers between devices, on_device(): mine = jnp.sum(lax.all_to_all(shares, 'line', 0, 0, tiled=False), axis=0)  6.79 us
  transfers between devices with their start and end apart: 4, of which 3 were waited for; matrix products, arithmetic and copies ran while one was open for 7% of the time, Pallas kernels for 0%

profile of v4, /device:TPU:7, one launch (start us, length us, event | category | flops | bytes accessed | tf_op | source)
XLA Modules:
  0.0 281.1 jit_solution(4228603197215569991)
XLA Ops:
  0.6 0.0 copy-start
  0.6 0.8 compare_and_fusion
  1.5 0.1 broadcast_in_dim.73
  1.6 0.1 broadcast_in_dim.75
  1.7 0.6 copy-done
  2.2 2.0 gather_fusion.1
  4.3 0.0 copy-start.4
  4.3 1.2 select_select_fusion
  5.5 6.4 %all-to-all-start = ((bf16[16,32,1024]{2,1,0:T(8,128)(2,1)}), bf16[16,32,1024]{2,1,0:T(8,128)(2,1)S(1)}, u32[]{:S(2)}, u32[]{:S(2)}) async-start(bf16[16,32,1024]{2,1,0:T(8,128)(2,1)} %select_select_fusion), calls=%async_computation | async-start | bytes 2097152 | tf_op jit(solution)/shard_map/all_to_all | solution.py:69
  12.0 0.0 copy-done.4
  12.0 0.0 copy-start.3
  12.0 0.0 copy-start.6
  12.0 2.7 gather_fusion
  14.7 2.2 broadcast_select_fusion
  16.9 0.0 copy-done.3
  16.9 0.0 copy-done.6
  16.9 4.8 %subtract_convert_fusion = bf16[1024,1024]{1,0:T(8,128)(2,1)} fusion(bf16[1024,1024]{1,0:T(8,128)(2,1)} %param.9, f32[24,1024]{1,0:T(8,128)S(1)} %copy-done.3, s32[1024]{0:T(1024)S(1)} %copy-done.6), kind=kOutput, calls=%fused_computation.2 | convolution fusion | flops 305160192 | bytes 4296704 | tf_op jit(solution)/shard_map/dot_general | solution.py:80
  21.7 5.2 %all-to-all-done = bf16[16,32,1024]{2,1,0:T(8,128)(2,1)S(1)} async-done(((bf16[16,32,1024]{2,1,0:T(8,128)(2,1)}), bf16[16,32,1024]{2,1,0:T(8,128)(2,1)S(1)}, u32[]{:S(2)}, u32[]{:S(2)}) %all-to-all-start) | async-done | bytes 1048608 | tf_op jit(solution)/shard_map/all_to_all | solution.py:69
  26.9 0.2 reduce_sum.57
  27.1 4.4 %fusion.5 = f32[1024,416]{1,0:T(8,128)} fusion(bf16[1024,1024]{1,0:T(8,128)(2,1)} %subtract_convert_fusion, bf16[32,1024]{1,0:T(8,128)(2,1)S(1)} %reduce_sum.57, bf16[384,1024]{1,0:T(8,128)(2,1)} %broadcast_select_fusion), kind=kOutput, calls=%fused_computation.13 | convolution fusion | flops 874119168 | bytes 4653056 | tf_op jit(solution)/shard_map/dot_general | solution.py:101
  31.5 0.0 copy-start.8
  31.5 0.0 copy-start.5
  31.5 0.0 copy-start.2
  31.5 10.2 %all-to-all-start.1 = ((f32[16,64,416]{2,1,0:T(8,128)}), f32[16,64,416]{2,1,0:T(8,128)}, u32[]{:S(2)}, u32[]{:S(2)}) async-start(f32[16,64,416]{2,1,0:T(8,128)} %bitcast.17), calls=%async_computation.1 | async-start | bytes 4194304 | tf_op jit(solution)/shard_map/all_to_all | solution.py:69
  41.7 0.0 copy-done.8
  41.7 0.8 reshape.74.lim_ref
  42.5 0.0 copy-done.5
  42.5 0.2 fusion.4
  42.7 0.2 concatenate.19
  43.0 0.1 pad.4.clone
  43.1 0.0 copy-done.2
  43.1 0.9 broadcast_multiply_fusion.lodf_ref
  44.0 48.8 %all-to-all-done.1 = f32[16,64,416]{2,1,0:T(8,128)} async-done(((f32[16,64,416]{2,1,0:T(8,128)}), f32[16,64,416]{2,1,0:T(8,128)}, u32[]{:S(2)}, u32[]{:S(2)}) %all-to-all-start.1) | async-done | bytes 1703968 | tf_op jit(solution)/shard_map/all_to_all | solution.py:69
  92.8 1.8 reduce_sum.58
  94.6 0.1 copy.44
  94.7 17.2 %all_gather.6 = f32[64,512]{0,1:T(8,128)S(1)} all-gather(f32[64,32]{0,1:T(8,128)S(1)} %copy.44), channel_id=1, replica_groups=mesh['bus'=16,'line'=16] {'line'}, dimensions={1}, use_global_device_ids=true | all-gather | bytes 139264 | tf_op jit(solution)/shard_map/all_gather | solution.py:106
  111.9 0.8 copy.45.out_ref
  112.6 1.7 copy.43
  114.3 19.6 %shard_map.112 = (f32[64,384,128]{2,1,0:T(8,128)}, f32[64,512]{1,0:T(8,128)}) custom-call(f32[8,384,8]{2,1,0:T(8,128)} %bitcast.15, f32[64,512]{1,0:T(8,128)} %copy.45.out_ref, f32[384,512]{1,0:T(8,128)} %broadcast_multiply_fusion.lodf_ref, f32[384,1]{1,0:T(8,128)} %reshape.74.lim_ref), custom_call_target="tpu_custom_call" | custom-call | tf_op jit(solution)/shard_map/pallas_call | solution.py:45
  133.9 0.9 broadcast_multiply_fusion.2
  134.8 0.1 copy.47
  134.9 0.9 maximum_bitcast_fusion
  135.8 6.8 %all-to-all-start.2 = ((f32[16,72,32]{1,2,0:T(8,128)}), f32[16,72,32]{1,2,0:T(8,128)S(1)}, u32[]{:S(2)}, u32[]{:S(2)}) async-start(f32[16,72,32]{1,2,0:T(8,128)} %maximum_bitcast_fusion), calls=%async_computation.2 | async-start | bytes 524288 | tf_op jit(solution)/shard_map/all_to_all | solution.py:117
  142.6 7.9 %reduce_sum.59 = f32[64,384]{1,0:T(8,128)S(1)} reduce(f32[64,384,128]{2,1,0:T(8,128)} %get-tuple-element.5, f32[]{:T(128)} %constant.32.clone.1), dimensions={2}, to_apply=%region_2.3 | reduce | flops 3121152 | bytes 12681220 | tf_op jit(solution)/shard_map/reduce_sum | solution.py:63
  150.5 0.0 all-to-all-done.2
  150.5 0.0 copy-start.1
  150.5 16.5 %all_gather.7 = f32[64,512]{0,1:T(8,128)S(1)} all-gather(f32[64,32]{0,1:T(8,128)S(1)} %bitcast.19), channel_id=1, replica_groups=mesh['bus'=16,'line'=16] {'line'}, dimensions={1}, use_global_device_ids=true | all-gather | bytes 139264 | tf_op jit(solution)/shard_map/all_gather | solution.py:120
  167.0 0.1 copy.54
  167.1 0.2 fusion.12
  167.3 0.5 fusion
  167.8 0.1 broadcast_in_dim.84
  167.9 34.3 %all_to_all.25 = bf16[16,64,416]{2,1,0:T(8,128)(2,1)S(1)} all-to-all(bf16[16,64,416]{2,1,0:T(8,128)(2,1)S(1)} %broadcast_in_dim.84), channel_id=1, replica_groups=mesh['bus'=16,'line'=16] {'bus'}, dimensions={0} | all-to-all | bytes 1703936 | tf_op jit(solution)/shard_map/all_to_all | solution.py:132
  202.2 0.0 copy-done.1
  202.2 3.2 %fusion.2 = f32[16,64,1024]{2,1,0:T(8,128)} fusion(bf16[16,64,416]{2,1,0:T(8,128)(2,1)S(1)} %all_to_all.25, bf16[32,1024]{1,0:T(8,128)(2,1)S(1)} %reduce_sum.57, bf16[384,1024]{1,0:T(8,128)(2,1)S(1)} %copy-done.1), kind=kOutput, calls=%fused_computation.9 | convolution fusion | flops 874119168 | bytes 5898240 | tf_op jit(solution)/shard_map/dot_general | solution.py:137
  205.5 10.2 %all-to-all-start.4 = ((f32[16,64,1024]{2,1,0:T(8,128)}), f32[16,64,1024]{2,1,0:T(8,128)}, u32[]{:S(2)}, u32[]{:S(2)}) async-start(f32[16,64,1024]{2,1,0:T(8,128)} %fusion.2), calls=%async_computation.4 | async-start | bytes 8388608 | tf_op jit(solution)/shard_map/all_to_all | solution.py:69
  215.7 0.8 copy.52
  216.5 0.0 copy-start.7
  216.5 60.5 %all-to-all-done.4 = f32[16,64,1024]{2,1,0:T(8,128)} async-done(((f32[16,64,1024]{2,1,0:T(8,128)}), f32[16,64,1024]{2,1,0:T(8,128)}, u32[]{:S(2)}, u32[]{:S(2)}) %all-to-all-start.4) | async-done | bytes 4194336 | tf_op jit(solution)/shard_map/all_to_all | solution.py:69
  277.0 2.5 reduce_sum.62
  279.5 0.0 copy-done.7
  279.5 1.6 add_convert_fusion
  (11 shorter events, 0.1 us)
Async XLA Ops:
  0.6 1.6 copy-start
  4.3 7.7 %copy-start.4 = (s32[384]{0:T(512)S(1)}, s32[384]{0:T(512)}, u32[]{:S(2)}) copy-start(s32[384]{0:T(512)} %param.15) | copy-start | bytes 4612
  5.5 21.4 %all-to-all-start = ((bf16[16,32,1024]{2,1,0:T(8,128)(2,1)}), bf16[16,32,1024]{2,1,0:T(8,128)(2,1)S(1)}, u32[]{:S(2)}, u32[]{:S(2)}) async-start(bf16[16,32,1024]{2,1,0:T(8,128)(2,1)} %select_select_fusion), calls=%async_computation | async-start | bytes 2097152 | tf_op jit(solution)/shard_map/all_to_all | solution.py:69
  12.0 4.9 %copy-start.3 = (f32[24,1024]{1,0:T(8,128)S(1)}, f32[24,1024]{1,0:T(8,128)}, u32[]{:S(2)}) copy-start(f32[24,1024]{1,0:T(8,128)} %param.10) | copy-start | bytes 294916
  12.0 4.9 %copy-start.6 = (s32[1024]{0:T(1024)S(1)}, s32[1024]{0:T(1024)}, u32[]{:S(2)}) copy-start(s32[1024]{0:T(1024)} %param.11) | copy-start | bytes 12292
  31.5 10.2 %copy-start.8 = (f32[384]{0:T(512)S(1)}, f32[384]{0:T(512)}, u32[]{:S(2)}) copy-start(f32[384]{0:T(512)} %param.14) | copy-start | bytes 4612
  31.5 11.0 %copy-start.5 = (s32[512]{0:T(512)S(1)}, s32[512]{0:T(512)}, u32[]{:S(2)}) copy-start(s32[512]{0:T(512)} %param.16) | copy-start | bytes 6148
  31.5 11.6 %copy-start.2 = (f32[384,512]{1,0:T(8,128)S(1)}, f32[384,512]{1,0:T(8,128)}, u32[]{:S(2)}) copy-start(f32[384,512]{1,0:T(8,128)} %param.13) | copy-start | bytes 2359300
  31.5 61.3 %all-to-all-start.1 = ((f32[16,64,416]{2,1,0:T(8,128)}), f32[16,64,416]{2,1,0:T(8,128)}, u32[]{:S(2)}, u32[]{:S(2)}) async-start(f32[16,64,416]{2,1,0:T(8,128)} %bitcast.17), calls=%async_computation.1 | async-start | bytes 4194304 | tf_op jit(solution)/shard_map/all_to_all | solution.py:69
  135.8 14.7 %all-to-all-start.2 = ((f32[16,72,32]{1,2,0:T(8,128)}), f32[16,72,32]{1,2,0:T(8,128)S(1)}, u32[]{:S(2)}, u32[]{:S(2)}) async-start(f32[16,72,32]{1,2,0:T(8,128)} %maximum_bitcast_fusion), calls=%async_computation.2 | async-start | bytes 524288 | tf_op jit(solution)/shard_map/all_to_all | solution.py:117
  150.5 51.7 %copy-start.1 = (bf16[384,1024]{1,0:T(8,128)(2,1)S(1)}, bf16[384,1024]{1,0:T(8,128)(2,1)}, u32[]{:S(2)}) copy-start(bf16[384,1024]{1,0:T(8,128)(2,1)} %broadcast_select_fusion) | copy-start | bytes 2359300
  205.5 71.5 %all-to-all-start.4 = ((f32[16,64,1024]{2,1,0:T(8,128)}), f32[16,64,1024]{2,1,0:T(8,128)}, u32[]{:S(2)}, u32[]{:S(2)}) async-start(f32[16,64,1024]{2,1,0:T(8,128)} %fusion.2), calls=%async_computation.4 | async-start | bytes 8388608 | tf_op jit(solution)/shard_map/all_to_all | solution.py:69
  216.5 63.0 %copy-start.7 = (f32[1024]{0:T(1024)S(1)}, f32[1024]{0:T(1024)}, u32[]{:S(2)}) copy-start(f32[1024]{0:T(1024)} %param.17) | copy-start | bytes 12292

commit v5 on v4

--- a/solution.py
+++ b/solution.py
@@ -69,6 +69,12 @@
     return jnp.sum(lax.all_to_all(blocks, axis, 0, 0, tiled=False), axis=0)
 
 
+def gather_columns(values, axis, count):
+    copies = jnp.broadcast_to(values[None], (count,) + values.shape)
+    gathered = lax.all_to_all(copies, axis, 0, 0, tiled=False)
+    return gathered.transpose(1, 0, 2).reshape(values.shape[0], count * values.shape[1])
+
+
 def on_device(
     generation, profiles, scen_profile, ptdf, lodf, limits, monitored, outages, cost_quad
 ):
@@ -103,7 +109,7 @@
     )
     flow_field = exchange_sum(flow_part, "bus", lax.axis_size("bus"))
     base = flow_field[:, :monitor_count]
-    outflow = lax.all_gather(flow_field[:, monitor_count:], "line", axis=1, tiled=True)
+    outflow = gather_columns(flow_field[:, monitor_count:], "line", line_count)
 
     direct, sens_part = penalty_slopes(base, outflow, lodf, limits)
 
@@ -117,7 +123,7 @@
     mine = jnp.sum(lax.all_to_all(shares, "line", 0, 0, tiled=False), axis=0)
     sens_mine = mine[:scen_rows]
     flag_mine = mine[scen_rows]
-    sens_total = lax.all_gather(sens_mine, "line", axis=1, tiled=True)
+    sens_total = gather_columns(sens_mine, "line", line_count)
     backward = sens_total / outage_total
     outage_sens = sens_total / math.sqrt(monitored_total)
 

time: 282 us -> 268 us (0.950)
  blocking collectives: 67.9 us -> 33.2 us
  starting transfers between devices: 33.6 us -> 42.3 us
  waiting for transfers between devices: 115 us -> 122 us
    all_gather x2 -> x0, blocking collectives: 33.6 us -> none  [the longest x1 17.2 us: on_device(): lax.all_gather(flow_field[:, monitor_count:], 'line', axis=1, tiled=True)]
    all_to_all x0 -> x2, starting transfers between devices: none -> 12 us  [gather_columns(): gathered = lax.all_to_all(copies, axis, 0, 0, tiled=False)]
    all_to_all x0 -> x2, waiting for transfers between devices: none -> 5.99 us  [gather_columns(): gathered = lax.all_to_all(copies, axis, 0, 0, tiled=False)]
  transfers between devices with their start and end apart: 4 -> 6, of which waited for: 3 -> 5; matrix products, arithmetic and copies ran while one was open for 7% -> 8% of each run, Pallas kernels for 0% -> 0%
where the time goes in v5:
time: 268 us; the launch traced here: 267 us
  waiting for transfers between devices  122 us (46%)
  starting transfers between devices  42.3 us (16%)
  blocking collectives  33.2 us (12%)
  other arithmetic  23.3 us (9%)
  Pallas kernels  19.6 us (7%)
  matrix products  12.9 us (5%)
  local copies, waits for them, and re-layouts  12.6 us (5%)
    all_to_all x3, waiting for transfers between devices, exchange_sum(): return jnp.sum(lax.all_to_all(blocks, axis, 0, 0, tiled=False), axis=0)  116 us
    all_to_all x1, blocking collectives, on_device(): lax.all_to_all(jnp.broadcast_to(piece[None], (bus_count,) + piece.shape),...  33.2 us
    all_to_all x3, starting transfers between devices, exchange_sum(): return jnp.sum(lax.all_to_all(blocks, axis, 0, 0, tiled=False), axis=0)  24.8 us
    pallas_call x1, Pallas kernels, penalty_slopes(): pl.pallas_call(kernel, grid=(blocks,), in_specs=[pl.BlockSpec((None, moni...  19.6 us
    all_to_all x2, starting transfers between devices, gather_columns(): gathered = lax.all_to_all(copies, axis, 0, 0, tiled=False)  12 us
    reduce_sum x1, other arithmetic, penalty_slopes(): direct = jnp.sum(direct_lanes, axis=2) / (2.0 * outage_total)  7.89 us
    all_to_all x2, waiting for transfers between devices, gather_columns(): gathered = lax.all_to_all(copies, axis, 0, 0, tiled=False)  5.99 us
    all_to_all x1, starting transfers between devices, on_device(): mine = jnp.sum(lax.all_to_all(shares, 'line', 0, 0, tiled=False), axis=0)  5.48 us
  transfers between devices with their start and end apart: 6, of which 5 were waited for; matrix products, arithmetic and copies ran while one was open for 8% of the time, Pallas kernels for 0%

profile of v5, /device:TPU:7, one launch (start us, length us, event | category | flops | bytes accessed | tf_op | source)
XLA Modules:
  0.0 266.8 jit_solution(11877698422899231446)
XLA Ops:
  0.6 0.0 copy-start
  0.6 0.8 compare_and_fusion
  1.5 0.1 broadcast_in_dim.85
  1.6 0.1 broadcast_in_dim.87
  1.7 0.6 copy-done
  2.2 2.0 gather_fusion.1
  4.3 0.0 copy-start.4
  4.3 1.2 select_select_fusion
  5.5 6.4 %all-to-all-start = ((bf16[16,32,1024]{2,1,0:T(8,128)(2,1)}), bf16[16,32,1024]{2,1,0:T(8,128)(2,1)S(1)}, u32[]{:S(2)}, u32[]{:S(2)}) async-start(bf16[16,32,1024]{2,1,0:T(8,128)(2,1)} %select_select_fusion), calls=%async_computation | async-start | bytes 2097152 | tf_op jit(solution)/shard_map/all_to_all | solution.py:69
  12.0 0.0 copy-done.4
  12.0 0.0 copy-start.3
  12.0 0.0 copy-start.6
  12.0 2.7 %gather_fusion = bf16[384,1024]{1,0:T(8,128)(2,1)} fusion(bf16[1024,1024]{1,0:T(8,128)(2,1)S(1)} %copy-done, s32[1024]{0:T(1024)S(1)} %pad_clamp_fusion.1), kind=kCustom, calls=%fused_computation | custom fusion | bytes 1574400 | tf_op jit(solution)/shard_map/jit(_take)/gather | solution.py:104
  14.7 2.2 broadcast_select_fusion
  16.9 0.0 copy-done.3
  16.9 0.0 copy-done.6
  16.9 4.8 %subtract_convert_fusion = bf16[1024,1024]{1,0:T(8,128)(2,1)} fusion(bf16[1024,1024]{1,0:T(8,128)(2,1)} %param.9, f32[24,1024]{1,0:T(8,128)S(1)} %copy-done.3, s32[1024]{0:T(1024)S(1)} %copy-done.6), kind=kOutput, calls=%fused_computation.2 | convolution fusion | flops 305160192 | bytes 4296704 | tf_op jit(solution)/shard_map/dot_general | solution.py:86
  21.7 5.2 %all-to-all-done = bf16[16,32,1024]{2,1,0:T(8,128)(2,1)S(1)} async-done(((bf16[16,32,1024]{2,1,0:T(8,128)(2,1)}), bf16[16,32,1024]{2,1,0:T(8,128)(2,1)S(1)}, u32[]{:S(2)}, u32[]{:S(2)}) %all-to-all-start) | async-done | bytes 1048608 | tf_op jit(solution)/shard_map/all_to_all | solution.py:69
  26.9 0.2 reduce_sum.57
  27.1 4.4 %fusion.5 = f32[1024,416]{1,0:T(8,128)} fusion(bf16[1024,1024]{1,0:T(8,128)(2,1)} %subtract_convert_fusion, bf16[32,1024]{1,0:T(8,128)(2,1)S(1)} %reduce_sum.57, bf16[384,1024]{1,0:T(8,128)(2,1)} %broadcast_select_fusion), kind=kOutput, calls=%fused_computation.13 | convolution fusion | flops 874119168 | bytes 4653056 | tf_op jit(solution)/shard_map/dot_general | solution.py:107
  31.5 10.2 %all-to-all-start.1 = ((f32[16,64,416]{2,1,0:T(8,128)}), f32[16,64,416]{2,1,0:T(8,128)}, u32[]{:S(2)}, u32[]{:S(2)}) async-start(f32[16,64,416]{2,1,0:T(8,128)} %bitcast.34), calls=%async_computation.1 | async-start | bytes 4194304 | tf_op jit(solution)/shard_map/all_to_all | solution.py:69
  41.7 0.0 copy-done.8
  41.7 0.0 copy-done.2
  41.7 0.0 copy-start.5
  41.7 0.9 broadcast_multiply_fusion.lodf_ref
  42.7 50.1 %all-to-all-done.1 = f32[16,64,416]{2,1,0:T(8,128)} async-done(((f32[16,64,416]{2,1,0:T(8,128)}), f32[16,64,416]{2,1,0:T(8,128)}, u32[]{:S(2)}, u32[]{:S(2)}) %all-to-all-start.1) | async-done | bytes 1703968 | tf_op jit(solution)/shard_map/all_to_all | solution.py:69
  92.8 1.8 reduce_sum.58
  94.6 0.1 copy.55
  94.7 0.8 reshape.87
  95.6 6.3 %all-to-all-start.2 = ((f32[16,1,2048]{2,1,0:T(1,128)}), f32[16,1,2048]{2,1,0:T(1,128)S(1)}, u32[]{:S(2)}, u32[]{:S(2)}) async-start(f32[16,1,2048]{2,1,0:T(1,128)} %reshape.87), calls=%async_computation.2 | async-start | bytes 262144 | tf_op jit(solution)/shard_map/all_to_all | solution.py:74
  101.8 0.0 copy-done.5
  101.8 0.2 fusion.4
  102.1 0.8 reshape.85.lim_ref
  102.9 0.2 concatenate.19
  103.1 0.1 pad.4.clone
  103.2 1.7 copy.54
  104.9 1.6 all-to-all-done.2
  106.5 0.5 broadcast.43
  107.0 0.9 reduce.3
  107.9 0.1 reshape.88
  108.1 0.8 copy.56.out_ref
  108.8 19.6 %shard_map.112 = (f32[64,384,128]{2,1,0:T(8,128)}, f32[64,512]{1,0:T(8,128)}) custom-call(f32[8,384,8]{2,1,0:T(8,128)} %bitcast.32, f32[64,512]{1,0:T(8,128)} %copy.56.out_ref, f32[384,512]{1,0:T(8,128)} %broadcast_multiply_fusion.lodf_ref, f32[384,1]{1,0:T(8,128)} %reshape.85.lim_ref), custom_call_target="tpu_custom_call" | custom-call | tf_op jit(solution)/shard_map/pallas_call | solution.py:45
  128.4 0.9 broadcast_multiply_fusion.3
  129.3 0.1 copy.58
  129.5 0.9 maximum_bitcast_fusion
  130.3 5.5 %all-to-all-start.3 = ((f32[16,72,32]{1,2,0:T(8,128)}), f32[16,72,32]{1,2,0:T(8,128)S(1)}, u32[]{:S(2)}, u32[]{:S(2)}) async-start(f32[16,72,32]{1,2,0:T(8,128)} %maximum_bitcast_fusion), calls=%async_computation.3 | async-start | bytes 524288 | tf_op jit(solution)/shard_map/all_to_all | solution.py:123
  135.8 7.9 %reduce_sum.59 = f32[64,384]{1,0:T(8,128)S(1)} reduce(f32[64,384,128]{2,1,0:T(8,128)} %get-tuple-element.5, f32[]{:T(128)} %constant.32.clone.1), dimensions={2}, to_apply=%region_2.3 | reduce | flops 3121152 | bytes 12681220 | tf_op jit(solution)/shard_map/reduce_sum | solution.py:63
  143.7 0.0 all-to-all-done.3
  143.8 0.8 reshape.89
  144.6 5.8 %all-to-all-start.4 = ((f32[16,1,2048]{2,1,0:T(1,128)}), f32[16,1,2048]{2,1,0:T(1,128)S(1)}, u32[]{:S(2)}, u32[]{:S(2)}) async-start(f32[16,1,2048]{2,1,0:T(1,128)} %reshape.89), calls=%async_computation.4 | async-start | bytes 262144 | tf_op jit(solution)/shard_map/all_to_all | solution.py:74
  150.4 0.2 fusion.10
  150.5 0.1 copy.65
  150.6 4.4 %all-to-all-done.4 = f32[16,1,2048]{2,1,0:T(1,128)S(1)} async-done(((f32[16,1,2048]{2,1,0:T(1,128)}), f32[16,1,2048]{2,1,0:T(1,128)S(1)}, u32[]{:S(2)}, u32[]{:S(2)}) %all-to-all-start.4) | async-done | bytes 131104 | tf_op jit(solution)/shard_map/all_to_all | solution.py:74
  155.0 0.9 reduce.4
  156.0 0.1 reshape.90
  156.1 0.5 fusion
  156.6 0.1 broadcast_in_dim.98
  156.7 33.2 %all_to_all.35 = bf16[16,64,416]{2,1,0:T(8,128)(2,1)S(1)} all-to-all(bf16[16,64,416]{2,1,0:T(8,128)(2,1)S(1)} %broadcast_in_dim.98), channel_id=1, replica_groups=mesh['bus'=16,'line'=16] {'bus'}, dimensions={0} | all-to-all | bytes 1703936 | tf_op jit(solution)/shard_map/all_to_all | solution.py:138
  190.0 3.2 %fusion.2 = f32[16,64,1024]{2,1,0:T(8,128)} fusion(bf16[16,64,416]{2,1,0:T(8,128)(2,1)S(1)} %all_to_all.35, bf16[32,1024]{1,0:T(8,128)(2,1)S(1)} %reduce_sum.57, bf16[384,1024]{1,0:T(8,128)(2,1)S(1)} %copy-done.1), kind=kOutput, calls=%fused_computation.9 | convolution fusion | flops 874119168 | bytes 5898240 | tf_op jit(solution)/shard_map/dot_general | solution.py:143
  193.2 8.2 %all-to-all-start.6 = ((f32[16,64,1024]{2,1,0:T(8,128)}), f32[16,64,1024]{2,1,0:T(8,128)}, u32[]{:S(2)}, u32[]{:S(2)}) async-start(f32[16,64,1024]{2,1,0:T(8,128)} %fusion.2), calls=%async_computation.6 | async-start | bytes 8388608 | tf_op jit(solution)/shard_map/all_to_all | solution.py:69
  201.4 0.8 copy.63
  202.2 60.6 %all-to-all-done.6 = f32[16,64,1024]{2,1,0:T(8,128)} async-done(((f32[16,64,1024]{2,1,0:T(8,128)}), f32[16,64,1024]{2,1,0:T(8,128)}, u32[]{:S(2)}, u32[]{:S(2)}) %all-to-all-start.6) | async-done | bytes 4194336 | tf_op jit(solution)/shard_map/all_to_all | solution.py:69
  262.7 2.5 reduce_sum.62
  265.2 1.6 add_convert_fusion
  (19 shorter events, 0.2 us)
Async XLA Ops:
  0.6 1.6 copy-start
  4.3 7.7 %copy-start.4 = (s32[384]{0:T(512)S(1)}, s32[384]{0:T(512)}, u32[]{:S(2)}) copy-start(s32[384]{0:T(512)} %param.15) | copy-start | bytes 4612
  5.5 21.4 %all-to-all-start = ((bf16[16,32,1024]{2,1,0:T(8,128)(2,1)}), bf16[16,32,1024]{2,1,0:T(8,128)(2,1)S(1)}, u32[]{:S(2)}, u32[]{:S(2)}) async-start(bf16[16,32,1024]{2,1,0:T(8,128)(2,1)} %select_select_fusion), calls=%async_computation | async-start | bytes 2097152 | tf_op jit(solution)/shard_map/all_to_all | solution.py:69
  12.0 4.9 %copy-start.3 = (f32[24,1024]{1,0:T(8,128)S(1)}, f32[24,1024]{1,0:T(8,128)}, u32[]{:S(2)}) copy-start(f32[24,1024]{1,0:T(8,128)} %param.10) | copy-start | bytes 294916
  12.0 4.9 %copy-start.6 = (s32[1024]{0:T(1024)S(1)}, s32[1024]{0:T(1024)}, u32[]{:S(2)}) copy-start(s32[1024]{0:T(1024)} %param.11) | copy-start | bytes 12292
  31.5 10.2 %copy-start.8 = (f32[384]{0:T(512)S(1)}, f32[384]{0:T(512)}, u32[]{:S(2)}) copy-start(f32[384]{0:T(512)} %param.14) | copy-start | bytes 4612
  31.5 10.2 %copy-start.2 = (f32[384,512]{1,0:T(8,128)S(1)}, f32[384,512]{1,0:T(8,128)}, u32[]{:S(2)}) copy-start(f32[384,512]{1,0:T(8,128)} %param.13) | copy-start | bytes 2359300
  31.5 61.3 %all-to-all-start.1 = ((f32[16,64,416]{2,1,0:T(8,128)}), f32[16,64,416]{2,1,0:T(8,128)}, u32[]{:S(2)}, u32[]{:S(2)}) async-start(f32[16,64,416]{2,1,0:T(8,128)} %bitcast.34), calls=%async_computation.1 | async-start | bytes 4194304 | tf_op jit(solution)/shard_map/all_to_all | solution.py:69
  41.7 60.1 %copy-start.5 = (s32[512]{0:T(512)S(1)}, s32[512]{0:T(512)}, u32[]{:S(2)}) copy-start(s32[512]{0:T(512)} %param.16) | copy-start | bytes 6148
  95.6 10.9 %all-to-all-start.2 = ((f32[16,1,2048]{2,1,0:T(1,128)}), f32[16,1,2048]{2,1,0:T(1,128)S(1)}, u32[]{:S(2)}, u32[]{:S(2)}) async-start(f32[16,1,2048]{2,1,0:T(1,128)} %reshape.87), calls=%async_computation.2 | async-start | bytes 262144 | tf_op jit(solution)/shard_map/all_to_all | solution.py:74
  130.3 13.4 %all-to-all-start.3 = ((f32[16,72,32]{1,2,0:T(8,128)}), f32[16,72,32]{1,2,0:T(8,128)S(1)}, u32[]{:S(2)}, u32[]{:S(2)}) async-start(f32[16,72,32]{1,2,0:T(8,128)} %maximum_bitcast_fusion), calls=%async_computation.3 | async-start | bytes 524288 | tf_op jit(solution)/shard_map/all_to_all | solution.py:123
  144.6 10.4 %all-to-all-start.4 = ((f32[16,1,2048]{2,1,0:T(1,128)}), f32[16,1,2048]{2,1,0:T(1,128)S(1)}, u32[]{:S(2)}, u32[]{:S(2)}) async-start(f32[16,1,2048]{2,1,0:T(1,128)} %reshape.89), calls=%async_computation.4 | async-start | bytes 262144 | tf_op jit(solution)/shard_map/all_to_all | solution.py:74
  156.1 33.9 %copy-start.1 = (bf16[384,1024]{1,0:T(8,128)(2,1)S(1)}, bf16[384,1024]{1,0:T(8,128)(2,1)}, u32[]{:S(2)}) copy-start(bf16[384,1024]{1,0:T(8,128)(2,1)} %broadcast_select_fusion) | copy-start | bytes 2359300
  193.2 69.5 %all-to-all-start.6 = ((f32[16,64,1024]{2,1,0:T(8,128)}), f32[16,64,1024]{2,1,0:T(8,128)}, u32[]{:S(2)}, u32[]{:S(2)}) async-start(f32[16,64,1024]{2,1,0:T(8,128)} %fusion.2), calls=%async_computation.6 | async-start | bytes 8388608 | tf_op jit(solution)/shard_map/all_to_all | solution.py:69
  202.2 63.0 %copy-start.7 = (f32[1024]{0:T(1024)S(1)}, f32[1024]{0:T(1024)}, u32[]{:S(2)}) copy-start(f32[1024]{0:T(1024)} %param.17) | copy-start | bytes 12292

commit v6 on v5

--- a/solution.py
+++ b/solution.py
@@ -4,9 +4,11 @@
 import jax.numpy as jnp
 from jax import lax
 from jax.experimental import pallas as pl
-from jax.sharding import PartitionSpec as P
+from jax.sharding import Mesh, PartitionSpec as P
 
 sharpness = 4.0
+BUS = ("y", "zh")
+LINE = ("zl", "x", "core")
 
 
 def penalty_slopes(base, outflow, lodf, limits):
@@ -75,19 +77,33 @@
     return gathered.transpose(1, 0, 2).reshape(values.shape[0], count * values.shape[1])
 
 
+def gather_rows(values, axis):
+    count = lax.axis_size(axis)
+    copies = jnp.broadcast_to(values[None], (count,) + values.shape)
+    gathered = lax.all_to_all(copies, axis, 0, 0, tiled=False)
+    return gathered.reshape((count * values.shape[0],) + values.shape[1:])
+
+
+def line_index():
+    index = lax.axis_index(LINE[0])
+    for name in LINE[1:]:
+        index = index * lax.axis_size(name) + lax.axis_index(name)
+    return index
+
+
 def on_device(
     generation, profiles, scen_profile, ptdf, lodf, limits, monitored, outages, cost_quad
 ):
-    line_count = lax.axis_size("line")
+    line_count = lax.axis_size(LINE)
     profile_count = profiles.shape[0]
     profile_pick = (
         scen_profile[:, None] == jnp.arange(profile_count, dtype=jnp.int32)[None, :]
     ).astype(jnp.float32)
     loads = jnp.dot(profile_pick, profiles, precision=lax.Precision.HIGHEST)
     injection = (generation.astype(jnp.float32) - loads).astype(jnp.bfloat16)
-    scen_rows = injection.shape[0] // lax.axis_size("bus")
+    scen_rows = injection.shape[0] // lax.axis_size(BUS)
     line_rows = ptdf.shape[0]
-    first_line = lax.axis_index("line") * line_rows
+    first_line = line_index() * line_rows
     local_monitored = monitored - first_line
     monitor_count = monitored.shape[0]
     outage_total = outages.shape[0]
@@ -100,16 +116,18 @@
         jnp.take(ptdf, jnp.clip(rel_outages, 0, line_rows - 1), axis=0),
         jnp.zeros((), ptdf.dtype),
     )
-    my_outage_rows = exchange_sum(outage_rows, "line", line_count)
+    my_outage_rows = exchange_sum(outage_rows, LINE, line_count)
     monitored_rows = jnp.take(ptdf, local_monitored, axis=0)
     rows = jnp.concatenate([monitored_rows, my_outage_rows], axis=0)
 
     flow_part = lax.dot_general(
         injection, rows, (((1,), (1,)), ((), ())), preferred_element_type=jnp.float32
     )
-    flow_field = exchange_sum(flow_part, "bus", lax.axis_size("bus"))
+    flow_field = exchange_sum(
+        exchange_sum(flow_part, "y", lax.axis_size("y")), "zh", lax.axis_size("zh")
+    )
     base = flow_field[:, :monitor_count]
-    outflow = gather_columns(flow_field[:, monitor_count:], "line", line_count)
+    outflow = gather_columns(flow_field[:, monitor_count:], LINE, line_count)
 
     direct, sens_part = penalty_slopes(base, outflow, lodf, limits)
 
@@ -120,10 +138,10 @@
     )
     out_share = outage_total // line_count
     shares = extended.reshape(extended.shape[0], line_count, out_share).transpose(1, 0, 2)
-    mine = jnp.sum(lax.all_to_all(shares, "line", 0, 0, tiled=False), axis=0)
+    mine = jnp.sum(lax.all_to_all(shares, LINE, 0, 0, tiled=False), axis=0)
     sens_mine = mine[:scen_rows]
     flag_mine = mine[scen_rows]
-    sens_total = gather_columns(sens_mine, "line", line_count)
+    sens_total = gather_columns(sens_mine, LINE, line_count)
     backward = sens_total / outage_total
     outage_sens = sens_total / math.sqrt(monitored_total)
 
@@ -134,37 +152,35 @@
         flag_mine[None, :] > 0.5, 0.0, sens_mine / outage_total
     ).astype(jnp.bfloat16)
     piece = jnp.concatenate([adjoint_monitored, adjoint_outage], axis=1)
-    bus_count = lax.axis_size("bus")
-    all_piece = lax.all_to_all(
-        jnp.broadcast_to(piece[None], (bus_count,) + piece.shape), "bus", 0, 0, tiled=False
-    ).reshape(bus_count * piece.shape[0], piece.shape[1])
+    all_piece = gather_rows(gather_rows(piece, "zh"), "y")
     grad_rows = all_piece.shape[0] // line_count
     pushed = exchange_sum(
-        jnp.dot(all_piece, rows, preferred_element_type=jnp.float32), "line", line_count
+        jnp.dot(all_piece, rows, preferred_element_type=jnp.float32), LINE, line_count
     )
     own_generation = lax.dynamic_slice_in_dim(
-        generation, lax.axis_index("line") * grad_rows, grad_rows, 0
+        generation, line_index() * grad_rows, grad_rows, 0
     ).astype(jnp.float32)
     gradient = (cost_quad[None, :] * own_generation + pushed).astype(jnp.bfloat16)
     return (gradient, outflow, outage_sens)
 
 
 def solution(mesh):
+    fine = Mesh(mesh.devices.reshape(4, 4, 2, 4, 2), BUS + LINE)
     placed = (
-        P(None, "bus"),
-        P(None, "bus"),
+        P(None, BUS),
+        P(None, BUS),
         P(),
-        P("line", "bus"),
-        P("line", None),
-        P("line"),
-        P("line"),
+        P(LINE, BUS),
+        P(LINE, None),
+        P(LINE),
+        P(LINE),
         P(),
-        P("bus"),
+        P(BUS),
     )
     return jax.shard_map(
         on_device,
-        mesh=mesh,
+        mesh=fine,
         in_specs=placed,
-        out_specs=(P("line", "bus"), P("bus", None), P("bus", None)),
+        out_specs=(P(LINE, BUS), P(BUS, None), P(BUS, None)),
         check_vma=False,
     )

time: 268 us -> 250 us (0.933)
  waiting for transfers between devices: 122 us -> 85.6 us
  blocking collectives: 33.2 us -> 52.5 us
  starting transfers between devices: 42.3 us -> 39.4 us
  local copies, waits for them, and re-layouts: 12.6 us -> 15.3 us
    all_to_all x3, waiting for transfers between devices: 116 us -> 79.7 us  [exchange_sum(): return jnp.sum(lax.all_to_all(blocks, axis, 0, 0, tiled=False), axis=0)]
    all_to_all x1 -> x3, blocking collectives: 33.2 us -> 52.5 us  [the longest x2 26.6 us: gather_rows(): gathered = lax.all_to_all(copies, axis, 0, 0, tiled=False)]
    all_to_all x3, starting transfers between devices: 24.8 us -> 21.9 us  [exchange_sum(): return jnp.sum(lax.all_to_all(blocks, axis, 0, 0, tiled=False), axis=0)]
  transfers between devices with their start and end apart: 6 -> 6, of which waited for: 5 -> 5; matrix products, arithmetic and copies ran while one was open for 8% -> 9% of each run, Pallas kernels for 0% -> 0%
where the time goes in v6:
time: 250 us; the launch traced here: 249 us
  waiting for transfers between devices  85.6 us (34%)
  blocking collectives  52.5 us (21%)
  starting transfers between devices  39.4 us (16%)
  other arithmetic  23.2 us (9%)
  Pallas kernels  19.6 us (8%)
  local copies, waits for them, and re-layouts  15.3 us (6%)
  matrix products  12.5 us (5%)
    all_to_all x3, waiting for transfers between devices, exchange_sum(): return jnp.sum(lax.all_to_all(blocks, axis, 0, 0, tiled=False), axis=0)  79.7 us
    all_to_all x2, blocking collectives, gather_rows(): gathered = lax.all_to_all(copies, axis, 0, 0, tiled=False)  26.6 us
    all_to_all x1, blocking collectives, exchange_sum(): return jnp.sum(lax.all_to_all(blocks, axis, 0, 0, tiled=False), axis=0)  25.9 us
    all_to_all x3, starting transfers between devices, exchange_sum(): return jnp.sum(lax.all_to_all(blocks, axis, 0, 0, tiled=False), axis=0)  21.9 us
    pallas_call x1, Pallas kernels, penalty_slopes(): pl.pallas_call(kernel, grid=(blocks,), in_specs=[pl.BlockSpec((None, moni...  19.6 us
    all_to_all x2, starting transfers between devices, gather_columns(): gathered = lax.all_to_all(copies, axis, 0, 0, tiled=False)  12.1 us
    reduce_sum x1, other arithmetic, penalty_slopes(): direct = jnp.sum(direct_lanes, axis=2) / (2.0 * outage_total)  7.89 us
    all_to_all x2, waiting for transfers between devices, gather_columns(): gathered = lax.all_to_all(copies, axis, 0, 0, tiled=False)  5.99 us
  transfers between devices with their start and end apart: 6, of which 5 were waited for; matrix products, arithmetic and copies ran while one was open for 9% of the time, Pallas kernels for 0%

profile of v6, /device:TPU:7, one launch (start us, length us, event | category | flops | bytes accessed | tf_op | source)
XLA Modules:
  0.0 249.2 jit_solution(8510252044589389083)
XLA Ops:
  0.6 0.0 copy-start
  0.7 0.8 compare_and_fusion
  1.5 0.1 broadcast_in_dim.92
  1.6 0.1 broadcast_in_dim.94
  1.7 0.6 copy-done
  2.2 2.0 gather_fusion.1
  4.3 0.0 copy-start.3
  4.3 1.2 select_select_fusion
  5.5 6.4 %all-to-all-start = ((bf16[16,32,1024]{2,1,0:T(8,128)(2,1)}), bf16[16,32,1024]{2,1,0:T(8,128)(2,1)S(1)}, u32[]{:S(2)}, u32[]{:S(2)}) async-start(bf16[16,32,1024]{2,1,0:T(8,128)(2,1)} %select_select_fusion), calls=%async_computation | async-start | bytes 2097152 | tf_op jit(solution)/shard_map/all_to_all | solution.py:71
  12.0 0.0 copy-start.2
  12.0 0.0 copy-start.5
  12.0 2.7 %gather_fusion = bf16[384,1024]{1,0:T(8,128)(2,1)} fusion(bf16[1024,1024]{1,0:T(8,128)(2,1)S(1)} %copy-done, s32[1024]{0:T(1024)S(1)} %pad_clamp_fusion.1), kind=kCustom, calls=%fused_computation | custom fusion | bytes 1574400 | tf_op jit(solution)/shard_map/jit(_take)/gather | solution.py:120
  14.7 2.2 broadcast_select_fusion
  16.9 4.9 %subtract_convert_fusion = bf16[1024,1024]{1,0:T(8,128)(2,1)} fusion(bf16[1024,1024]{1,0:T(8,128)(2,1)} %param.9, f32[24,1024]{1,0:T(8,128)S(1)} %copy-done.2, s32[1024]{0:T(1024)S(1)} %copy-done.5), kind=kOutput, calls=%fused_computation.2 | convolution fusion | flops 305160192 | bytes 4296704 | tf_op jit(solution)/shard_map/dot_general | solution.py:102
  21.7 5.2 %all-to-all-done = bf16[16,32,1024]{2,1,0:T(8,128)(2,1)S(1)} async-done(((bf16[16,32,1024]{2,1,0:T(8,128)(2,1)}), bf16[16,32,1024]{2,1,0:T(8,128)(2,1)S(1)}, u32[]{:S(2)}, u32[]{:S(2)}) %all-to-all-start) | async-done | bytes 1048608 | tf_op jit(solution)/shard_map/all_to_all | solution.py:71
  26.9 0.2 reduce_sum.66
  27.1 2.8 %fusion.5 = f32[1024,416]{0,1:T(8,128)S(1)} fusion(bf16[1024,1024]{1,0:T(8,128)(2,1)} %subtract_convert_fusion, bf16[32,1024]{1,0:T(8,128)(2,1)S(1)} %reduce_sum.66, bf16[384,1024]{1,0:T(8,128)(2,1)} %broadcast_select_fusion), kind=kOutput, calls=%fused_computation.14 | convolution fusion | flops 874119168 | bytes 4653056 | tf_op jit(solution)/shard_map/dot_general | solution.py:123
  29.9 0.2 copy.77
  30.1 25.9 %all_to_all.45 = f32[4,256,416]{1,2,0:T(8,128)} all-to-all(f32[4,256,416]{1,2,0:T(8,128)S(1)} %bitcast.38), channel_id=1, replica_groups=mesh['y'=4,'zh'=4,'zl'=2,'x'=4,'core'=2] {'y'}, dimensions={0} | all-to-all | bytes 3407872 | tf_op jit(solution)/shard_map/all_to_all | solution.py:71
  56.0 1.7 reduce_sum.67
  57.7 1.0 copy.60
  58.7 7.4 %all-to-all-start.2 = ((f32[4,64,416]{2,1,0:T(8,128)}), f32[4,64,416]{2,1,0:T(8,128)S(1)}, u32[]{:S(2)}, u32[]{:S(2)}) async-start(f32[4,64,416]{2,1,0:T(8,128)} %bitcast.1), calls=%async_computation.2 | async-start | bytes 1048576 | tf_op jit(solution)/shard_map/all_to_all | solution.py:71
  66.1 0.0 copy-done.7
  66.1 0.9 broadcast_multiply_fusion.lodf_ref
  67.1 13.9 %all-to-all-done.2 = f32[4,64,416]{2,1,0:T(8,128)S(1)} async-done(((f32[4,64,416]{2,1,0:T(8,128)}), f32[4,64,416]{2,1,0:T(8,128)S(1)}, u32[]{:S(2)}, u32[]{:S(2)}) %all-to-all-start.2) | async-done | bytes 426016 | tf_op jit(solution)/shard_map/all_to_all | solution.py:71
  81.1 0.1 copy.62
  81.2 0.8 reshape.92
  82.0 6.3 %all-to-all-start.3 = ((f32[16,1,2048]{2,1,0:T(1,128)}), f32[16,1,2048]{2,1,0:T(1,128)S(1)}, u32[]{:S(2)}, u32[]{:S(2)}) async-start(f32[16,1,2048]{2,1,0:T(1,128)} %reshape.92), calls=%async_computation.3 | async-start | bytes 262144 | tf_op jit(solution)/shard_map/all_to_all | solution.py:76
  88.3 0.2 fusion.4
  88.6 0.8 reshape.90.lim_ref
  89.3 0.2 concatenate.19
  89.6 0.1 pad.4.clone
  89.7 1.7 copy.61
  91.3 1.6 all-to-all-done.3
  93.0 0.5 broadcast.43
  93.5 0.9 reduce.3
  94.4 0.1 reshape.93
  94.5 0.8 copy.63.out_ref
  95.3 19.6 %shard_map.112 = (f32[64,384,128]{2,1,0:T(8,128)}, f32[64,512]{1,0:T(8,128)}) custom-call(f32[8,384,8]{2,1,0:T(8,128)} %bitcast.39, f32[64,512]{1,0:T(8,128)} %copy.63.out_ref, f32[384,512]{1,0:T(8,128)} %broadcast_multiply_fusion.lodf_ref, f32[384,1]{1,0:T(8,128)} %reshape.90.lim_ref), custom_call_target="tpu_custom_call" | custom-call | tf_op jit(solution)/shard_map/pallas_call | solution.py:47
  114.9 0.9 broadcast_multiply_fusion.3
  115.8 0.1 copy.65
  116.0 0.9 maximum_bitcast_fusion
  116.8 5.5 %all-to-all-start.4 = ((f32[16,72,32]{1,2,0:T(8,128)}), f32[16,72,32]{1,2,0:T(8,128)S(1)}, u32[]{:S(2)}, u32[]{:S(2)}) async-start(f32[16,72,32]{1,2,0:T(8,128)} %maximum_bitcast_fusion), calls=%async_computation.4 | async-start | bytes 524288 | tf_op jit(solution)/shard_map/all_to_all | solution.py:141
  122.3 7.9 %reduce_sum.69 = f32[64,384]{1,0:T(8,128)S(1)} reduce(f32[64,384,128]{2,1,0:T(8,128)} %get-tuple-element.5, f32[]{:T(128)} %constant.39.clone.1), dimensions={2}, to_apply=%region_3.4 | reduce | flops 3121152 | bytes 12681220 | tf_op jit(solution)/shard_map/reduce_sum | solution.py:65
  130.2 0.0 all-to-all-done.4
  130.3 0.8 reshape.94
  131.1 5.8 %all-to-all-start.5 = ((f32[16,1,2048]{2,1,0:T(1,128)}), f32[16,1,2048]{2,1,0:T(1,128)S(1)}, u32[]{:S(2)}, u32[]{:S(2)}) async-start(f32[16,1,2048]{2,1,0:T(1,128)} %reshape.94), calls=%async_computation.5 | async-start | bytes 262144 | tf_op jit(solution)/shard_map/all_to_all | solution.py:76
  136.8 0.2 fusion.10
  137.0 0.1 copy.74
  137.1 4.4 %all-to-all-done.5 = f32[16,1,2048]{2,1,0:T(1,128)S(1)} async-done(((f32[16,1,2048]{2,1,0:T(1,128)}), f32[16,1,2048]{2,1,0:T(1,128)S(1)}, u32[]{:S(2)}, u32[]{:S(2)}) %all-to-all-start.5) | async-done | bytes 131104 | tf_op jit(solution)/shard_map/all_to_all | solution.py:76
  141.5 0.9 reduce.4
  142.4 0.1 reshape.95
  142.6 0.5 fusion
  143.1 12.4 %all_to_all.46 = bf16[4,64,416]{2,1,0:T(8,128)(2,1)S(1)} all-to-all(bf16[4,64,416]{2,1,0:T(8,128)(2,1)S(1)} %broadcast_in_dim.105), channel_id=1, replica_groups=mesh['y'=4,'zh'=4,'zl'=2,'x'=4,'core'=2] {'zh'}, dimensions={0} | all-to-all | bytes 425984 | tf_op jit(solution)/shard_map/all_to_all | solution.py:83
  155.6 0.1 copy.69
  155.7 0.1 broadcast_in_dim.107
  155.8 14.1 %all_to_all.47 = bf16[4,256,416]{1,2,0:T(8,128)(2,1)} all-to-all(bf16[4,256,416]{1,2,0:T(8,128)(2,1)S(1)} %broadcast_in_dim.107), channel_id=1, replica_groups=mesh['y'=4,'zh'=4,'zl'=2,'x'=4,'core'=2] {'y'}, dimensions={0} | all-to-all | bytes 1703936 | tf_op jit(solution)/shard_map/all_to_all | solution.py:83
  169.9 1.4 copy.70
  171.4 4.3 %fusion.2 = f32[16,64,1024]{2,1,0:T(8,128)} fusion(bf16[16,64,416]{2,1,0:T(8,128)(2,1)S(1)} %bitcast.41, bf16[32,1024]{1,0:T(8,128)(2,1)S(1)} %reduce_sum.66, bf16[384,1024]{1,0:T(8,128)(2,1)} %broadcast_select_fusion), kind=kOutput, calls=%fused_computation.10 | convolution fusion | flops 874119168 | bytes 5898240 | tf_op jit(solution)/shard_map/dot_general | solution.py:158
  175.7 8.0 %all-to-all-start.8 = ((f32[16,64,1024]{2,1,0:T(8,128)}), f32[16,64,1024]{2,1,0:T(8,128)}, u32[]{:S(2)}, u32[]{:S(2)}) async-start(f32[16,64,1024]{2,1,0:T(8,128)} %fusion.2), calls=%async_computation.8 | async-start | bytes 8388608 | tf_op jit(solution)/shard_map/all_to_all | solution.py:71
  183.7 0.8 copy.72
  184.5 60.6 %all-to-all-done.8 = f32[16,64,1024]{2,1,0:T(8,128)} async-done(((f32[16,64,1024]{2,1,0:T(8,128)}), f32[16,64,1024]{2,1,0:T(8,128)}, u32[]{:S(2)}, u32[]{:S(2)}) %all-to-all-start.8) | async-done | bytes 4194336 | tf_op jit(solution)/shard_map/all_to_all | solution.py:71
  245.1 2.5 reduce_sum.72
  247.6 1.6 add_convert_fusion
  (25 shorter events, 0.3 us)
Async XLA Ops:
  0.6 1.6 copy-start
  4.3 7.7 %copy-start.3 = (s32[384]{0:T(512)S(1)}, s32[384]{0:T(512)}, u32[]{:S(2)}) copy-start(s32[384]{0:T(512)} %param.15) | copy-start | bytes 4612
  5.5 21.4 %all-to-all-start = ((bf16[16,32,1024]{2,1,0:T(8,128)(2,1)}), bf16[16,32,1024]{2,1,0:T(8,128)(2,1)S(1)}, u32[]{:S(2)}, u32[]{:S(2)}) async-start(bf16[16,32,1024]{2,1,0:T(8,128)(2,1)} %select_select_fusion), calls=%async_computation | async-start | bytes 2097152 | tf_op jit(solution)/shard_map/all_to_all | solution.py:71
  12.0 4.9 %copy-start.2 = (f32[24,1024]{1,0:T(8,128)S(1)}, f32[24,1024]{1,0:T(8,128)}, u32[]{:S(2)}) copy-start(f32[24,1024]{1,0:T(8,128)} %param.10) | copy-start | bytes 294916
  12.0 4.9 %copy-start.5 = (s32[1024]{0:T(1024)S(1)}, s32[1024]{0:T(1024)}, u32[]{:S(2)}) copy-start(s32[1024]{0:T(1024)} %param.11) | copy-start | bytes 12292
  56.0 10.1 %copy-start.7 = (f32[384]{0:T(512)S(1)}, f32[384]{0:T(512)}, u32[]{:S(2)}) copy-start(f32[384]{0:T(512)} %param.14) | copy-start | bytes 4612
  56.0 10.1 %copy-start.1 = (f32[384,512]{1,0:T(8,128)S(1)}, f32[384,512]{1,0:T(8,128)}, u32[]{:S(2)}) copy-start(f32[384,512]{1,0:T(8,128)} %param.13) | copy-start | bytes 2359300
  58.7 29.6 %copy-start.4 = (s32[512]{0:T(512)S(1)}, s32[512]{0:T(512)}, u32[]{:S(2)}) copy-start(s32[512]{0:T(512)} %param.16) | copy-start | bytes 6148
  58.7 22.3 %all-to-all-start.2 = ((f32[4,64,416]{2,1,0:T(8,128)}), f32[4,64,416]{2,1,0:T(8,128)S(1)}, u32[]{:S(2)}, u32[]{:S(2)}) async-start(f32[4,64,416]{2,1,0:T(8,128)} %bitcast.1), calls=%async_computation.2 | async-start | bytes 1048576 | tf_op jit(solution)/shard_map/all_to_all | solution.py:71
  82.0 11.0 %all-to-all-start.3 = ((f32[16,1,2048]{2,1,0:T(1,128)}), f32[16,1,2048]{2,1,0:T(1,128)S(1)}, u32[]{:S(2)}, u32[]{:S(2)}) async-start(f32[16,1,2048]{2,1,0:T(1,128)} %reshape.92), calls=%async_computation.3 | async-start | bytes 262144 | tf_op jit(solution)/shard_map/all_to_all | solution.py:76
  116.8 13.4 %all-to-all-start.4 = ((f32[16,72,32]{1,2,0:T(8,128)}), f32[16,72,32]{1,2,0:T(8,128)S(1)}, u32[]{:S(2)}, u32[]{:S(2)}) async-start(f32[16,72,32]{1,2,0:T(8,128)} %maximum_bitcast_fusion), calls=%async_computation.4 | async-start | bytes 524288 | tf_op jit(solution)/shard_map/all_to_all | solution.py:141
  131.1 10.4 %all-to-all-start.5 = ((f32[16,1,2048]{2,1,0:T(1,128)}), f32[16,1,2048]{2,1,0:T(1,128)S(1)}, u32[]{:S(2)}, u32[]{:S(2)}) async-start(f32[16,1,2048]{2,1,0:T(1,128)} %reshape.94), calls=%async_computation.5 | async-start | bytes 262144 | tf_op jit(solution)/shard_map/all_to_all | solution.py:76
  175.7 69.4 %all-to-all-start.8 = ((f32[16,64,1024]{2,1,0:T(8,128)}), f32[16,64,1024]{2,1,0:T(8,128)}, u32[]{:S(2)}, u32[]{:S(2)}) async-start(f32[16,64,1024]{2,1,0:T(8,128)} %fusion.2), calls=%async_computation.8 | async-start | bytes 8388608 | tf_op jit(solution)/shard_map/all_to_all | solution.py:71
  184.5 63.0 %copy-start.6 = (f32[1024]{0:T(1024)S(1)}, f32[1024]{0:T(1024)}, u32[]{:S(2)}) copy-start(f32[1024]{0:T(1024)} %param.17) | copy-start | bytes 12292

commit v7 on v6

--- a/solution.py
+++ b/solution.py
@@ -154,9 +154,15 @@
     piece = jnp.concatenate([adjoint_monitored, adjoint_outage], axis=1)
     all_piece = gather_rows(gather_rows(piece, "zh"), "y")
     grad_rows = all_piece.shape[0] // line_count
-    pushed = exchange_sum(
-        jnp.dot(all_piece, rows, preferred_element_type=jnp.float32), LINE, line_count
+    staged_order = [lax.axis_size(name) for name in LINE]
+    ordered_piece = (
+        all_piece.reshape(staged_order + [grad_rows, all_piece.shape[1]])
+        .transpose(2, 1, 0, 3, 4)
+        .reshape(all_piece.shape)
     )
+    pushed = jnp.dot(ordered_piece, rows, preferred_element_type=jnp.float32)
+    for name in LINE[::-1]:
+        pushed = exchange_sum(pushed, name, lax.axis_size(name))
     own_generation = lax.dynamic_slice_in_dim(
         generation, line_index() * grad_rows, grad_rows, 0
     ).astype(jnp.float32)

time: 250 us -> 237 us (0.948); the launches traced: 249 us -> 233 us
  waiting for transfers between devices: 85.6 us -> 31.1 us
  blocking collectives: 52.5 us -> 92.8 us
  starting transfers between devices: 39.4 us -> 34.9 us
  other arithmetic: 23.2 us -> 27.5 us
  matrix products: 12.5 us -> 9.46 us
    all_to_all x3, waiting for transfers between devices: 79.7 us -> 25.2 us  [exchange_sum(): return jnp.sum(lax.all_to_all(blocks, axis, 0, 0, tiled=False), axis=0)]
    all_to_all x1 -> x3, blocking collectives: 25.9 us -> 66.3 us  [exchange_sum(): return jnp.sum(lax.all_to_all(blocks, axis, 0, 0, tiled=False), axis=0)]
    all_to_all x3, starting transfers between devices: 21.9 us -> 17.3 us  [exchange_sum(): return jnp.sum(lax.all_to_all(blocks, axis, 0, 0, tiled=False), axis=0)]
    reduce_sum x4 -> x6, other arithmetic: 4.4 us -> 8.66 us  [exchange_sum(): return jnp.sum(lax.all_to_all(blocks, axis, 0, 0, tiled=False), axis=0)]
    dot_general x1, matrix products: 4.31 us -> 1.25 us  [on_device(): pushed = jnp.dot(ordered_piece, rows, preferred_element_type=jnp.float32)]
  transfers between devices with their start and end apart: 6 -> 6, of which waited for: 5 -> 5; matrix products, arithmetic and copies ran while one was open for 9% -> 10% of each run, Pallas kernels for 0% -> 0%
where the time goes in v7:
time: 237 us; the launch traced here: 233 us
  blocking collectives  92.8 us (39%)
  starting transfers between devices  34.9 us (15%)
  waiting for transfers between devices  31.1 us (13%)
  other arithmetic  27.5 us (12%)
  Pallas kernels  19.6 us (8%)
  local copies, waits for them, and re-layouts  16.4 us (7%)
  matrix products  9.46 us (4%)
    all_to_all x3, blocking collectives, exchange_sum(): return jnp.sum(lax.all_to_all(blocks, axis, 0, 0, tiled=False), axis=0)  66.3 us
    all_to_all x2, blocking collectives, gather_rows(): gathered = lax.all_to_all(copies, axis, 0, 0, tiled=False)  26.6 us
    all_to_all x3, waiting for transfers between devices, exchange_sum(): return jnp.sum(lax.all_to_all(blocks, axis, 0, 0, tiled=False), axis=0)  25.2 us
    pallas_call x1, Pallas kernels, penalty_slopes(): pl.pallas_call(kernel, grid=(blocks,), in_specs=[pl.BlockSpec((None, moni...  19.6 us
    all_to_all x3, starting transfers between devices, exchange_sum(): return jnp.sum(lax.all_to_all(blocks, axis, 0, 0, tiled=False), axis=0)  17.3 us
    all_to_all x2, starting transfers between devices, gather_columns(): gathered = lax.all_to_all(copies, axis, 0, 0, tiled=False)  12.1 us
    reduce_sum x6, other arithmetic, exchange_sum(): return jnp.sum(lax.all_to_all(blocks, axis, 0, 0, tiled=False), axis=0)  8.66 us
    reduce_sum x1, other arithmetic, penalty_slopes(): direct = jnp.sum(direct_lanes, axis=2) / (2.0 * outage_total)  7.89 us
  transfers between devices with their start and end apart: 6, of which 5 were waited for; matrix products, arithmetic and copies ran while one was open for 10% of the time, Pallas kernels for 0%

profile of v7, /device:TPU:7, one launch (start us, length us, event | category | flops | bytes accessed | tf_op | source)
XLA Modules:
  0.0 232.8 jit_solution(11303509381876729227)
XLA Ops:
  0.6 0.0 copy-start
  0.7 0.8 compare_and_fusion
  1.5 0.1 broadcast_in_dim.92
  1.6 0.1 broadcast_in_dim.94
  1.7 0.6 copy-done
  2.2 2.0 gather_fusion.1
  4.3 1.2 select_select_fusion
  5.5 6.4 %all-to-all-start = ((bf16[16,32,1024]{2,1,0:T(8,128)(2,1)}), bf16[16,32,1024]{2,1,0:T(8,128)(2,1)S(1)}, u32[]{:S(2)}, u32[]{:S(2)}) async-start(bf16[16,32,1024]{2,1,0:T(8,128)(2,1)} %select_select_fusion), calls=%async_computation | async-start | bytes 2097152 | tf_op jit(solution)/shard_map/all_to_all | solution.py:71
  12.0 2.7 %gather_fusion = bf16[384,1024]{1,0:T(8,128)(2,1)} fusion(bf16[1024,1024]{1,0:T(8,128)(2,1)S(1)} %copy-done, s32[1024]{0:T(1024)S(1)} %pad_clamp_fusion.1), kind=kCustom, calls=%fused_computation | custom fusion | bytes 1574400 | tf_op jit(solution)/shard_map/jit(_take)/gather | solution.py:120
  14.7 2.2 broadcast_select_fusion
  16.9 4.9 %subtract_convert_fusion = bf16[1024,1024]{1,0:T(8,128)(2,1)} fusion(bf16[1024,1024]{1,0:T(8,128)(2,1)} %param.9, f32[24,1024]{1,0:T(8,128)S(1)} %copy-done.3, s32[1024]{0:T(1024)S(1)} %copy-done.6), kind=kOutput, calls=%fused_computation.2 | convolution fusion | flops 305160192 | bytes 4296704 | tf_op jit(solution)/shard_map/dot_general | solution.py:102
  21.7 5.2 %all-to-all-done = bf16[16,32,1024]{2,1,0:T(8,128)(2,1)S(1)} async-done(((bf16[16,32,1024]{2,1,0:T(8,128)(2,1)}), bf16[16,32,1024]{2,1,0:T(8,128)(2,1)S(1)}, u32[]{:S(2)}, u32[]{:S(2)}) %all-to-all-start) | async-done | bytes 1048608 | tf_op jit(solution)/shard_map/all_to_all | solution.py:71
  26.9 0.2 reduce_sum.84
  27.1 2.8 %fusion.5 = f32[1024,416]{0,1:T(8,128)S(1)} fusion(bf16[1024,1024]{1,0:T(8,128)(2,1)} %subtract_convert_fusion, bf16[32,1024]{1,0:T(8,128)(2,1)S(1)} %reduce_sum.84, bf16[384,1024]{1,0:T(8,128)(2,1)} %broadcast_select_fusion), kind=kOutput, calls=%fused_computation.14 | convolution fusion | flops 874119168 | bytes 4653056 | tf_op jit(solution)/shard_map/dot_general | solution.py:123
  29.9 0.2 copy.88
  30.1 25.9 %all_to_all.55 = f32[4,256,416]{1,2,0:T(8,128)} all-to-all(f32[4,256,416]{1,2,0:T(8,128)S(1)} %bitcast.44), channel_id=1, replica_groups=mesh['y'=4,'zh'=4,'zl'=2,'x'=4,'core'=2] {'y'}, dimensions={0} | all-to-all | bytes 3407872 | tf_op jit(solution)/shard_map/all_to_all | solution.py:71
  56.0 1.7 reduce_sum.85
  57.7 1.0 copy.68
  58.7 7.4 %all-to-all-start.2 = ((f32[4,64,416]{2,1,0:T(8,128)}), f32[4,64,416]{2,1,0:T(8,128)S(1)}, u32[]{:S(2)}, u32[]{:S(2)}) async-start(f32[4,64,416]{2,1,0:T(8,128)} %bitcast.1), calls=%async_computation.2 | async-start | bytes 1048576 | tf_op jit(solution)/shard_map/all_to_all | solution.py:71
  66.1 0.9 broadcast_multiply_fusion.lodf_ref
  67.1 13.9 %all-to-all-done.2 = f32[4,64,416]{2,1,0:T(8,128)S(1)} async-done(((f32[4,64,416]{2,1,0:T(8,128)}), f32[4,64,416]{2,1,0:T(8,128)S(1)}, u32[]{:S(2)}, u32[]{:S(2)}) %all-to-all-start.2) | async-done | bytes 426016 | tf_op jit(solution)/shard_map/all_to_all | solution.py:71
  81.1 0.1 copy.70
  81.2 0.8 reshape.100
  82.0 6.3 %all-to-all-start.3 = ((f32[16,1,2048]{2,1,0:T(1,128)}), f32[16,1,2048]{2,1,0:T(1,128)S(1)}, u32[]{:S(2)}, u32[]{:S(2)}) async-start(f32[16,1,2048]{2,1,0:T(1,128)} %reshape.100), calls=%async_computation.3 | async-start | bytes 262144 | tf_op jit(solution)/shard_map/all_to_all | solution.py:76
  88.3 0.2 fusion.4
  88.6 0.8 reshape.98.lim_ref
  89.3 0.2 concatenate.19
  89.6 0.1 pad.4.clone
  89.7 1.7 copy.69
  91.3 1.6 all-to-all-done.3
  93.0 0.5 broadcast.43
  93.5 0.9 reduce.3
  94.4 0.1 reshape.101
  94.5 0.8 copy.71.out_ref
  95.3 19.6 %shard_map.112 = (f32[64,384,128]{2,1,0:T(8,128)}, f32[64,512]{1,0:T(8,128)}) custom-call(f32[8,384,8]{2,1,0:T(8,128)} %bitcast.45, f32[64,512]{1,0:T(8,128)} %copy.71.out_ref, f32[384,512]{1,0:T(8,128)} %broadcast_multiply_fusion.lodf_ref, f32[384,1]{1,0:T(8,128)} %reshape.98.lim_ref), custom_call_target="tpu_custom_call" | custom-call | tf_op jit(solution)/shard_map/pallas_call | solution.py:47
  114.9 0.9 broadcast_multiply_fusion.3
  115.8 0.1 copy.73
  116.0 0.9 maximum_bitcast_fusion
  116.8 5.5 %all-to-all-start.4 = ((f32[16,72,32]{1,2,0:T(8,128)}), f32[16,72,32]{1,2,0:T(8,128)S(1)}, u32[]{:S(2)}, u32[]{:S(2)}) async-start(f32[16,72,32]{1,2,0:T(8,128)} %maximum_bitcast_fusion), calls=%async_computation.4 | async-start | bytes 524288 | tf_op jit(solution)/shard_map/all_to_all | solution.py:141
  122.3 7.9 %reduce_sum.87 = f32[64,384]{1,0:T(8,128)S(1)} reduce(f32[64,384,128]{2,1,0:T(8,128)} %get-tuple-element.5, f32[]{:T(128)} %constant.39.clone.1), dimensions={2}, to_apply=%region_3.4 | reduce | flops 3121152 | bytes 12681220 | tf_op jit(solution)/shard_map/reduce_sum | solution.py:65
  130.3 0.8 reshape.102
  131.1 5.8 %all-to-all-start.5 = ((f32[16,1,2048]{2,1,0:T(1,128)}), f32[16,1,2048]{2,1,0:T(1,128)S(1)}, u32[]{:S(2)}, u32[]{:S(2)}) async-start(f32[16,1,2048]{2,1,0:T(1,128)} %reshape.102), calls=%async_computation.5 | async-start | bytes 262144 | tf_op jit(solution)/shard_map/all_to_all | solution.py:76
  136.8 0.2 fusion.10
  137.0 0.1 copy.85
  137.1 4.4 %all-to-all-done.5 = f32[16,1,2048]{2,1,0:T(1,128)S(1)} async-done(((f32[16,1,2048]{2,1,0:T(1,128)}), f32[16,1,2048]{2,1,0:T(1,128)S(1)}, u32[]{:S(2)}, u32[]{:S(2)}) %all-to-all-start.5) | async-done | bytes 131104 | tf_op jit(solution)/shard_map/all_to_all | solution.py:76
  141.5 0.9 reduce.4
  142.4 0.1 reshape.103
  142.6 0.5 fusion
  143.1 12.4 %all_to_all.56 = bf16[4,64,416]{2,1,0:T(8,128)(2,1)S(1)} all-to-all(bf16[4,64,416]{2,1,0:T(8,128)(2,1)S(1)} %broadcast_in_dim.105), channel_id=1, replica_groups=mesh['y'=4,'zh'=4,'zl'=2,'x'=4,'core'=2] {'zh'}, dimensions={0} | all-to-all | bytes 425984 | tf_op jit(solution)/shard_map/all_to_all | solution.py:83
  155.6 0.1 copy.77
  155.7 0.1 broadcast_in_dim.107
  155.8 14.1 %all_to_all.57 = bf16[4,256,416]{1,2,0:T(8,128)(2,1)} all-to-all(bf16[4,256,416]{1,2,0:T(8,128)(2,1)S(1)} %broadcast_in_dim.107), channel_id=1, replica_groups=mesh['y'=4,'zh'=4,'zl'=2,'x'=4,'core'=2] {'y'}, dimensions={0} | all-to-all | bytes 1703936 | tf_op jit(solution)/shard_map/all_to_all | solution.py:83
  169.9 1.4 copy.78
  171.4 0.1 copy.79
  171.5 1.0 copy-done.1
  172.5 1.2 fusion.2
  173.8 10.7 %all_to_all.58 = f32[2,512,1024]{2,1,0:T(8,128)} all-to-all(f32[2,512,1024]{2,1,0:T(8,128)S(1)} %fusion.2), channel_id=1, replica_groups=mesh['y'=4,'zh'=4,'zl'=2,'x'=4,'core'=2] {'core'}, dimensions={0} | all-to-all | bytes 8388608 | tf_op jit(solution)/shard_map/all_to_all | solution.py:71
  184.5 4.1 %reduce_sum.90 = f32[512,1024]{1,0:T(8,128)} reduce(f32[2,512,1024]{2,1,0:T(8,128)} %all_to_all.58, f32[]{:T(128)} %constant.39.clone.1), dimensions={0}, to_apply=%region_6.7 | reduce | flops 524288 | bytes 6291460 | tf_op jit(solution)/shard_map/reduce_sum | solution.py:71
  188.6 29.6 %all_to_all.59 = f32[4,128,1024]{2,1,0:T(8,128)} all-to-all(f32[4,128,1024]{2,1,0:T(8,128)} %bitcast.43), channel_id=1, replica_groups=mesh['y'=4,'zh'=4,'zl'=2,'x'=4,'core'=2] {'x'}, dimensions={0} | all-to-all | bytes 4194304 | tf_op jit(solution)/shard_map/all_to_all | solution.py:71
  218.3 2.6 %reduce_sum.91 = f32[128,1024]{1,0:T(8,128)} reduce(f32[4,128,1024]{2,1,0:T(8,128)} %all_to_all.59, f32[]{:T(128)} %constant.39.clone.1), dimensions={0}, to_apply=%region_7.8 | reduce | flops 393216 | bytes 2621444 | tf_op jit(solution)/shard_map/reduce_sum | solution.py:71
  220.9 3.5 %all-to-all-start.10 = ((f32[2,64,1024]{2,1,0:T(8,128)}), f32[2,64,1024]{2,1,0:T(8,128)S(1)}, u32[]{:S(2)}, u32[]{:S(2)}) async-start(f32[2,64,1024]{2,1,0:T(8,128)} %bitcast.16), calls=%async_computation.10 | async-start | bytes 1048576 | tf_op jit(solution)/shard_map/all_to_all | solution.py:71
  224.4 0.8 copy.82
  225.1 6.1 %all-to-all-done.10 = f32[2,64,1024]{2,1,0:T(8,128)S(1)} async-done(((f32[2,64,1024]{2,1,0:T(8,128)}), f32[2,64,1024]{2,1,0:T(8,128)S(1)}, u32[]{:S(2)}, u32[]{:S(2)}) %all-to-all-start.10) | async-done | bytes 524320 | tf_op jit(solution)/shard_map/all_to_all | solution.py:71
  231.2 1.6 add_convert_fusion
  (32 shorter events, 0.3 us)
Async XLA Ops:
  0.6 1.6 copy-start
  4.3 7.7 %copy-start.4 = (s32[384]{0:T(512)S(1)}, s32[384]{0:T(512)}, u32[]{:S(2)}) copy-start(s32[384]{0:T(512)} %param.15) | copy-start | bytes 4612
  5.5 21.4 %all-to-all-start = ((bf16[16,32,1024]{2,1,0:T(8,128)(2,1)}), bf16[16,32,1024]{2,1,0:T(8,128)(2,1)S(1)}, u32[]{:S(2)}, u32[]{:S(2)}) async-start(bf16[16,32,1024]{2,1,0:T(8,128)(2,1)} %select_select_fusion), calls=%async_computation | async-start | bytes 2097152 | tf_op jit(solution)/shard_map/all_to_all | solution.py:71
  12.0 4.9 %copy-start.3 = (f32[24,1024]{1,0:T(8,128)S(1)}, f32[24,1024]{1,0:T(8,128)}, u32[]{:S(2)}) copy-start(f32[24,1024]{1,0:T(8,128)} %param.10) | copy-start | bytes 294916
  12.0 4.9 %copy-start.6 = (s32[1024]{0:T(1024)S(1)}, s32[1024]{0:T(1024)}, u32[]{:S(2)}) copy-start(s32[1024]{0:T(1024)} %param.11) | copy-start | bytes 12292
  56.0 10.1 %copy-start.8 = (f32[384]{0:T(512)S(1)}, f32[384]{0:T(512)}, u32[]{:S(2)}) copy-start(f32[384]{0:T(512)} %param.14) | copy-start | bytes 4612
  56.0 10.1 %copy-start.2 = (f32[384,512]{1,0:T(8,128)S(1)}, f32[384,512]{1,0:T(8,128)}, u32[]{:S(2)}) copy-start(f32[384,512]{1,0:T(8,128)} %param.13) | copy-start | bytes 2359300
  58.7 29.6 %copy-start.5 = (s32[512]{0:T(512)S(1)}, s32[512]{0:T(512)}, u32[]{:S(2)}) copy-start(s32[512]{0:T(512)} %param.16) | copy-start | bytes 6148
  58.7 22.3 %all-to-all-start.2 = ((f32[4,64,416]{2,1,0:T(8,128)}), f32[4,64,416]{2,1,0:T(8,128)S(1)}, u32[]{:S(2)}, u32[]{:S(2)}) async-start(f32[4,64,416]{2,1,0:T(8,128)} %bitcast.1), calls=%async_computation.2 | async-start | bytes 1048576 | tf_op jit(solution)/shard_map/all_to_all | solution.py:71
  82.0 11.0 %all-to-all-start.3 = ((f32[16,1,2048]{2,1,0:T(1,128)}), f32[16,1,2048]{2,1,0:T(1,128)S(1)}, u32[]{:S(2)}, u32[]{:S(2)}) async-start(f32[16,1,2048]{2,1,0:T(1,128)} %reshape.100), calls=%async_computation.3 | async-start | bytes 262144 | tf_op jit(solution)/shard_map/all_to_all | solution.py:76
  116.8 13.4 %all-to-all-start.4 = ((f32[16,72,32]{1,2,0:T(8,128)}), f32[16,72,32]{1,2,0:T(8,128)S(1)}, u32[]{:S(2)}, u32[]{:S(2)}) async-start(f32[16,72,32]{1,2,0:T(8,128)} %maximum_bitcast_fusion), calls=%async_computation.4 | async-start | bytes 524288 | tf_op jit(solution)/shard_map/all_to_all | solution.py:141
  131.1 10.4 %all-to-all-start.5 = ((f32[16,1,2048]{2,1,0:T(1,128)}), f32[16,1,2048]{2,1,0:T(1,128)S(1)}, u32[]{:S(2)}, u32[]{:S(2)}) async-start(f32[16,1,2048]{2,1,0:T(1,128)} %reshape.102), calls=%async_computation.5 | async-start | bytes 262144 | tf_op jit(solution)/shard_map/all_to_all | solution.py:76
  171.4 1.1 copy-start.1
  218.3 13.0 %copy-start.7 = (f32[1024]{0:T(1024)S(1)}, f32[1024]{0:T(1024)}, u32[]{:S(2)}) copy-start(f32[1024]{0:T(1024)} %param.17) | copy-start | bytes 12292
  220.9 10.3 %all-to-all-start.10 = ((f32[2,64,1024]{2,1,0:T(8,128)}), f32[2,64,1024]{2,1,0:T(8,128)S(1)}, u32[]{:S(2)}, u32[]{:S(2)}) async-start(f32[2,64,1024]{2,1,0:T(8,128)} %bitcast.16), calls=%async_computation.10 | async-start | bytes 1048576 | tf_op jit(solution)/shard_map/all_to_all | solution.py:71

commit v8 on v7

--- a/solution.py
+++ b/solution.py
@@ -4,6 +4,7 @@
 import jax.numpy as jnp
 from jax import lax
 from jax.experimental import pallas as pl
+from jax.experimental.pallas import tpu as pltpu
 from jax.sharding import Mesh, PartitionSpec as P
 
 sharpness = 4.0
@@ -23,7 +24,7 @@
     lodf2 = half * lodf
     lim2 = (half * limits).reshape(monitor_count, 1)
 
-    def kernel(base_ref, out_ref, lodf_ref, lim_ref, direct_ref, sens_ref):
+    def kernel(base_ref, out_ref, lodf_ref, lim_ref, direct_ref, sens_ref, fold_ref):
         for i in range(sb):
             flow_row = out_ref[i:i + 1, :]
 
@@ -36,15 +37,16 @@
                 folded = slope[:, 0:lanes]
                 for q in range(1, outage_total // lanes):
                     folded = folded + slope[:, q * lanes:(q + 1) * lanes]
-                direct_ref[i, pl.ds(r, ch), :] = folded
+                fold_ref[pl.ds(r, ch), :] = folded
                 return acc + weight * slope
 
             acc = lax.fori_loop(0, monitor_count // ch, body,
                                 jnp.zeros((ch, outage_total), jnp.float32),
                                 unroll=monitor_count // ch)
             sens_ref[i:i + 1, :] = jnp.sum(acc, axis=0, keepdims=True)
+            direct_ref[:, i:i + 1] = jnp.sum(fold_ref[...], axis=1, keepdims=True)
 
-    direct_lanes, sens = pl.pallas_call(
+    direct3, sens = pl.pallas_call(
         kernel,
         grid=(blocks,),
         in_specs=[
@@ -54,15 +56,16 @@
             pl.BlockSpec((monitor_count, 1), lambda g: (0, 0)),
         ],
         out_specs=[
-            pl.BlockSpec((sb, monitor_count, lanes), lambda g: (g, 0, 0)),
+            pl.BlockSpec((None, monitor_count, sb), lambda g: (g, 0, 0)),
             pl.BlockSpec((sb, outage_total), lambda g: (g, 0)),
         ],
         out_shape=[
-            jax.ShapeDtypeStruct((scen_rows, monitor_count, lanes), jnp.float32),
+            jax.ShapeDtypeStruct((blocks, monitor_count, sb), jnp.float32),
             jax.ShapeDtypeStruct((scen_rows, outage_total), jnp.float32),
         ],
+        scratch_shapes=[pltpu.VMEM((monitor_count, lanes), jnp.float32)],
     )(base3, outflow, lodf2, lim2)
-    direct = jnp.sum(direct_lanes, axis=2) / (2.0 * outage_total)
+    direct = direct3.transpose(0, 2, 1).reshape(scen_rows, monitor_count) / (2.0 * outage_total)
     return direct, sens / (2.0 * half)
 
 

time: 237 us -> 240 us (1.013)
  Pallas kernels: 19.6 us -> 25 us
  other arithmetic: 27.5 us -> 22.3 us
    reduce_sum x1 -> x0, other arithmetic: 7.89 us -> none  [penalty_slopes(): direct = jnp.sum(direct_lanes, axis=2) / (2.0 * outage_total)]
    pallas_call x1, Pallas kernels: 19.6 us -> 25 us  [penalty_slopes(): pl.pallas_call(kernel, grid=(blocks,), in_specs=[pl.BlockSpec((None, moni...]
    div x0 -> x1, other arithmetic: none -> 2.67 us  [penalty_slopes(): direct3.transpose(0, 2, 1).reshape(scen_rows, monitor_count)]
  transfers between devices with their start and end apart: 6 -> 6, of which waited for: 5 -> 6; matrix products, arithmetic and copies ran while one was open for 10% -> 8% of each run, Pallas kernels for 0% -> 0%
where the time goes in v8:
time: 240 us; the launch traced here: 236 us
  blocking collectives  92.9 us (39%)
  starting transfers between devices  34.6 us (14%)
  waiting for transfers between devices  32.8 us (14%)
  Pallas kernels  25 us (10%)
  other arithmetic  22.3 us (9%)
  local copies, waits for them, and re-layouts  18.2 us (8%)
  matrix products  9.46 us (4%)
    all_to_all x3, blocking collectives, exchange_sum(): return jnp.sum(lax.all_to_all(blocks, axis, 0, 0, tiled=False), axis=0)  66.3 us
    all_to_all x2, blocking collectives, gather_rows(): gathered = lax.all_to_all(copies, axis, 0, 0, tiled=False)  26.5 us
    all_to_all x3, waiting for transfers between devices, exchange_sum(): return jnp.sum(lax.all_to_all(blocks, axis, 0, 0, tiled=False), axis=0)  25.2 us
    pallas_call x1, Pallas kernels, penalty_slopes(): pl.pallas_call(kernel, grid=(blocks,), in_specs=[pl.BlockSpec((None, moni...  25 us
    all_to_all x3, starting transfers between devices, exchange_sum(): return jnp.sum(lax.all_to_all(blocks, axis, 0, 0, tiled=False), axis=0)  17.3 us
    all_to_all x2, starting transfers between devices, gather_columns(): gathered = lax.all_to_all(copies, axis, 0, 0, tiled=False)  11.8 us
    reduce_sum x6, other arithmetic, exchange_sum(): return jnp.sum(lax.all_to_all(blocks, axis, 0, 0, tiled=False), axis=0)  8.66 us
    all_to_all x2, waiting for transfers between devices, gather_columns(): gathered = lax.all_to_all(copies, axis, 0, 0, tiled=False)  6.06 us
  transfers between devices with their start and end apart: 6, of which 6 were waited for; matrix products, arithmetic and copies ran while one was open for 8% of the time, Pallas kernels for 0%

profile of v8, /device:TPU:7, one launch (start us, length us, event | category | flops | bytes accessed | tf_op | source)
XLA Modules:
  0.0 236.1 jit_solution(883465083003116615)
XLA Ops:
  0.7 0.8 compare_and_fusion
  1.5 0.1 broadcast_in_dim.94
  1.6 0.1 broadcast_in_dim.92
  1.7 0.6 copy-done
  2.2 2.0 gather_fusion.1
  4.3 1.2 select_select_fusion
  5.5 6.4 %all-to-all-start = ((bf16[16,32,1024]{2,1,0:T(8,128)(2,1)}), bf16[16,32,1024]{2,1,0:T(8,128)(2,1)S(1)}, u32[]{:S(2)}, u32[]{:S(2)}) async-start(bf16[16,32,1024]{2,1,0:T(8,128)(2,1)} %select_select_fusion), calls=%async_computation | async-start | bytes 2097152 | tf_op jit(solution)/shard_map/all_to_all | solution.py:74
  12.0 2.7 %gather_fusion = bf16[384,1024]{1,0:T(8,128)(2,1)} fusion(bf16[1024,1024]{1,0:T(8,128)(2,1)S(1)} %copy-done, s32[1024]{0:T(1024)S(1)} %pad_clamp_fusion.1), kind=kCustom, calls=%fused_computation | custom fusion | bytes 1574400 | tf_op jit(solution)/shard_map/jit(_take)/gather | solution.py:123
  14.7 2.2 broadcast_select_fusion
  16.9 4.9 %subtract_convert_fusion = bf16[1024,1024]{1,0:T(8,128)(2,1)} fusion(bf16[1024,1024]{1,0:T(8,128)(2,1)} %param.9, f32[24,1024]{1,0:T(8,128)S(1)} %copy-done.3, s32[1024]{0:T(1024)S(1)} %copy-done.6), kind=kOutput, calls=%fused_computation.2 | convolution fusion | flops 305160192 | bytes 4296704 | tf_op jit(solution)/shard_map/dot_general | solution.py:105
  21.7 5.2 %all-to-all-done = bf16[16,32,1024]{2,1,0:T(8,128)(2,1)S(1)} async-done(((bf16[16,32,1024]{2,1,0:T(8,128)(2,1)}), bf16[16,32,1024]{2,1,0:T(8,128)(2,1)S(1)}, u32[]{:S(2)}, u32[]{:S(2)}) %all-to-all-start) | async-done | bytes 1048608 | tf_op jit(solution)/shard_map/all_to_all | solution.py:74
  26.9 0.2 reduce_sum.75
  27.1 2.8 %fusion.5 = f32[1024,416]{0,1:T(8,128)S(1)} fusion(bf16[1024,1024]{1,0:T(8,128)(2,1)} %subtract_convert_fusion, bf16[32,1024]{1,0:T(8,128)(2,1)S(1)} %reduce_sum.75, bf16[384,1024]{1,0:T(8,128)(2,1)} %broadcast_select_fusion), kind=kOutput, calls=%fused_computation.15 | convolution fusion | flops 874119168 | bytes 4653056 | tf_op jit(solution)/shard_map/dot_general | solution.py:126
  29.9 0.2 copy.93
  30.1 25.9 %all_to_all.55 = f32[4,256,416]{1,2,0:T(8,128)} all-to-all(f32[4,256,416]{1,2,0:T(8,128)S(1)} %bitcast.48), channel_id=1, replica_groups=mesh['y'=4,'zh'=4,'zl'=2,'x'=4,'core'=2] {'y'}, dimensions={0} | all-to-all | bytes 3407872 | tf_op jit(solution)/shard_map/all_to_all | solution.py:74
  56.0 1.7 reduce_sum.76
  57.7 1.0 copy.72
  58.7 7.4 %all-to-all-start.2 = ((f32[4,64,416]{2,1,0:T(8,128)}), f32[4,64,416]{2,1,0:T(8,128)S(1)}, u32[]{:S(2)}, u32[]{:S(2)}) async-start(f32[4,64,416]{2,1,0:T(8,128)} %bitcast.1), calls=%async_computation.2 | async-start | bytes 1048576 | tf_op jit(solution)/shard_map/all_to_all | solution.py:74
  66.1 0.9 broadcast_multiply_fusion.lodf_ref
  67.1 13.9 %all-to-all-done.2 = f32[4,64,416]{2,1,0:T(8,128)S(1)} async-done(((f32[4,64,416]{2,1,0:T(8,128)}), f32[4,64,416]{2,1,0:T(8,128)S(1)}, u32[]{:S(2)}, u32[]{:S(2)}) %all-to-all-start.2) | async-done | bytes 426016 | tf_op jit(solution)/shard_map/all_to_all | solution.py:74
  81.1 0.1 copy.74
  81.2 0.8 reshape.103
  82.0 6.3 %all-to-all-start.3 = ((f32[16,1,2048]{2,1,0:T(1,128)}), f32[16,1,2048]{2,1,0:T(1,128)S(1)}, u32[]{:S(2)}, u32[]{:S(2)}) async-start(f32[16,1,2048]{2,1,0:T(1,128)} %reshape.103), calls=%async_computation.3 | async-start | bytes 262144 | tf_op jit(solution)/shard_map/all_to_all | solution.py:79
  88.3 0.2 fusion.4
  88.6 0.8 reshape.101.lim_ref
  89.4 0.2 concatenate.19
  89.6 0.1 pad.4.clone
  89.7 1.6 copy.73
  91.3 1.7 all-to-all-done.3
  93.0 0.5 broadcast.47
  93.5 0.9 reduce.3
  94.4 0.1 reshape.104
  94.5 0.8 copy.75.out_ref
  95.3 25.0 %shard_map.112 = (f32[8,384,8]{2,1,0:T(8,128)}, f32[64,512]{1,0:T(8,128)}) custom-call(f32[8,384,8]{2,1,0:T(8,128)} %bitcast.49, f32[64,512]{1,0:T(8,128)} %copy.75.out_ref, f32[384,512]{1,0:T(8,128)} %broadcast_multiply_fusion.lodf_ref, f32[384,1]{1,0:T(8,128)} %reshape.101.lim_ref), custom_call_target="tpu_custom_call" | custom-call | tf_op jit(solution)/shard_map/pallas_call | solution.py:49
  120.3 0.9 broadcast_multiply_fusion.3
  121.2 0.1 copy.78
  121.3 0.9 maximum_bitcast_fusion
  122.2 5.5 %all-to-all-start.4 = ((f32[16,72,32]{1,2,0:T(8,128)}), f32[16,72,32]{1,2,0:T(8,128)S(1)}, u32[]{:S(2)}, u32[]{:S(2)}) async-start(f32[16,72,32]{1,2,0:T(8,128)} %maximum_bitcast_fusion), calls=%async_computation.4 | async-start | bytes 524288 | tf_op jit(solution)/shard_map/all_to_all | solution.py:144
  127.7 2.7 %multiply_bitcast_fusion = f32[8,8,384]{1,2,0:T(8,128)} fusion(f32[8,384,8]{2,1,0:T(8,128)} %get-tuple-element.5), kind=kLoop, calls=%fused_computation.4 | loop fusion | flops 24576 | bytes 196608 | tf_op jit(solution)/shard_map/div | solution.py:68
  130.3 1.8 copy.77
  132.2 1.6 all-to-all-done.4
  133.8 0.8 reshape.105
  134.6 5.4 %all-to-all-start.5 = ((f32[16,1,2048]{2,1,0:T(1,128)}), f32[16,1,2048]{2,1,0:T(1,128)S(1)}, u32[]{:S(2)}, u32[]{:S(2)}) async-start(f32[16,1,2048]{2,1,0:T(1,128)} %reshape.105), calls=%async_computation.5 | async-start | bytes 262144 | tf_op jit(solution)/shard_map/all_to_all | solution.py:79
  140.1 0.2 fusion.10
  140.2 0.1 copy.90
  140.3 4.4 %all-to-all-done.5 = f32[16,1,2048]{2,1,0:T(1,128)S(1)} async-done(((f32[16,1,2048]{2,1,0:T(1,128)}), f32[16,1,2048]{2,1,0:T(1,128)S(1)}, u32[]{:S(2)}, u32[]{:S(2)}) %all-to-all-start.5) | async-done | bytes 131104 | tf_op jit(solution)/shard_map/all_to_all | solution.py:79
  144.7 0.9 reduce.4
  145.7 0.1 reshape.106
  145.8 0.5 fusion
  146.4 12.4 %all_to_all.56 = bf16[4,64,416]{2,1,0:T(8,128)(2,1)S(1)} all-to-all(bf16[4,64,416]{2,1,0:T(8,128)(2,1)S(1)} %broadcast_in_dim.105), channel_id=1, replica_groups=mesh['y'=4,'zh'=4,'zl'=2,'x'=4,'core'=2] {'zh'}, dimensions={0} | all-to-all | bytes 425984 | tf_op jit(solution)/shard_map/all_to_all | solution.py:86
  158.8 0.1 copy.82
  159.0 14.1 %all_to_all.57 = bf16[4,256,416]{1,2,0:T(8,128)(2,1)} all-to-all(bf16[4,256,416]{1,2,0:T(8,128)(2,1)S(1)} %broadcast_in_dim.107), channel_id=1, replica_groups=mesh['y'=4,'zh'=4,'zl'=2,'x'=4,'core'=2] {'y'}, dimensions={0} | all-to-all | bytes 1703936 | tf_op jit(solution)/shard_map/all_to_all | solution.py:86
  173.1 1.4 copy.83
  174.6 0.1 copy.84
  174.7 1.0 copy-done.1
  175.7 1.2 fusion.2
  177.0 10.7 %all_to_all.58 = f32[2,512,1024]{2,1,0:T(8,128)} all-to-all(f32[2,512,1024]{2,1,0:T(8,128)S(1)} %fusion.2), channel_id=1, replica_groups=mesh['y'=4,'zh'=4,'zl'=2,'x'=4,'core'=2] {'core'}, dimensions={0} | all-to-all | bytes 8388608 | tf_op jit(solution)/shard_map/all_to_all | solution.py:74
  187.7 4.1 %reduce_sum.80 = f32[512,1024]{1,0:T(8,128)} reduce(f32[2,512,1024]{2,1,0:T(8,128)} %all_to_all.58, f32[]{:T(128)} %constant.39.clone.1), dimensions={0}, to_apply=%region_5.6 | reduce | flops 524288 | bytes 6291460 | tf_op jit(solution)/shard_map/reduce_sum | solution.py:74
  191.8 29.7 %all_to_all.59 = f32[4,128,1024]{2,1,0:T(8,128)} all-to-all(f32[4,128,1024]{2,1,0:T(8,128)} %bitcast.47), channel_id=1, replica_groups=mesh['y'=4,'zh'=4,'zl'=2,'x'=4,'core'=2] {'x'}, dimensions={0} | all-to-all | bytes 4194304 | tf_op jit(solution)/shard_map/all_to_all | solution.py:74
  221.5 2.6 %reduce_sum.81 = f32[128,1024]{1,0:T(8,128)} reduce(f32[4,128,1024]{2,1,0:T(8,128)} %all_to_all.59, f32[]{:T(128)} %constant.39.clone.1), dimensions={0}, to_apply=%region_6.7 | reduce | flops 393216 | bytes 2621444 | tf_op jit(solution)/shard_map/reduce_sum | solution.py:74
  224.1 3.5 %all-to-all-start.10 = ((f32[2,64,1024]{2,1,0:T(8,128)}), f32[2,64,1024]{2,1,0:T(8,128)S(1)}, u32[]{:S(2)}, u32[]{:S(2)}) async-start(f32[2,64,1024]{2,1,0:T(8,128)} %bitcast.18), calls=%async_computation.10 | async-start | bytes 1048576 | tf_op jit(solution)/shard_map/all_to_all | solution.py:74
  227.6 0.8 copy.87
  228.4 6.1 %all-to-all-done.10 = f32[2,64,1024]{2,1,0:T(8,128)S(1)} async-done(((f32[2,64,1024]{2,1,0:T(8,128)}), f32[2,64,1024]{2,1,0:T(8,128)S(1)}, u32[]{:S(2)}, u32[]{:S(2)}) %all-to-all-start.10) | async-done | bytes 524320 | tf_op jit(solution)/shard_map/all_to_all | solution.py:74
  234.5 1.6 add_convert_fusion
  (33 shorter events, 0.4 us)
Async XLA Ops:
  0.6 1.6 copy-start
  4.3 7.7 %copy-start.4 = (s32[384]{0:T(512)S(1)}, s32[384]{0:T(512)}, u32[]{:S(2)}) copy-start(s32[384]{0:T(512)} %param.15) | copy-start | bytes 4612
  5.5 21.4 %all-to-all-start = ((bf16[16,32,1024]{2,1,0:T(8,128)(2,1)}), bf16[16,32,1024]{2,1,0:T(8,128)(2,1)S(1)}, u32[]{:S(2)}, u32[]{:S(2)}) async-start(bf16[16,32,1024]{2,1,0:T(8,128)(2,1)} %select_select_fusion), calls=%async_computation | async-start | bytes 2097152 | tf_op jit(solution)/shard_map/all_to_all | solution.py:74
  12.0 4.9 %copy-start.3 = (f32[24,1024]{1,0:T(8,128)S(1)}, f32[24,1024]{1,0:T(8,128)}, u32[]{:S(2)}) copy-start(f32[24,1024]{1,0:T(8,128)} %param.10) | copy-start | bytes 294916
  12.0 4.9 %copy-start.6 = (s32[1024]{0:T(1024)S(1)}, s32[1024]{0:T(1024)}, u32[]{:S(2)}) copy-start(s32[1024]{0:T(1024)} %param.11) | copy-start | bytes 12292
  56.0 10.1 %copy-start.8 = (f32[384]{0:T(512)S(1)}, f32[384]{0:T(512)}, u32[]{:S(2)}) copy-start(f32[384]{0:T(512)} %param.14) | copy-start | bytes 4612
  56.0 10.1 %copy-start.2 = (f32[384,512]{1,0:T(8,128)S(1)}, f32[384,512]{1,0:T(8,128)}, u32[]{:S(2)}) copy-start(f32[384,512]{1,0:T(8,128)} %param.13) | copy-start | bytes 2359300
  58.7 29.6 %copy-start.5 = (s32[512]{0:T(512)S(1)}, s32[512]{0:T(512)}, u32[]{:S(2)}) copy-start(s32[512]{0:T(512)} %param.16) | copy-start | bytes 6148
  58.7 22.3 %all-to-all-start.2 = ((f32[4,64,416]{2,1,0:T(8,128)}), f32[4,64,416]{2,1,0:T(8,128)S(1)}, u32[]{:S(2)}, u32[]{:S(2)}) async-start(f32[4,64,416]{2,1,0:T(8,128)} %bitcast.1), calls=%async_computation.2 | async-start | bytes 1048576 | tf_op jit(solution)/shard_map/all_to_all | solution.py:74
  82.0 11.0 %all-to-all-start.3 = ((f32[16,1,2048]{2,1,0:T(1,128)}), f32[16,1,2048]{2,1,0:T(1,128)S(1)}, u32[]{:S(2)}, u32[]{:S(2)}) async-start(f32[16,1,2048]{2,1,0:T(1,128)} %reshape.103), calls=%async_computation.3 | async-start | bytes 262144 | tf_op jit(solution)/shard_map/all_to_all | solution.py:79
  122.2 11.6 %all-to-all-start.4 = ((f32[16,72,32]{1,2,0:T(8,128)}), f32[16,72,32]{1,2,0:T(8,128)S(1)}, u32[]{:S(2)}, u32[]{:S(2)}) async-start(f32[16,72,32]{1,2,0:T(8,128)} %maximum_bitcast_fusion), calls=%async_computation.4 | async-start | bytes 524288 | tf_op jit(solution)/shard_map/all_to_all | solution.py:144
  134.6 10.1 %all-to-all-start.5 = ((f32[16,1,2048]{2,1,0:T(1,128)}), f32[16,1,2048]{2,1,0:T(1,128)S(1)}, u32[]{:S(2)}, u32[]{:S(2)}) async-start(f32[16,1,2048]{2,1,0:T(1,128)} %reshape.105), calls=%async_computation.5 | async-start | bytes 262144 | tf_op jit(solution)/shard_map/all_to_all | solution.py:79
  174.6 1.1 copy-start.1
  221.5 13.0 %copy-start.7 = (f32[1024]{0:T(1024)S(1)}, f32[1024]{0:T(1024)}, u32[]{:S(2)}) copy-start(f32[1024]{0:T(1024)} %param.17) | copy-start | bytes 12292
  224.1 10.3 %all-to-all-start.10 = ((f32[2,64,1024]{2,1,0:T(8,128)}), f32[2,64,1024]{2,1,0:T(8,128)S(1)}, u32[]{:S(2)}, u32[]{:S(2)}) async-start(f32[2,64,1024]{2,1,0:T(8,128)} %bitcast.18), calls=%async_computation.10 | async-start | bytes 1048576 | tf_op jit(solution)/shard_map/all_to_all | solution.py:74

commit v9 on v7

--- a/solution.py
+++ b/solution.py
@@ -131,26 +131,14 @@
 
     direct, sens_part = penalty_slopes(base, outflow, lodf, limits)
 
-    matches = (outages[:, None] == monitored[None, :]).astype(jnp.float32)
-    flag_part = jnp.sum(matches, axis=1)
-    extended = jnp.concatenate(
-        [sens_part, flag_part[None, :], jnp.zeros((7, outage_total), jnp.float32)], axis=0
-    )
     out_share = outage_total // line_count
-    shares = extended.reshape(extended.shape[0], line_count, out_share).transpose(1, 0, 2)
-    mine = jnp.sum(lax.all_to_all(shares, LINE, 0, 0, tiled=False), axis=0)
-    sens_mine = mine[:scen_rows]
-    flag_mine = mine[scen_rows]
+    shares = sens_part.reshape(scen_rows, line_count, out_share).transpose(1, 0, 2)
+    sens_mine = jnp.sum(lax.all_to_all(shares, LINE, 0, 0, tiled=False), axis=0)
     sens_total = gather_columns(sens_mine, LINE, line_count)
-    backward = sens_total / outage_total
     outage_sens = sens_total / math.sqrt(monitored_total)
 
-    adjoint_monitored = (
-        direct + jnp.dot(backward, matches, precision=lax.Precision.HIGHEST)
-    ).astype(jnp.bfloat16)
-    adjoint_outage = jnp.where(
-        flag_mine[None, :] > 0.5, 0.0, sens_mine / outage_total
-    ).astype(jnp.bfloat16)
+    adjoint_monitored = direct.astype(jnp.bfloat16)
+    adjoint_outage = (sens_mine / outage_total).astype(jnp.bfloat16)
     piece = jnp.concatenate([adjoint_monitored, adjoint_outage], axis=1)
     all_piece = gather_rows(gather_rows(piece, "zh"), "y")
     grad_rows = all_piece.shape[0] // line_count

time: 237 us -> 233 us (0.983)
  blocking collectives: 92.8 us -> 62.8 us
  waiting for transfers between devices: 31.1 us -> 52.7 us
  starting transfers between devices: 34.9 us -> 40.8 us
    all_to_all x3 -> x2, blocking collectives: 66.3 us -> 38 us  [exchange_sum(): return jnp.sum(lax.all_to_all(blocks, axis, 0, 0, tiled=False), axis=0)]
    all_to_all x3 -> x4, waiting for transfers between devices: 25.2 us -> 48.5 us  [exchange_sum(): return jnp.sum(lax.all_to_all(blocks, axis, 0, 0, tiled=False), axis=0)]
    all_to_all x3 -> x4, starting transfers between devices: 17.3 us -> 21.9 us  [exchange_sum(): return jnp.sum(lax.all_to_all(blocks, axis, 0, 0, tiled=False), axis=0)]
    unnamed x26 -> x25, local copies, waits for them, and re-layouts: 4.44 us -> 5.3 us
  transfers between devices with their start and end apart: 6 -> 7, of which waited for: 5 -> 6; matrix products, arithmetic and copies ran while one was open for 10% -> 11% of each run, Pallas kernels for 0% -> 0%
where the time goes in v9:
time: 233 us; the launch traced here: 230 us
  blocking collectives  62.8 us (27%)
  waiting for transfers between devices  52.7 us (23%)
  starting transfers between devices  40.8 us (18%)
  other arithmetic  27.2 us (12%)
  Pallas kernels  19.6 us (8%)
  local copies, waits for them, and re-layouts  17.1 us (7%)
  matrix products  8.96 us (4%)
    all_to_all x4, waiting for transfers between devices, exchange_sum(): return jnp.sum(lax.all_to_all(blocks, axis, 0, 0, tiled=False), axis=0)  48.5 us
    all_to_all x2, blocking collectives, exchange_sum(): return jnp.sum(lax.all_to_all(blocks, axis, 0, 0, tiled=False), axis=0)  38 us
    all_to_all x2, blocking collectives, gather_rows(): gathered = lax.all_to_all(copies, axis, 0, 0, tiled=False)  24.7 us
    all_to_all x4, starting transfers between devices, exchange_sum(): return jnp.sum(lax.all_to_all(blocks, axis, 0, 0, tiled=False), axis=0)  21.9 us
    pallas_call x1, Pallas kernels, penalty_slopes(): pl.pallas_call(kernel, grid=(blocks,), in_specs=[pl.BlockSpec((None, moni...  19.6 us
    all_to_all x2, starting transfers between devices, gather_columns(): gathered = lax.all_to_all(copies, axis, 0, 0, tiled=False)  13.4 us
    reduce_sum x6, other arithmetic, exchange_sum(): return jnp.sum(lax.all_to_all(blocks, axis, 0, 0, tiled=False), axis=0)  8.66 us
    reduce_sum x1, other arithmetic, penalty_slopes(): direct = jnp.sum(direct_lanes, axis=2) / (2.0 * outage_total)  7.89 us
  transfers between devices with their start and end apart: 7, of which 6 were waited for; matrix products, arithmetic and copies ran while one was open for 11% of the time, Pallas kernels for 0%

profile of v9, /device:TPU:7, one launch (start us, length us, event | category | flops | bytes accessed | tf_op | source)
XLA Modules:
  0.0 230.0 jit_solution(3319577056236530942)
XLA Ops:
  0.6 0.0 copy-start
  0.7 0.8 compare_and_fusion
  1.5 0.1 broadcast_in_dim.74
  1.6 0.1 broadcast_in_dim.72
  1.7 0.6 copy-done
  2.2 2.0 gather_fusion.1
  4.3 0.0 copy-start.6
  4.3 1.2 select_select_fusion
  5.5 6.4 %all-to-all-start = ((bf16[16,32,1024]{2,1,0:T(8,128)(2,1)}), bf16[16,32,1024]{2,1,0:T(8,128)(2,1)S(1)}, u32[]{:S(2)}, u32[]{:S(2)}) async-start(bf16[16,32,1024]{2,1,0:T(8,128)(2,1)} %select_select_fusion), calls=%async_computation | async-start | bytes 2097152 | tf_op jit(solution)/shard_map/all_to_all | solution.py:71
  12.0 0.0 copy-start.3
  12.0 2.7 %gather_fusion = bf16[384,1024]{1,0:T(8,128)(2,1)} fusion(bf16[1024,1024]{1,0:T(8,128)(2,1)S(1)} %copy-done, s32[1024]{0:T(1024)S(1)} %pad_clamp_fusion.1), kind=kCustom, calls=%fused_computation | custom fusion | bytes 1574400 | tf_op jit(solution)/shard_map/jit(_take)/gather | solution.py:120
  14.7 2.2 broadcast_select_fusion
  16.9 4.9 %subtract_convert_fusion = bf16[1024,1024]{1,0:T(8,128)(2,1)} fusion(bf16[1024,1024]{1,0:T(8,128)(2,1)} %param.9, f32[24,1024]{1,0:T(8,128)S(1)} %copy-done.3, s32[1024]{0:T(1024)S(1)} %copy-done.4), kind=kOutput, calls=%fused_computation.2 | convolution fusion | flops 305160192 | bytes 4296704 | tf_op jit(solution)/shard_map/dot_general | solution.py:102
  21.7 5.2 %all-to-all-done = bf16[16,32,1024]{2,1,0:T(8,128)(2,1)S(1)} async-done(((bf16[16,32,1024]{2,1,0:T(8,128)(2,1)}), bf16[16,32,1024]{2,1,0:T(8,128)(2,1)S(1)}, u32[]{:S(2)}, u32[]{:S(2)}) %all-to-all-start) | async-done | bytes 1048608 | tf_op jit(solution)/shard_map/all_to_all | solution.py:71
  26.9 0.2 reduce_sum.75
  27.1 2.8 %fusion.2 = f32[1024,416]{0,1:T(8,128)S(1)} fusion(bf16[1024,1024]{1,0:T(8,128)(2,1)} %subtract_convert_fusion, bf16[32,1024]{1,0:T(8,128)(2,1)S(1)} %reduce_sum.75, bf16[384,1024]{1,0:T(8,128)(2,1)} %broadcast_select_fusion), kind=kOutput, calls=%fused_computation.9 | convolution fusion | flops 874119168 | bytes 4653056 | tf_op jit(solution)/shard_map/dot_general | solution.py:123
  29.9 0.2 copy.68
  30.1 25.9 %all_to_all.55 = f32[4,256,416]{1,2,0:T(8,128)} all-to-all(f32[4,256,416]{1,2,0:T(8,128)S(1)} %bitcast.42), channel_id=1, replica_groups=mesh['y'=4,'zh'=4,'zl'=2,'x'=4,'core'=2] {'y'}, dimensions={0} | all-to-all | bytes 3407872 | tf_op jit(solution)/shard_map/all_to_all | solution.py:71
  56.0 1.7 reduce_sum.76
  57.7 1.0 copy.51
  58.7 7.4 %all-to-all-start.2 = ((f32[4,64,416]{2,1,0:T(8,128)}), f32[4,64,416]{2,1,0:T(8,128)S(1)}, u32[]{:S(2)}, u32[]{:S(2)}) async-start(f32[4,64,416]{2,1,0:T(8,128)} %bitcast.1), calls=%async_computation.2 | async-start | bytes 1048576 | tf_op jit(solution)/shard_map/all_to_all | solution.py:71
  66.1 0.9 broadcast_multiply_fusion.lodf_ref
  67.0 14.0 %all-to-all-done.2 = f32[4,64,416]{2,1,0:T(8,128)S(1)} async-done(((f32[4,64,416]{2,1,0:T(8,128)}), f32[4,64,416]{2,1,0:T(8,128)S(1)}, u32[]{:S(2)}, u32[]{:S(2)}) %all-to-all-start.2) | async-done | bytes 426016 | tf_op jit(solution)/shard_map/all_to_all | solution.py:71
  81.1 0.1 copy.53
  81.2 0.8 reshape.94
  82.0 6.3 %all-to-all-start.3 = ((f32[16,1,2048]{2,1,0:T(1,128)}), f32[16,1,2048]{2,1,0:T(1,128)S(1)}, u32[]{:S(2)}, u32[]{:S(2)}) async-start(f32[16,1,2048]{2,1,0:T(1,128)} %reshape.94), calls=%async_computation.3 | async-start | bytes 262144 | tf_op jit(solution)/shard_map/all_to_all | solution.py:76
  88.3 0.8 reshape.93.lim_ref
  89.1 1.7 copy.52
  90.8 2.1 all-to-all-done.3
  93.0 0.5 broadcast.32
  93.5 0.9 reduce.1
  94.4 0.1 reshape.95
  94.5 0.8 copy.54.out_ref
  95.3 19.6 %shard_map.112 = (f32[64,384,128]{2,1,0:T(8,128)}, f32[64,512]{1,0:T(8,128)}) custom-call(f32[8,384,8]{2,1,0:T(8,128)} %bitcast.43, f32[64,512]{1,0:T(8,128)} %copy.54.out_ref, f32[384,512]{1,0:T(8,128)} %broadcast_multiply_fusion.lodf_ref, f32[384,1]{1,0:T(8,128)} %reshape.93.lim_ref), custom_call_target="tpu_custom_call" | custom-call | tf_op jit(solution)/shard_map/pallas_call | solution.py:47
  114.9 0.9 broadcast_multiply_fusion.2
  115.8 0.1 copy.56
  115.9 0.8 reshape.96
  116.8 5.5 %all-to-all-start.4 = ((f32[16,1,2048]{2,1,0:T(1,128)}), f32[16,1,2048]{2,1,0:T(1,128)S(1)}, u32[]{:S(2)}, u32[]{:S(2)}) async-start(f32[16,1,2048]{2,1,0:T(1,128)} %reshape.96), calls=%async_computation.4 | async-start | bytes 262144 | tf_op jit(solution)/shard_map/all_to_all | solution.py:136
  122.3 7.9 %reduce_sum.78 = f32[64,384]{1,0:T(8,128)S(1)} reduce(f32[64,384,128]{2,1,0:T(8,128)} %get-tuple-element.5, f32[]{:T(128)} %constant.38.clone.1), dimensions={2}, to_apply=%region_3.4 | reduce | flops 3121152 | bytes 12681220 | tf_op jit(solution)/shard_map/reduce_sum | solution.py:65
  130.2 1.0 reduce.2
  131.1 0.1 reshape.97
  131.3 0.1 copy.57
  131.4 12.0 %all_to_all.56 = bf16[4,64,416]{2,1,0:T(8,128)(2,1)S(1)} all-to-all(bf16[4,64,416]{2,1,0:T(8,128)(2,1)S(1)} %broadcast_in_dim.80), channel_id=1, replica_groups=mesh['y'=4,'zh'=4,'zl'=2,'x'=4,'core'=2] {'zh'}, dimensions={0} | all-to-all | bytes 425984 | tf_op jit(solution)/shard_map/all_to_all | solution.py:83
  143.4 0.1 copy.58
  143.6 0.1 broadcast_in_dim.82
  143.6 12.7 %all_to_all.57 = bf16[4,256,416]{1,2,0:T(8,128)(2,1)} all-to-all(bf16[4,256,416]{1,2,0:T(8,128)(2,1)S(1)} %broadcast_in_dim.82), channel_id=1, replica_groups=mesh['y'=4,'zh'=4,'zl'=2,'x'=4,'core'=2] {'y'}, dimensions={0} | all-to-all | bytes 1703936 | tf_op jit(solution)/shard_map/all_to_all | solution.py:83
  156.4 1.4 copy.59
  157.8 0.1 copy.60
  157.9 1.0 copy-done.1
  159.0 1.2 fusion
  160.2 12.1 %all_to_all.58 = f32[2,512,1024]{2,1,0:T(8,128)} all-to-all(f32[2,512,1024]{2,1,0:T(8,128)S(1)} %fusion), channel_id=1, replica_groups=mesh['y'=4,'zh'=4,'zl'=2,'x'=4,'core'=2] {'core'}, dimensions={0} | all-to-all | bytes 8388608 | tf_op jit(solution)/shard_map/all_to_all | solution.py:71
  172.3 4.1 %reduce_sum.80 = f32[512,1024]{1,0:T(8,128)} reduce(f32[2,512,1024]{2,1,0:T(8,128)} %all_to_all.58, f32[]{:T(128)} %constant.38.clone.1), dimensions={0}, to_apply=%region_5.6 | reduce | flops 524288 | bytes 6291460 | tf_op jit(solution)/shard_map/reduce_sum | solution.py:71
  176.5 4.5 %all-to-all-start.8 = ((f32[4,128,1024]{2,1,0:T(8,128)}), f32[4,128,1024]{2,1,0:T(8,128)}, u32[]{:S(2)}, u32[]{:S(2)}) async-start(f32[4,128,1024]{2,1,0:T(8,128)} %bitcast.41), calls=%async_computation.8 | async-start | bytes 4194304 | tf_op jit(solution)/shard_map/all_to_all | solution.py:71
  181.0 0.8 reshape.98
  181.8 23.5 %all-to-all-done.8 = f32[4,128,1024]{2,1,0:T(8,128)} async-done(((f32[4,128,1024]{2,1,0:T(8,128)}), f32[4,128,1024]{2,1,0:T(8,128)}, u32[]{:S(2)}, u32[]{:S(2)}) %all-to-all-start.8) | async-done | bytes 2097184 | tf_op jit(solution)/shard_map/all_to_all | solution.py:71
  205.4 7.1 %all-to-all-start.10 = ((f32[16,1,2048]{2,1,0:T(1,128)}), f32[16,1,2048]{2,1,0:T(1,128)S(1)}, u32[]{:S(2)}, u32[]{:S(2)}) async-start(f32[16,1,2048]{2,1,0:T(1,128)} %reshape.98), calls=%async_computation.10 | async-start | bytes 262144 | tf_op jit(solution)/shard_map/all_to_all | solution.py:76
  212.5 2.6 %reduce_sum.81 = f32[128,1024]{1,0:T(8,128)} reduce(f32[4,128,1024]{2,1,0:T(8,128)} %all-to-all-done.8, f32[]{:T(128)} %constant.38.clone.1), dimensions={0}, to_apply=%region_6.7 | reduce | flops 393216 | bytes 2621444 | tf_op jit(solution)/shard_map/reduce_sum | solution.py:71
  215.1 2.0 all-to-all-done.10
  217.1 3.5 %all-to-all-start.9 = ((f32[2,64,1024]{2,1,0:T(8,128)}), f32[2,64,1024]{2,1,0:T(8,128)S(1)}, u32[]{:S(2)}, u32[]{:S(2)}) async-start(f32[2,64,1024]{2,1,0:T(8,128)} %bitcast.14), calls=%async_computation.9 | async-start | bytes 1048576 | tf_op jit(solution)/shard_map/all_to_all | solution.py:71
  220.6 1.0 reduce.3
  221.6 0.1 reshape.99
  221.7 0.8 copy.63
  222.5 5.8 %all-to-all-done.9 = f32[2,64,1024]{2,1,0:T(8,128)S(1)} async-done(((f32[2,64,1024]{2,1,0:T(8,128)}), f32[2,64,1024]{2,1,0:T(8,128)S(1)}, u32[]{:S(2)}, u32[]{:S(2)}) %all-to-all-start.9) | async-done | bytes 524320 | tf_op jit(solution)/shard_map/all_to_all | solution.py:71
  228.4 1.6 add_convert_fusion
  (28 shorter events, 0.3 us)
Async XLA Ops:
  0.6 1.6 copy-start
  4.3 7.7 %copy-start.6 = (s32[384]{0:T(512)S(1)}, s32[384]{0:T(512)}, u32[]{:S(2)}) copy-start(s32[384]{0:T(512)} %param.15) | copy-start | bytes 4612
  5.5 21.4 %all-to-all-start = ((bf16[16,32,1024]{2,1,0:T(8,128)(2,1)}), bf16[16,32,1024]{2,1,0:T(8,128)(2,1)S(1)}, u32[]{:S(2)}, u32[]{:S(2)}) async-start(bf16[16,32,1024]{2,1,0:T(8,128)(2,1)} %select_select_fusion), calls=%async_computation | async-start | bytes 2097152 | tf_op jit(solution)/shard_map/all_to_all | solution.py:71
  12.0 4.9 %copy-start.3 = (f32[24,1024]{1,0:T(8,128)S(1)}, f32[24,1024]{1,0:T(8,128)}, u32[]{:S(2)}) copy-start(f32[24,1024]{1,0:T(8,128)} %param.10) | copy-start | bytes 294916
  12.0 4.9 %copy-start.4 = (s32[1024]{0:T(1024)S(1)}, s32[1024]{0:T(1024)}, u32[]{:S(2)}) copy-start(s32[1024]{0:T(1024)} %param.11) | copy-start | bytes 12292
  56.0 10.1 %copy-start.2 = (f32[384,512]{1,0:T(8,128)S(1)}, f32[384,512]{1,0:T(8,128)}, u32[]{:S(2)}) copy-start(f32[384,512]{1,0:T(8,128)} %param.13) | copy-start | bytes 2359300
  58.7 29.6 %copy-start.7 = (f32[384]{0:T(512)S(1)}, f32[384]{0:T(512)}, u32[]{:S(2)}) copy-start(f32[384]{0:T(512)} %param.14) | copy-start | bytes 4612
  58.7 22.3 %all-to-all-start.2 = ((f32[4,64,416]{2,1,0:T(8,128)}), f32[4,64,416]{2,1,0:T(8,128)S(1)}, u32[]{:S(2)}, u32[]{:S(2)}) async-start(f32[4,64,416]{2,1,0:T(8,128)} %bitcast.1), calls=%async_computation.2 | async-start | bytes 1048576 | tf_op jit(solution)/shard_map/all_to_all | solution.py:71
  82.0 11.0 %all-to-all-start.3 = ((f32[16,1,2048]{2,1,0:T(1,128)}), f32[16,1,2048]{2,1,0:T(1,128)S(1)}, u32[]{:S(2)}, u32[]{:S(2)}) async-start(f32[16,1,2048]{2,1,0:T(1,128)} %reshape.94), calls=%async_computation.3 | async-start | bytes 262144 | tf_op jit(solution)/shard_map/all_to_all | solution.py:76
  116.8 13.4 %all-to-all-start.4 = ((f32[16,1,2048]{2,1,0:T(1,128)}), f32[16,1,2048]{2,1,0:T(1,128)S(1)}, u32[]{:S(2)}, u32[]{:S(2)}) async-start(f32[16,1,2048]{2,1,0:T(1,128)} %reshape.96), calls=%async_computation.4 | async-start | bytes 262144 | tf_op jit(solution)/shard_map/all_to_all | solution.py:136
  157.8 1.1 copy-start.1
  176.5 28.9 %all-to-all-start.8 = ((f32[4,128,1024]{2,1,0:T(8,128)}), f32[4,128,1024]{2,1,0:T(8,128)}, u32[]{:S(2)}, u32[]{:S(2)}) async-start(f32[4,128,1024]{2,1,0:T(8,128)} %bitcast.41), calls=%async_computation.8 | async-start | bytes 4194304 | tf_op jit(solution)/shard_map/all_to_all | solution.py:71
  205.4 11.8 %all-to-all-start.10 = ((f32[16,1,2048]{2,1,0:T(1,128)}), f32[16,1,2048]{2,1,0:T(1,128)S(1)}, u32[]{:S(2)}, u32[]{:S(2)}) async-start(f32[16,1,2048]{2,1,0:T(1,128)} %reshape.98), calls=%async_computation.10 | async-start | bytes 262144 | tf_op jit(solution)/shard_map/all_to_all | solution.py:76
  215.1 13.3 %copy-start.5 = (f32[1024]{0:T(1024)S(1)}, f32[1024]{0:T(1024)}, u32[]{:S(2)}) copy-start(f32[1024]{0:T(1024)} %param.17) | copy-start | bytes 12292
  217.1 11.2 %all-to-all-start.9 = ((f32[2,64,1024]{2,1,0:T(8,128)}), f32[2,64,1024]{2,1,0:T(8,128)S(1)}, u32[]{:S(2)}, u32[]{:S(2)}) async-start(f32[2,64,1024]{2,1,0:T(8,128)} %bitcast.14), calls=%async_computation.9 | async-start | bytes 1048576 | tf_op jit(solution)/shard_map/all_to_all | solution.py:71

commit v10 on v9

--- a/solution.py
+++ b/solution.py
@@ -131,14 +131,20 @@
 
     direct, sens_part = penalty_slopes(base, outflow, lodf, limits)
 
+    matches = (outages[:, None] == monitored[None, :]).astype(jnp.float32)
+    is_outage = jnp.sum(matches, axis=0)
+    direct_at = jnp.dot(direct, matches.T, precision=lax.Precision.HIGHEST)
     out_share = outage_total // line_count
-    shares = sens_part.reshape(scen_rows, line_count, out_share).transpose(1, 0, 2)
-    sens_mine = jnp.sum(lax.all_to_all(shares, LINE, 0, 0, tiled=False), axis=0)
+    both = jnp.concatenate([sens_part, direct_at], axis=0)
+    shares = both.reshape(both.shape[0], line_count, out_share).transpose(1, 0, 2)
+    mine = jnp.sum(lax.all_to_all(shares, LINE, 0, 0, tiled=False), axis=0)
+    sens_mine = mine[:scen_rows]
+    direct_mine = mine[scen_rows:]
     sens_total = gather_columns(sens_mine, LINE, line_count)
     outage_sens = sens_total / math.sqrt(monitored_total)
 
-    adjoint_monitored = direct.astype(jnp.bfloat16)
-    adjoint_outage = (sens_mine / outage_total).astype(jnp.bfloat16)
+    adjoint_monitored = jnp.where(is_outage[None, :] > 0.5, 0.0, direct).astype(jnp.bfloat16)
+    adjoint_outage = (direct_mine + sens_mine / outage_total).astype(jnp.bfloat16)
     piece = jnp.concatenate([adjoint_monitored, adjoint_outage], axis=1)
     all_piece = gather_rows(gather_rows(piece, "zh"), "y")
     grad_rows = all_piece.shape[0] // line_count

time: 233 us -> 238 us (1.021)
  waiting for transfers between devices: 52.7 us -> 60 us
    all_to_all x1, waiting for transfers between devices: 0.01 us -> 5.88 us  [on_device(): mine = jnp.sum(lax.all_to_all(shares, LINE, 0, 0, tiled=False), axis=0)]
    unnamed x25 -> x27, local copies, waits for them, and re-layouts: 5.3 us -> 4.37 us
  transfers between devices with their start and end apart: 7 -> 7, of which waited for: 6 -> 7; matrix products, arithmetic and copies ran while one was open for 11% -> 8% of each run, Pallas kernels for 0% -> 0%
where the time goes in v10:
time: 238 us; the launch traced here: 235 us
  blocking collectives  63.3 us (27%)
  waiting for transfers between devices  60 us (25%)
  starting transfers between devices  39 us (16%)
  other arithmetic  25.6 us (11%)
  Pallas kernels  19.6 us (8%)
  local copies, waits for them, and re-layouts  16.9 us (7%)
  matrix products  9.56 us (4%)
    all_to_all x4, waiting for transfers between devices, exchange_sum(): return jnp.sum(lax.all_to_all(blocks, axis, 0, 0, tiled=False), axis=0)  49.9 us
    all_to_all x2, blocking collectives, exchange_sum(): return jnp.sum(lax.all_to_all(blocks, axis, 0, 0, tiled=False), axis=0)  36.5 us
    all_to_all x2, blocking collectives, gather_rows(): gathered = lax.all_to_all(copies, axis, 0, 0, tiled=False)  26.7 us
    all_to_all x4, starting transfers between devices, exchange_sum(): return jnp.sum(lax.all_to_all(blocks, axis, 0, 0, tiled=False), axis=0)  21.8 us
    pallas_call x1, Pallas kernels, penalty_slopes(): pl.pallas_call(kernel, grid=(blocks,), in_specs=[pl.BlockSpec((None, moni...  19.6 us
    all_to_all x2, starting transfers between devices, gather_columns(): gathered = lax.all_to_all(copies, axis, 0, 0, tiled=False)  11.7 us
    reduce_sum x6, other arithmetic, exchange_sum(): return jnp.sum(lax.all_to_all(blocks, axis, 0, 0, tiled=False), axis=0)  8.66 us
    reduce_sum x1, other arithmetic, penalty_slopes(): direct = jnp.sum(direct_lanes, axis=2) / (2.0 * outage_total)  7.93 us
  transfers between devices with their start and end apart: 7, of which 7 were waited for; matrix products, arithmetic and copies ran while one was open for 8% of the time, Pallas kernels for 0%

profile of v10, /device:TPU:7, one launch (start us, length us, event | category | flops | bytes accessed | tf_op | source)
XLA Modules:
  0.0 234.8 jit_solution(1124307378108138204)
XLA Ops:
  0.6 0.0 copy-start
  0.7 0.8 compare_and_fusion
  1.5 0.1 broadcast_in_dim.89
  1.6 0.1 broadcast_in_dim.91
  1.7 0.6 copy-done
  2.2 2.0 gather_fusion.1
  4.3 0.0 copy-start.5
  4.3 1.2 select_select_fusion
  5.5 6.4 %all-to-all-start = ((bf16[16,32,1024]{2,1,0:T(8,128)(2,1)}), bf16[16,32,1024]{2,1,0:T(8,128)(2,1)S(1)}, u32[]{:S(2)}, u32[]{:S(2)}) async-start(bf16[16,32,1024]{2,1,0:T(8,128)(2,1)} %select_select_fusion), calls=%async_computation | async-start | bytes 2097152 | tf_op jit(solution)/shard_map/all_to_all | solution.py:71
  12.0 0.0 copy-start.4
  12.0 2.7 %gather_fusion = bf16[384,1024]{1,0:T(8,128)(2,1)} fusion(bf16[1024,1024]{1,0:T(8,128)(2,1)S(1)} %copy-done, s32[1024]{0:T(1024)S(1)} %pad_clamp_fusion.1), kind=kCustom, calls=%fused_computation | custom fusion | bytes 1574400 | tf_op jit(solution)/shard_map/jit(_take)/gather | solution.py:120
  14.7 2.2 broadcast_select_fusion
  16.9 4.9 %subtract_convert_fusion = bf16[1024,1024]{1,0:T(8,128)(2,1)} fusion(bf16[1024,1024]{1,0:T(8,128)(2,1)} %param.9, f32[24,1024]{1,0:T(8,128)S(1)} %copy-done.4, s32[1024]{0:T(1024)S(1)} %copy-done.7), kind=kOutput, calls=%fused_computation.2 | convolution fusion | flops 305160192 | bytes 4296704 | tf_op jit(solution)/shard_map/dot_general | solution.py:102
  21.7 5.2 %all-to-all-done = bf16[16,32,1024]{2,1,0:T(8,128)(2,1)S(1)} async-done(((bf16[16,32,1024]{2,1,0:T(8,128)(2,1)}), bf16[16,32,1024]{2,1,0:T(8,128)(2,1)S(1)}, u32[]{:S(2)}, u32[]{:S(2)}) %all-to-all-start) | async-done | bytes 1048608 | tf_op jit(solution)/shard_map/all_to_all | solution.py:71
  26.9 0.2 reduce_sum.85
  27.1 2.8 %fusion.5 = f32[1024,416]{0,1:T(8,128)S(1)} fusion(bf16[1024,1024]{1,0:T(8,128)(2,1)} %subtract_convert_fusion, bf16[32,1024]{1,0:T(8,128)(2,1)S(1)} %reduce_sum.85, bf16[384,1024]{1,0:T(8,128)(2,1)} %broadcast_select_fusion), kind=kOutput, calls=%fused_computation.13 | convolution fusion | flops 874119168 | bytes 4653056 | tf_op jit(solution)/shard_map/dot_general | solution.py:123
  29.9 0.2 copy.68
  30.1 25.9 %all_to_all.55 = f32[4,256,416]{1,2,0:T(8,128)} all-to-all(f32[4,256,416]{1,2,0:T(8,128)S(1)} %bitcast.39), channel_id=1, replica_groups=mesh['y'=4,'zh'=4,'zl'=2,'x'=4,'core'=2] {'y'}, dimensions={0} | all-to-all | bytes 3407872 | tf_op jit(solution)/shard_map/all_to_all | solution.py:71
  56.0 1.7 reduce_sum.86
  57.7 1.0 copy.51
  58.7 7.4 %all-to-all-start.2 = ((f32[4,64,416]{2,1,0:T(8,128)}), f32[4,64,416]{2,1,0:T(8,128)S(1)}, u32[]{:S(2)}, u32[]{:S(2)}) async-start(f32[4,64,416]{2,1,0:T(8,128)} %bitcast.1), calls=%async_computation.2 | async-start | bytes 1048576 | tf_op jit(solution)/shard_map/all_to_all | solution.py:71
  66.1 0.9 broadcast_multiply_fusion.lodf_ref
  67.0 14.0 %all-to-all-done.2 = f32[4,64,416]{2,1,0:T(8,128)S(1)} async-done(((f32[4,64,416]{2,1,0:T(8,128)}), f32[4,64,416]{2,1,0:T(8,128)S(1)}, u32[]{:S(2)}, u32[]{:S(2)}) %all-to-all-start.2) | async-done | bytes 426016 | tf_op jit(solution)/shard_map/all_to_all | solution.py:71
  81.0 0.1 copy.53
  81.2 0.8 reshape.100
  82.0 6.3 %all-to-all-start.3 = ((f32[16,1,2048]{2,1,0:T(1,128)}), f32[16,1,2048]{2,1,0:T(1,128)S(1)}, u32[]{:S(2)}, u32[]{:S(2)}) async-start(f32[16,1,2048]{2,1,0:T(1,128)} %reshape.100), calls=%async_computation.3 | async-start | bytes 262144 | tf_op jit(solution)/shard_map/all_to_all | solution.py:76
  88.3 0.8 reshape.99.lim_ref
  89.1 1.7 copy.52
  90.8 2.1 all-to-all-done.3
  93.0 0.5 broadcast.39
  93.5 0.9 reduce.1
  94.4 0.1 reshape.101
  94.5 0.8 copy.54.out_ref
  95.3 19.6 %shard_map.112 = (f32[64,384,128]{2,1,0:T(8,128)}, f32[64,512]{1,0:T(8,128)}) custom-call(f32[8,384,8]{2,1,0:T(8,128)} %bitcast.40, f32[64,512]{1,0:T(8,128)} %copy.54.out_ref, f32[384,512]{1,0:T(8,128)} %broadcast_multiply_fusion.lodf_ref, f32[384,1]{1,0:T(8,128)} %reshape.99.lim_ref), custom_call_target="tpu_custom_call" | custom-call | tf_op jit(solution)/shard_map/pallas_call | solution.py:47
  114.9 7.9 %reduce_sum.88 = f32[64,384]{1,0:T(8,128)S(1)} reduce(f32[64,384,128]{2,1,0:T(8,128)} %get-tuple-element.5, f32[]{:T(128)} %constant.35.clone.1), dimensions={2}, to_apply=%region_4.5 | reduce | flops 3121152 | bytes 12681220 | tf_op jit(solution)/shard_map/reduce_sum | solution.py:65
  122.9 0.6 fusion
  123.5 0.8 copy.56
  124.3 5.5 %all-to-all-start.4 = ((f32[16,128,32]{1,2,0:T(8,128)}), f32[16,128,32]{1,2,0:T(8,128)S(1)}, u32[]{:S(2)}, u32[]{:S(2)}) async-start(f32[16,128,32]{1,2,0:T(8,128)} %bitcast.7), calls=%async_computation.4 | async-start | bytes 524288 | tf_op jit(solution)/shard_map/all_to_all | solution.py:140
  129.8 0.2 fusion.4
  130.0 5.9 %all-to-all-done.4 = f32[16,128,32]{1,2,0:T(8,128)S(1)} async-done(((f32[16,128,32]{1,2,0:T(8,128)}), f32[16,128,32]{1,2,0:T(8,128)S(1)}, u32[]{:S(2)}, u32[]{:S(2)}) %all-to-all-start.4) | async-done | bytes 262176 | tf_op jit(solution)/shard_map/all_to_all | solution.py:140
  135.9 0.1 fusion.16
  136.0 0.1 copy.57
  136.1 12.5 %all_to_all.56 = bf16[4,64,416]{2,1,0:T(8,128)(2,1)S(1)} all-to-all(bf16[4,64,416]{2,1,0:T(8,128)(2,1)S(1)} %broadcast_in_dim.97), channel_id=1, replica_groups=mesh['y'=4,'zh'=4,'zl'=2,'x'=4,'core'=2] {'zh'}, dimensions={0} | all-to-all | bytes 425984 | tf_op jit(solution)/shard_map/all_to_all | solution.py:83
  148.6 0.1 copy.58
  148.8 0.1 broadcast_in_dim.99
  148.8 14.2 %all_to_all.57 = bf16[4,256,416]{1,2,0:T(8,128)(2,1)} all-to-all(bf16[4,256,416]{1,2,0:T(8,128)(2,1)S(1)} %broadcast_in_dim.99), channel_id=1, replica_groups=mesh['y'=4,'zh'=4,'zl'=2,'x'=4,'core'=2] {'y'}, dimensions={0} | all-to-all | bytes 1703936 | tf_op jit(solution)/shard_map/all_to_all | solution.py:83
  163.1 1.4 copy.59
  164.5 0.1 copy.60
  164.6 1.0 copy-done.1
  165.6 1.2 fusion.2
  166.9 10.7 %all_to_all.58 = f32[2,512,1024]{2,1,0:T(8,128)} all-to-all(f32[2,512,1024]{2,1,0:T(8,128)S(1)} %fusion.2), channel_id=1, replica_groups=mesh['y'=4,'zh'=4,'zl'=2,'x'=4,'core'=2] {'core'}, dimensions={0} | all-to-all | bytes 8388608 | tf_op jit(solution)/shard_map/all_to_all | solution.py:71
  177.5 4.1 %reduce_sum.90 = f32[512,1024]{1,0:T(8,128)} reduce(f32[2,512,1024]{2,1,0:T(8,128)} %all_to_all.58, f32[]{:T(128)} %constant.35.clone.1), dimensions={0}, to_apply=%region_6.7 | reduce | flops 524288 | bytes 6291460 | tf_op jit(solution)/shard_map/reduce_sum | solution.py:71
  181.7 4.5 %all-to-all-start.8 = ((f32[4,128,1024]{2,1,0:T(8,128)}), f32[4,128,1024]{2,1,0:T(8,128)}, u32[]{:S(2)}, u32[]{:S(2)}) async-start(f32[4,128,1024]{2,1,0:T(8,128)} %bitcast.38), calls=%async_computation.8 | async-start | bytes 4194304 | tf_op jit(solution)/shard_map/all_to_all | solution.py:71
  186.2 0.8 reshape.102
  187.0 25.0 %all-to-all-done.8 = f32[4,128,1024]{2,1,0:T(8,128)} async-done(((f32[4,128,1024]{2,1,0:T(8,128)}), f32[4,128,1024]{2,1,0:T(8,128)}, u32[]{:S(2)}, u32[]{:S(2)}) %all-to-all-start.8) | async-done | bytes 2097184 | tf_op jit(solution)/shard_map/all_to_all | solution.py:71
  212.0 5.4 %all-to-all-start.10 = ((f32[16,1,2048]{2,1,0:T(1,128)}), f32[16,1,2048]{2,1,0:T(1,128)S(1)}, u32[]{:S(2)}, u32[]{:S(2)}) async-start(f32[16,1,2048]{2,1,0:T(1,128)} %reshape.102), calls=%async_computation.10 | async-start | bytes 262144 | tf_op jit(solution)/shard_map/all_to_all | solution.py:76
  217.3 2.6 %reduce_sum.91 = f32[128,1024]{1,0:T(8,128)} reduce(f32[4,128,1024]{2,1,0:T(8,128)} %all-to-all-done.8, f32[]{:T(128)} %constant.35.clone.1), dimensions={0}, to_apply=%region_7.8 | reduce | flops 393216 | bytes 2621444 | tf_op jit(solution)/shard_map/reduce_sum | solution.py:71
  219.9 2.0 all-to-all-done.10
  222.0 3.5 %all-to-all-start.9 = ((f32[2,64,1024]{2,1,0:T(8,128)}), f32[2,64,1024]{2,1,0:T(8,128)S(1)}, u32[]{:S(2)}, u32[]{:S(2)}) async-start(f32[2,64,1024]{2,1,0:T(8,128)} %bitcast.14), calls=%async_computation.9 | async-start | bytes 1048576 | tf_op jit(solution)/shard_map/all_to_all | solution.py:71
  225.5 1.0 reduce.2
  226.4 0.1 reshape.103
  226.6 0.8 copy.63
  227.4 5.8 %all-to-all-done.9 = f32[2,64,1024]{2,1,0:T(8,128)S(1)} async-done(((f32[2,64,1024]{2,1,0:T(8,128)}), f32[2,64,1024]{2,1,0:T(8,128)S(1)}, u32[]{:S(2)}, u32[]{:S(2)}) %all-to-all-start.9) | async-done | bytes 524320 | tf_op jit(solution)/shard_map/all_to_all | solution.py:71
  233.2 1.6 add_convert_fusion
  (33 shorter events, 0.3 us)
Async XLA Ops:
  0.6 1.6 copy-start
  4.3 7.7 %copy-start.5 = (s32[384]{0:T(512)S(1)}, s32[384]{0:T(512)}, u32[]{:S(2)}) copy-start(s32[384]{0:T(512)} %param.15) | copy-start | bytes 4612
  5.5 21.4 %all-to-all-start = ((bf16[16,32,1024]{2,1,0:T(8,128)(2,1)}), bf16[16,32,1024]{2,1,0:T(8,128)(2,1)S(1)}, u32[]{:S(2)}, u32[]{:S(2)}) async-start(bf16[16,32,1024]{2,1,0:T(8,128)(2,1)} %select_select_fusion), calls=%async_computation | async-start | bytes 2097152 | tf_op jit(solution)/shard_map/all_to_all | solution.py:71
  12.0 4.9 %copy-start.4 = (f32[24,1024]{1,0:T(8,128)S(1)}, f32[24,1024]{1,0:T(8,128)}, u32[]{:S(2)}) copy-start(f32[24,1024]{1,0:T(8,128)} %param.10) | copy-start | bytes 294916
  12.0 4.9 %copy-start.7 = (s32[1024]{0:T(1024)S(1)}, s32[1024]{0:T(1024)}, u32[]{:S(2)}) copy-start(s32[1024]{0:T(1024)} %param.11) | copy-start | bytes 12292
  56.0 10.1 %copy-start.2 = (f32[384,512]{1,0:T(8,128)S(1)}, f32[384,512]{1,0:T(8,128)}, u32[]{:S(2)}) copy-start(f32[384,512]{1,0:T(8,128)} %param.13) | copy-start | bytes 2359300
  58.7 29.6 %copy-start.9 = (f32[384]{0:T(512)S(1)}, f32[384]{0:T(512)}, u32[]{:S(2)}) copy-start(f32[384]{0:T(512)} %param.14) | copy-start | bytes 4612
  58.7 22.3 %all-to-all-start.2 = ((f32[4,64,416]{2,1,0:T(8,128)}), f32[4,64,416]{2,1,0:T(8,128)S(1)}, u32[]{:S(2)}, u32[]{:S(2)}) async-start(f32[4,64,416]{2,1,0:T(8,128)} %bitcast.1), calls=%async_computation.2 | async-start | bytes 1048576 | tf_op jit(solution)/shard_map/all_to_all | solution.py:71
  82.0 11.0 %all-to-all-start.3 = ((f32[16,1,2048]{2,1,0:T(1,128)}), f32[16,1,2048]{2,1,0:T(1,128)S(1)}, u32[]{:S(2)}, u32[]{:S(2)}) async-start(f32[16,1,2048]{2,1,0:T(1,128)} %reshape.100), calls=%async_computation.3 | async-start | bytes 262144 | tf_op jit(solution)/shard_map/all_to_all | solution.py:76
  114.9 7.9 %copy-start.6 = (s32[512]{0:T(512)S(1)}, s32[512]{0:T(512)}, u32[]{:S(2)}) copy-start(s32[512]{0:T(512)} %param.16) | copy-start | bytes 6148
  114.9 8.6 %copy-start.3 = (f32[64,512]{1,0:T(8,128)S(1)}, f32[64,512]{1,0:T(8,128)}, u32[]{:S(2)}) copy-start(f32[64,512]{1,0:T(8,128)} %get-tuple-element.6) | copy-start | bytes 393220
  124.3 11.5 %all-to-all-start.4 = ((f32[16,128,32]{1,2,0:T(8,128)}), f32[16,128,32]{1,2,0:T(8,128)S(1)}, u32[]{:S(2)}, u32[]{:S(2)}) async-start(f32[16,128,32]{1,2,0:T(8,128)} %bitcast.7), calls=%async_computation.4 | async-start | bytes 524288 | tf_op jit(solution)/shard_map/all_to_all | solution.py:140
  164.5 1.1 copy-start.1
  181.7 30.3 %all-to-all-start.8 = ((f32[4,128,1024]{2,1,0:T(8,128)}), f32[4,128,1024]{2,1,0:T(8,128)}, u32[]{:S(2)}, u32[]{:S(2)}) async-start(f32[4,128,1024]{2,1,0:T(8,128)} %bitcast.38), calls=%async_computation.8 | async-start | bytes 4194304 | tf_op jit(solution)/shard_map/all_to_all | solution.py:71
  212.0 10.0 %all-to-all-start.10 = ((f32[16,1,2048]{2,1,0:T(1,128)}), f32[16,1,2048]{2,1,0:T(1,128)S(1)}, u32[]{:S(2)}, u32[]{:S(2)}) async-start(f32[16,1,2048]{2,1,0:T(1,128)} %reshape.102), calls=%async_computation.10 | async-start | bytes 262144 | tf_op jit(solution)/shard_map/all_to_all | solution.py:76
  219.9 13.3 %copy-start.8 = (f32[1024]{0:T(1024)S(1)}, f32[1024]{0:T(1024)}, u32[]{:S(2)}) copy-start(f32[1024]{0:T(1024)} %param.17) | copy-start | bytes 12292
  222.0 11.2 %all-to-all-start.9 = ((f32[2,64,1024]{2,1,0:T(8,128)}), f32[2,64,1024]{2,1,0:T(8,128)S(1)}, u32[]{:S(2)}, u32[]{:S(2)}) async-start(f32[2,64,1024]{2,1,0:T(8,128)} %bitcast.14), calls=%async_computation.9 | async-start | bytes 1048576 | tf_op jit(solution)/shard_map/all_to_all | solution.py:71

commit v11 on v7

--- a/solution.py
+++ b/solution.py
@@ -157,11 +157,11 @@
     staged_order = [lax.axis_size(name) for name in LINE]
     ordered_piece = (
         all_piece.reshape(staged_order + [grad_rows, all_piece.shape[1]])
-        .transpose(2, 1, 0, 3, 4)
+        .transpose(2, 0, 1, 3, 4)
         .reshape(all_piece.shape)
     )
     pushed = jnp.dot(ordered_piece, rows, preferred_element_type=jnp.float32)
-    for name in LINE[::-1]:
+    for name in ("core", "zl", "x"):
         pushed = exchange_sum(pushed, name, lax.axis_size(name))
     own_generation = lax.dynamic_slice_in_dim(
         generation, line_index() * grad_rows, grad_rows, 0

time: 237 us -> 244 us (1.030)
  waiting for transfers between devices: 31.1 us -> 36.5 us
    all_to_all x3, waiting for transfers between devices: 25.2 us -> 30.5 us  [exchange_sum(): return jnp.sum(lax.all_to_all(blocks, axis, 0, 0, tiled=False), axis=0)]
  transfers between devices with their start and end apart: 6 -> 6, of which waited for: 5 -> 5; matrix products, arithmetic and copies ran while one was open for 10% -> 9% of each run, Pallas kernels for 0% -> 0%
where the time goes in v11:
time: 244 us; the launch traced here: 240 us
  blocking collectives  93.4 us (38%)
  waiting for transfers between devices  36.5 us (15%)
  starting transfers between devices  36 us (15%)
  other arithmetic  27.8 us (11%)
  Pallas kernels  19.6 us (8%)
  local copies, waits for them, and re-layouts  16.4 us (7%)
  matrix products  9.46 us (4%)
    all_to_all x3, blocking collectives, exchange_sum(): return jnp.sum(lax.all_to_all(blocks, axis, 0, 0, tiled=False), axis=0)  66.8 us
    all_to_all x3, waiting for transfers between devices, exchange_sum(): return jnp.sum(lax.all_to_all(blocks, axis, 0, 0, tiled=False), axis=0)  30.5 us
    all_to_all x2, blocking collectives, gather_rows(): gathered = lax.all_to_all(copies, axis, 0, 0, tiled=False)  26.6 us
    pallas_call x1, Pallas kernels, penalty_slopes(): pl.pallas_call(kernel, grid=(blocks,), in_specs=[pl.BlockSpec((None, moni...  19.6 us
    all_to_all x3, starting transfers between devices, exchange_sum(): return jnp.sum(lax.all_to_all(blocks, axis, 0, 0, tiled=False), axis=0)  18.4 us
    all_to_all x2, starting transfers between devices, gather_columns(): gathered = lax.all_to_all(copies, axis, 0, 0, tiled=False)  12.1 us
    reduce_sum x6, other arithmetic, exchange_sum(): return jnp.sum(lax.all_to_all(blocks, axis, 0, 0, tiled=False), axis=0)  8.94 us
    reduce_sum x1, other arithmetic, penalty_slopes(): direct = jnp.sum(direct_lanes, axis=2) / (2.0 * outage_total)  7.89 us
  transfers between devices with their start and end apart: 6, of which 5 were waited for; matrix products, arithmetic and copies ran while one was open for 9% of the time, Pallas kernels for 0%

profile of v11, /device:TPU:7, one launch (start us, length us, event | category | flops | bytes accessed | tf_op | source)
XLA Modules:
  0.0 240.1 jit_solution(4660555158011892157)
XLA Ops:
  0.7 0.8 compare_and_fusion
  1.5 0.1 broadcast_in_dim.92
  1.6 0.1 broadcast_in_dim.94
  1.7 0.6 copy-done
  2.2 2.0 gather_fusion.1
  4.3 1.2 select_select_fusion
  5.5 6.4 %all-to-all-start = ((bf16[16,32,1024]{2,1,0:T(8,128)(2,1)}), bf16[16,32,1024]{2,1,0:T(8,128)(2,1)S(1)}, u32[]{:S(2)}, u32[]{:S(2)}) async-start(bf16[16,32,1024]{2,1,0:T(8,128)(2,1)} %select_select_fusion), calls=%async_computation | async-start | bytes 2097152 | tf_op jit(solution)/shard_map/all_to_all | solution.py:71
  12.0 2.7 %gather_fusion = bf16[384,1024]{1,0:T(8,128)(2,1)} fusion(bf16[1024,1024]{1,0:T(8,128)(2,1)S(1)} %copy-done, s32[1024]{0:T(1024)S(1)} %pad_clamp_fusion.1), kind=kCustom, calls=%fused_computation | custom fusion | bytes 1574400 | tf_op jit(solution)/shard_map/jit(_take)/gather | solution.py:120
  14.7 2.2 broadcast_select_fusion
  16.9 4.9 %subtract_convert_fusion = bf16[1024,1024]{1,0:T(8,128)(2,1)} fusion(bf16[1024,1024]{1,0:T(8,128)(2,1)} %param.9, f32[24,1024]{1,0:T(8,128)S(1)} %copy-done.3, s32[1024]{0:T(1024)S(1)} %copy-done.6), kind=kOutput, calls=%fused_computation.2 | convolution fusion | flops 305160192 | bytes 4296704 | tf_op jit(solution)/shard_map/dot_general | solution.py:102
  21.7 5.2 %all-to-all-done = bf16[16,32,1024]{2,1,0:T(8,128)(2,1)S(1)} async-done(((bf16[16,32,1024]{2,1,0:T(8,128)(2,1)}), bf16[16,32,1024]{2,1,0:T(8,128)(2,1)S(1)}, u32[]{:S(2)}, u32[]{:S(2)}) %all-to-all-start) | async-done | bytes 1048608 | tf_op jit(solution)/shard_map/all_to_all | solution.py:71
  26.9 0.2 reduce_sum.84
  27.1 2.8 %fusion.5 = f32[1024,416]{0,1:T(8,128)S(1)} fusion(bf16[1024,1024]{1,0:T(8,128)(2,1)} %subtract_convert_fusion, bf16[32,1024]{1,0:T(8,128)(2,1)S(1)} %reduce_sum.84, bf16[384,1024]{1,0:T(8,128)(2,1)} %broadcast_select_fusion), kind=kOutput, calls=%fused_computation.14 | convolution fusion | flops 874119168 | bytes 4653056 | tf_op jit(solution)/shard_map/dot_general | solution.py:123
  29.9 0.2 copy.88
  30.1 25.9 %all_to_all.55 = f32[4,256,416]{1,2,0:T(8,128)} all-to-all(f32[4,256,416]{1,2,0:T(8,128)S(1)} %bitcast.44), channel_id=1, replica_groups=mesh['y'=4,'zh'=4,'zl'=2,'x'=4,'core'=2] {'y'}, dimensions={0} | all-to-all | bytes 3407872 | tf_op jit(solution)/shard_map/all_to_all | solution.py:71
  56.0 1.7 reduce_sum.85
  57.7 1.0 copy.68
  58.7 7.4 %all-to-all-start.2 = ((f32[4,64,416]{2,1,0:T(8,128)}), f32[4,64,416]{2,1,0:T(8,128)S(1)}, u32[]{:S(2)}, u32[]{:S(2)}) async-start(f32[4,64,416]{2,1,0:T(8,128)} %bitcast.1), calls=%async_computation.2 | async-start | bytes 1048576 | tf_op jit(solution)/shard_map/all_to_all | solution.py:71
  66.1 0.9 broadcast_multiply_fusion.lodf_ref
  67.1 13.9 %all-to-all-done.2 = f32[4,64,416]{2,1,0:T(8,128)S(1)} async-done(((f32[4,64,416]{2,1,0:T(8,128)}), f32[4,64,416]{2,1,0:T(8,128)S(1)}, u32[]{:S(2)}, u32[]{:S(2)}) %all-to-all-start.2) | async-done | bytes 426016 | tf_op jit(solution)/shard_map/all_to_all | solution.py:71
  81.1 0.1 copy.70
  81.2 0.8 reshape.100
  82.0 6.3 %all-to-all-start.3 = ((f32[16,1,2048]{2,1,0:T(1,128)}), f32[16,1,2048]{2,1,0:T(1,128)S(1)}, u32[]{:S(2)}, u32[]{:S(2)}) async-start(f32[16,1,2048]{2,1,0:T(1,128)} %reshape.100), calls=%async_computation.3 | async-start | bytes 262144 | tf_op jit(solution)/shard_map/all_to_all | solution.py:76
  88.3 0.2 fusion.4
  88.6 0.8 reshape.98.lim_ref
  89.3 0.2 concatenate.19
  89.6 0.1 pad.4.clone
  89.7 1.7 copy.69
  91.3 1.6 all-to-all-done.3
  93.0 0.5 broadcast.43
  93.5 0.9 reduce.3
  94.4 0.1 reshape.101
  94.5 0.8 copy.71.out_ref
  95.3 19.6 %shard_map.112 = (f32[64,384,128]{2,1,0:T(8,128)}, f32[64,512]{1,0:T(8,128)}) custom-call(f32[8,384,8]{2,1,0:T(8,128)} %bitcast.45, f32[64,512]{1,0:T(8,128)} %copy.71.out_ref, f32[384,512]{1,0:T(8,128)} %broadcast_multiply_fusion.lodf_ref, f32[384,1]{1,0:T(8,128)} %reshape.98.lim_ref), custom_call_target="tpu_custom_call" | custom-call | tf_op jit(solution)/shard_map/pallas_call | solution.py:47
  114.9 0.9 broadcast_multiply_fusion.3
  115.8 0.1 copy.73
  116.0 0.9 maximum_bitcast_fusion
  116.8 5.5 %all-to-all-start.4 = ((f32[16,72,32]{1,2,0:T(8,128)}), f32[16,72,32]{1,2,0:T(8,128)S(1)}, u32[]{:S(2)}, u32[]{:S(2)}) async-start(f32[16,72,32]{1,2,0:T(8,128)} %maximum_bitcast_fusion), calls=%async_computation.4 | async-start | bytes 524288 | tf_op jit(solution)/shard_map/all_to_all | solution.py:141
  122.3 7.9 %reduce_sum.87 = f32[64,384]{1,0:T(8,128)S(1)} reduce(f32[64,384,128]{2,1,0:T(8,128)} %get-tuple-element.5, f32[]{:T(128)} %constant.39.clone.1), dimensions={2}, to_apply=%region_3.4 | reduce | flops 3121152 | bytes 12681220 | tf_op jit(solution)/shard_map/reduce_sum | solution.py:65
  130.3 0.8 reshape.102
  131.1 5.8 %all-to-all-start.5 = ((f32[16,1,2048]{2,1,0:T(1,128)}), f32[16,1,2048]{2,1,0:T(1,128)S(1)}, u32[]{:S(2)}, u32[]{:S(2)}) async-start(f32[16,1,2048]{2,1,0:T(1,128)} %reshape.102), calls=%async_computation.5 | async-start | bytes 262144 | tf_op jit(solution)/shard_map/all_to_all | solution.py:76
  136.8 0.2 fusion.10
  137.0 0.1 copy.85
  137.1 4.4 %all-to-all-done.5 = f32[16,1,2048]{2,1,0:T(1,128)S(1)} async-done(((f32[16,1,2048]{2,1,0:T(1,128)}), f32[16,1,2048]{2,1,0:T(1,128)S(1)}, u32[]{:S(2)}, u32[]{:S(2)}) %all-to-all-start.5) | async-done | bytes 131104 | tf_op jit(solution)/shard_map/all_to_all | solution.py:76
  141.5 0.9 reduce.4
  142.4 0.1 reshape.103
  142.6 0.5 fusion
  143.1 12.4 %all_to_all.56 = bf16[4,64,416]{2,1,0:T(8,128)(2,1)S(1)} all-to-all(bf16[4,64,416]{2,1,0:T(8,128)(2,1)S(1)} %broadcast_in_dim.105), channel_id=1, replica_groups=mesh['y'=4,'zh'=4,'zl'=2,'x'=4,'core'=2] {'zh'}, dimensions={0} | all-to-all | bytes 425984 | tf_op jit(solution)/shard_map/all_to_all | solution.py:83
  155.6 0.1 copy.77
  155.7 0.1 broadcast_in_dim.107
  155.8 14.1 %all_to_all.57 = bf16[4,256,416]{1,2,0:T(8,128)(2,1)} all-to-all(bf16[4,256,416]{1,2,0:T(8,128)(2,1)S(1)} %broadcast_in_dim.107), channel_id=1, replica_groups=mesh['y'=4,'zh'=4,'zl'=2,'x'=4,'core'=2] {'y'}, dimensions={0} | all-to-all | bytes 1703936 | tf_op jit(solution)/shard_map/all_to_all | solution.py:83
  169.9 1.4 copy.78
  171.4 0.1 copy.79
  171.5 1.0 copy-done.1
  172.5 1.2 fusion.2
  173.8 10.7 %all_to_all.58 = f32[2,512,1024]{2,1,0:T(8,128)} all-to-all(f32[2,512,1024]{2,1,0:T(8,128)S(1)} %fusion.2), channel_id=1, replica_groups=mesh['y'=4,'zh'=4,'zl'=2,'x'=4,'core'=2] {'core'}, dimensions={0} | all-to-all | bytes 8388608 | tf_op jit(solution)/shard_map/all_to_all | solution.py:71
  184.5 4.1 %reduce_sum.90 = f32[512,1024]{1,0:T(8,128)} reduce(f32[2,512,1024]{2,1,0:T(8,128)} %all_to_all.58, f32[]{:T(128)} %constant.39.clone.1), dimensions={0}, to_apply=%region_6.7 | reduce | flops 524288 | bytes 6291460 | tf_op jit(solution)/shard_map/reduce_sum | solution.py:71
  188.6 30.2 %all_to_all.59 = f32[2,256,1024]{2,1,0:T(8,128)} all-to-all(f32[2,256,1024]{2,1,0:T(8,128)} %bitcast.43), channel_id=1, replica_groups=mesh['y'=4,'zh'=4,'zl'=2,'x'=4,'core'=2] {'zl'}, dimensions={0} | all-to-all | bytes 4194304 | tf_op jit(solution)/shard_map/all_to_all | solution.py:71
  218.8 2.8 %reduce_sum.91 = f32[256,1024]{1,0:T(8,128)} reduce(f32[2,256,1024]{2,1,0:T(8,128)} %all_to_all.59, f32[]{:T(128)} %constant.39.clone.1), dimensions={0}, to_apply=%region_7.8 | reduce | flops 262144 | bytes 3145732 | tf_op jit(solution)/shard_map/reduce_sum | solution.py:71
  221.7 4.6 %all-to-all-start.10 = ((f32[4,64,1024]{2,1,0:T(8,128)}), f32[4,64,1024]{2,1,0:T(8,128)S(1)}, u32[]{:S(2)}, u32[]{:S(2)}) async-start(f32[4,64,1024]{2,1,0:T(8,128)} %bitcast.47), calls=%async_computation.10 | async-start | bytes 2097152 | tf_op jit(solution)/shard_map/all_to_all | solution.py:71
  226.2 0.8 copy.82
  227.0 11.4 %all-to-all-done.10 = f32[4,64,1024]{2,1,0:T(8,128)S(1)} async-done(((f32[4,64,1024]{2,1,0:T(8,128)}), f32[4,64,1024]{2,1,0:T(8,128)S(1)}, u32[]{:S(2)}, u32[]{:S(2)}) %all-to-all-start.10) | async-done | bytes 1048608 | tf_op jit(solution)/shard_map/all_to_all | solution.py:71
  238.4 0.1 reduce_sum.92
  238.5 1.6 add_convert_fusion
  (32 shorter events, 0.3 us)
Async XLA Ops:
  0.6 1.6 copy-start
  4.3 7.7 %copy-start.4 = (s32[384]{0:T(512)S(1)}, s32[384]{0:T(512)}, u32[]{:S(2)}) copy-start(s32[384]{0:T(512)} %param.15) | copy-start | bytes 4612
  5.5 21.4 %all-to-all-start = ((bf16[16,32,1024]{2,1,0:T(8,128)(2,1)}), bf16[16,32,1024]{2,1,0:T(8,128)(2,1)S(1)}, u32[]{:S(2)}, u32[]{:S(2)}) async-start(bf16[16,32,1024]{2,1,0:T(8,128)(2,1)} %select_select_fusion), calls=%async_computation | async-start | bytes 2097152 | tf_op jit(solution)/shard_map/all_to_all | solution.py:71
  12.0 4.9 %copy-start.3 = (f32[24,1024]{1,0:T(8,128)S(1)}, f32[24,1024]{1,0:T(8,128)}, u32[]{:S(2)}) copy-start(f32[24,1024]{1,0:T(8,128)} %param.10) | copy-start | bytes 294916
  12.0 4.9 %copy-start.6 = (s32[1024]{0:T(1024)S(1)}, s32[1024]{0:T(1024)}, u32[]{:S(2)}) copy-start(s32[1024]{0:T(1024)} %param.11) | copy-start | bytes 12292
  56.0 10.1 %copy-start.8 = (f32[384]{0:T(512)S(1)}, f32[384]{0:T(512)}, u32[]{:S(2)}) copy-start(f32[384]{0:T(512)} %param.14) | copy-start | bytes 4612
  56.0 10.1 %copy-start.2 = (f32[384,512]{1,0:T(8,128)S(1)}, f32[384,512]{1,0:T(8,128)}, u32[]{:S(2)}) copy-start(f32[384,512]{1,0:T(8,128)} %param.13) | copy-start | bytes 2359300
  58.7 29.6 %copy-start.5 = (s32[512]{0:T(512)S(1)}, s32[512]{0:T(512)}, u32[]{:S(2)}) copy-start(s32[512]{0:T(512)} %param.16) | copy-start | bytes 6148
  58.7 22.3 %all-to-all-start.2 = ((f32[4,64,416]{2,1,0:T(8,128)}), f32[4,64,416]{2,1,0:T(8,128)S(1)}, u32[]{:S(2)}, u32[]{:S(2)}) async-start(f32[4,64,416]{2,1,0:T(8,128)} %bitcast.1), calls=%async_computation.2 | async-start | bytes 1048576 | tf_op jit(solution)/shard_map/all_to_all | solution.py:71
  82.0 11.0 %all-to-all-start.3 = ((f32[16,1,2048]{2,1,0:T(1,128)}), f32[16,1,2048]{2,1,0:T(1,128)S(1)}, u32[]{:S(2)}, u32[]{:S(2)}) async-start(f32[16,1,2048]{2,1,0:T(1,128)} %reshape.100), calls=%async_computation.3 | async-start | bytes 262144 | tf_op jit(solution)/shard_map/all_to_all | solution.py:76
  116.8 13.4 %all-to-all-start.4 = ((f32[16,72,32]{1,2,0:T(8,128)}), f32[16,72,32]{1,2,0:T(8,128)S(1)}, u32[]{:S(2)}, u32[]{:S(2)}) async-start(f32[16,72,32]{1,2,0:T(8,128)} %maximum_bitcast_fusion), calls=%async_computation.4 | async-start | bytes 524288 | tf_op jit(solution)/shard_map/all_to_all | solution.py:141
  131.1 10.4 %all-to-all-start.5 = ((f32[16,1,2048]{2,1,0:T(1,128)}), f32[16,1,2048]{2,1,0:T(1,128)S(1)}, u32[]{:S(2)}, u32[]{:S(2)}) async-start(f32[16,1,2048]{2,1,0:T(1,128)} %reshape.102), calls=%async_computation.5 | async-start | bytes 262144 | tf_op jit(solution)/shard_map/all_to_all | solution.py:76
  171.4 1.1 copy-start.1
  221.7 16.8 %copy-start.7 = (f32[1024]{0:T(1024)S(1)}, f32[1024]{0:T(1024)}, u32[]{:S(2)}) copy-start(f32[1024]{0:T(1024)} %param.17) | copy-start | bytes 12292
  221.7 16.7 %all-to-all-start.10 = ((f32[4,64,1024]{2,1,0:T(8,128)}), f32[4,64,1024]{2,1,0:T(8,128)S(1)}, u32[]{:S(2)}, u32[]{:S(2)}) async-start(f32[4,64,1024]{2,1,0:T(8,128)} %bitcast.47), calls=%async_computation.10 | async-start | bytes 2097152 | tf_op jit(solution)/shard_map/all_to_all | solution.py:71

commit v12 on v7

--- a/solution.py
+++ b/solution.py
@@ -62,7 +62,11 @@
             jax.ShapeDtypeStruct((scen_rows, outage_total), jnp.float32),
         ],
     )(base3, outflow, lodf2, lim2)
-    direct = jnp.sum(direct_lanes, axis=2) / (2.0 * outage_total)
+    lane_ones = jnp.ones((lanes, 1), jnp.float32)
+    direct = jnp.dot(
+        direct_lanes.reshape(scen_rows * monitor_count, lanes), lane_ones,
+        precision=lax.Precision.HIGHEST,
+    ).reshape(scen_rows, monitor_count) / (2.0 * outage_total)
     return direct, sens / (2.0 * half)
 
 

time: 237 us -> 243 us (1.025)
  matrix products: 9.46 us -> 23 us
  other arithmetic: 27.5 us -> 19.6 us
    dot_general x0 -> x1, matrix products: none -> 13.5 us  [penalty_slopes(): jnp.dot(direct_lanes.reshape(scen_rows * monitor_count, lanes), lane_ones...]
    reduce_sum x1 -> x0, other arithmetic: 7.89 us -> none  [penalty_slopes(): direct = jnp.sum(direct_lanes, axis=2) / (2.0 * outage_total)]
  transfers between devices with their start and end apart: 6 -> 6, of which waited for: 5 -> 5; matrix products, arithmetic and copies ran while one was open for 10% -> 12% of each run, Pallas kernels for 0% -> 0%
where the time goes in v12:
time: 243 us; the launch traced here: 238 us
  blocking collectives  92.8 us (38%)
  starting transfers between devices  34.9 us (14%)
  waiting for transfers between devices  31.1 us (13%)
  matrix products  23 us (9%)
  other arithmetic  19.6 us (8%)
  Pallas kernels  19.6 us (8%)
  local copies, waits for them, and re-layouts  16.4 us (7%)
    all_to_all x3, blocking collectives, exchange_sum(): return jnp.sum(lax.all_to_all(blocks, axis, 0, 0, tiled=False), axis=0)  66.2 us
    all_to_all x2, blocking collectives, gather_rows(): gathered = lax.all_to_all(copies, axis, 0, 0, tiled=False)  26.6 us
    all_to_all x3, waiting for transfers between devices, exchange_sum(): return jnp.sum(lax.all_to_all(blocks, axis, 0, 0, tiled=False), axis=0)  25.2 us
    pallas_call x1, Pallas kernels, penalty_slopes(): pl.pallas_call(kernel, grid=(blocks,), in_specs=[pl.BlockSpec((None, moni...  19.6 us
    all_to_all x3, starting transfers between devices, exchange_sum(): return jnp.sum(lax.all_to_all(blocks, axis, 0, 0, tiled=False), axis=0)  17.3 us
    dot_general x1, matrix products, penalty_slopes(): jnp.dot(direct_lanes.reshape(scen_rows * monitor_count, lanes), lane_ones...  13.5 us
    all_to_all x2, starting transfers between devices, gather_columns(): gathered = lax.all_to_all(copies, axis, 0, 0, tiled=False)  12.1 us
    reduce_sum x6, other arithmetic, exchange_sum(): return jnp.sum(lax.all_to_all(blocks, axis, 0, 0, tiled=False), axis=0)  8.66 us
  transfers between devices with their start and end apart: 6, of which 5 were waited for; matrix products, arithmetic and copies ran while one was open for 12% of the time, Pallas kernels for 0%

profile of v12, /device:TPU:7, one launch (start us, length us, event | category | flops | bytes accessed | tf_op | source)
XLA Modules:
  0.0 238.5 jit_solution(12904563393724109295)
XLA Ops:
  0.6 0.0 copy-start
  0.7 0.8 compare_and_fusion
  1.5 0.1 broadcast_in_dim.95
  1.6 0.1 broadcast_in_dim.97
  1.7 0.6 copy-done
  2.2 2.0 gather_fusion.1
  4.3 1.2 select_select_fusion
  5.5 6.4 %all-to-all-start = ((bf16[16,32,1024]{2,1,0:T(8,128)(2,1)}), bf16[16,32,1024]{2,1,0:T(8,128)(2,1)S(1)}, u32[]{:S(2)}, u32[]{:S(2)}) async-start(bf16[16,32,1024]{2,1,0:T(8,128)(2,1)} %select_select_fusion), calls=%async_computation | async-start | bytes 2097152 | tf_op jit(solution)/shard_map/all_to_all | solution.py:75
  12.0 2.7 %gather_fusion = bf16[384,1024]{1,0:T(8,128)(2,1)} fusion(bf16[1024,1024]{1,0:T(8,128)(2,1)S(1)} %copy-done, s32[1024]{0:T(1024)S(1)} %pad_clamp_fusion.1), kind=kCustom, calls=%fused_computation | custom fusion | bytes 1574400 | tf_op jit(solution)/shard_map/jit(_take)/gather | solution.py:124
  14.7 2.2 broadcast_select_fusion
  16.9 4.9 %subtract_convert_fusion = bf16[1024,1024]{1,0:T(8,128)(2,1)} fusion(bf16[1024,1024]{1,0:T(8,128)(2,1)} %param.9, f32[24,1024]{1,0:T(8,128)S(1)} %copy-done.3, s32[1024]{0:T(1024)S(1)} %copy-done.6), kind=kOutput, calls=%fused_computation.2 | convolution fusion | flops 305160192 | bytes 4296704 | tf_op jit(solution)/shard_map/dot_general | solution.py:106
  21.7 5.2 %all-to-all-done = bf16[16,32,1024]{2,1,0:T(8,128)(2,1)S(1)} async-done(((bf16[16,32,1024]{2,1,0:T(8,128)(2,1)}), bf16[16,32,1024]{2,1,0:T(8,128)(2,1)S(1)}, u32[]{:S(2)}, u32[]{:S(2)}) %all-to-all-start) | async-done | bytes 1048608 | tf_op jit(solution)/shard_map/all_to_all | solution.py:75
  26.9 0.2 reduce_sum.75
  27.1 2.8 %fusion.5 = f32[1024,416]{0,1:T(8,128)S(1)} fusion(bf16[1024,1024]{1,0:T(8,128)(2,1)} %subtract_convert_fusion, bf16[32,1024]{1,0:T(8,128)(2,1)S(1)} %reduce_sum.75, bf16[384,1024]{1,0:T(8,128)(2,1)} %broadcast_select_fusion), kind=kOutput, calls=%fused_computation.14 | convolution fusion | flops 874119168 | bytes 4653056 | tf_op jit(solution)/shard_map/dot_general | solution.py:127
  29.9 0.2 copy.90
  30.1 25.9 %all_to_all.55 = f32[4,256,416]{1,2,0:T(8,128)} all-to-all(f32[4,256,416]{1,2,0:T(8,128)S(1)} %bitcast.49), channel_id=1, replica_groups=mesh['y'=4,'zh'=4,'zl'=2,'x'=4,'core'=2] {'y'}, dimensions={0} | all-to-all | bytes 3407872 | tf_op jit(solution)/shard_map/all_to_all | solution.py:75
  56.0 1.7 reduce_sum.76
  57.7 1.0 copy.68
  58.7 7.4 %all-to-all-start.2 = ((f32[4,64,416]{2,1,0:T(8,128)}), f32[4,64,416]{2,1,0:T(8,128)S(1)}, u32[]{:S(2)}, u32[]{:S(2)}) async-start(f32[4,64,416]{2,1,0:T(8,128)} %bitcast.1), calls=%async_computation.2 | async-start | bytes 1048576 | tf_op jit(solution)/shard_map/all_to_all | solution.py:75
  66.1 0.9 broadcast_multiply_fusion.lodf_ref
  67.1 13.9 %all-to-all-done.2 = f32[4,64,416]{2,1,0:T(8,128)S(1)} async-done(((f32[4,64,416]{2,1,0:T(8,128)}), f32[4,64,416]{2,1,0:T(8,128)S(1)}, u32[]{:S(2)}, u32[]{:S(2)}) %all-to-all-start.2) | async-done | bytes 426016 | tf_op jit(solution)/shard_map/all_to_all | solution.py:75
  81.1 0.1 copy.70
  81.2 0.8 reshape.109
  82.0 6.3 %all-to-all-start.3 = ((f32[16,1,2048]{2,1,0:T(1,128)}), f32[16,1,2048]{2,1,0:T(1,128)S(1)}, u32[]{:S(2)}, u32[]{:S(2)}) async-start(f32[16,1,2048]{2,1,0:T(1,128)} %reshape.109), calls=%async_computation.3 | async-start | bytes 262144 | tf_op jit(solution)/shard_map/all_to_all | solution.py:80
  88.3 0.2 fusion.4
  88.6 0.8 reshape.107.lim_ref
  89.3 0.2 concatenate.19
  89.6 0.1 pad.4.clone
  89.7 1.7 copy.69
  91.3 1.6 all-to-all-done.3
  93.0 0.5 broadcast.48
  93.5 0.9 reduce.3
  94.4 0.1 reshape.110
  94.5 0.8 copy.71.out_ref
  95.3 19.6 %shard_map.112 = (f32[64,384,128]{2,1,0:T(8,128)}, f32[64,512]{1,0:T(8,128)}) custom-call(f32[8,384,8]{2,1,0:T(8,128)} %bitcast.50, f32[64,512]{1,0:T(8,128)} %copy.71.out_ref, f32[384,512]{1,0:T(8,128)} %broadcast_multiply_fusion.lodf_ref, f32[384,1]{1,0:T(8,128)} %reshape.107.lim_ref), custom_call_target="tpu_custom_call" | custom-call | tf_op jit(solution)/shard_map/pallas_call | solution.py:47
  114.9 0.9 broadcast_multiply_fusion.3
  115.8 0.1 copy.73
  116.0 0.9 maximum_bitcast_fusion
  116.8 5.5 %all-to-all-start.4 = ((f32[16,72,32]{1,2,0:T(8,128)}), f32[16,72,32]{1,2,0:T(8,128)S(1)}, u32[]{:S(2)}, u32[]{:S(2)}) async-start(f32[16,72,32]{1,2,0:T(8,128)} %maximum_bitcast_fusion), calls=%async_computation.4 | async-start | bytes 524288 | tf_op jit(solution)/shard_map/all_to_all | solution.py:145
  122.3 13.5 %fusion.11 = f32[1,64,384]{2,0,1:T(1,128)S(1)} fusion(f32[64,384,128]{2,1,0:T(8,128)} %get-tuple-element.5), kind=kOutput, calls=%fused_computation.40 | convolution fusion | flops 37748736 | bytes 12681216 | tf_op jit(solution)/shard_map/dot_general | solution.py:66
  135.9 0.8 reshape.111
  136.7 5.8 %all-to-all-start.5 = ((f32[16,1,2048]{2,1,0:T(1,128)}), f32[16,1,2048]{2,1,0:T(1,128)S(1)}, u32[]{:S(2)}, u32[]{:S(2)}) async-start(f32[16,1,2048]{2,1,0:T(1,128)} %reshape.111), calls=%async_computation.5 | async-start | bytes 262144 | tf_op jit(solution)/shard_map/all_to_all | solution.py:80
  142.5 0.2 fusion.10
  142.7 0.1 copy.86
  142.8 4.4 %all-to-all-done.5 = f32[16,1,2048]{2,1,0:T(1,128)S(1)} async-done(((f32[16,1,2048]{2,1,0:T(1,128)}), f32[16,1,2048]{2,1,0:T(1,128)S(1)}, u32[]{:S(2)}, u32[]{:S(2)}) %all-to-all-start.5) | async-done | bytes 131104 | tf_op jit(solution)/shard_map/all_to_all | solution.py:80
  147.1 0.9 reduce.4
  148.1 0.1 reshape.112
  148.2 0.5 fusion
  148.8 12.4 %all_to_all.56 = bf16[4,64,416]{2,1,0:T(8,128)(2,1)S(1)} all-to-all(bf16[4,64,416]{2,1,0:T(8,128)(2,1)S(1)} %broadcast_in_dim.109), channel_id=1, replica_groups=mesh['y'=4,'zh'=4,'zl'=2,'x'=4,'core'=2] {'zh'}, dimensions={0} | all-to-all | bytes 425984 | tf_op jit(solution)/shard_map/all_to_all | solution.py:87
  161.2 0.1 copy.77
  161.4 0.1 broadcast_in_dim.111
  161.4 14.1 %all_to_all.57 = bf16[4,256,416]{1,2,0:T(8,128)(2,1)} all-to-all(bf16[4,256,416]{1,2,0:T(8,128)(2,1)S(1)} %broadcast_in_dim.111), channel_id=1, replica_groups=mesh['y'=4,'zh'=4,'zl'=2,'x'=4,'core'=2] {'y'}, dimensions={0} | all-to-all | bytes 1703936 | tf_op jit(solution)/shard_map/all_to_all | solution.py:87
  175.6 1.4 copy.78
  177.1 0.1 copy.79
  177.1 1.0 copy-done.1
  178.2 1.2 fusion.2
  179.4 10.7 %all_to_all.58 = f32[2,512,1024]{2,1,0:T(8,128)} all-to-all(f32[2,512,1024]{2,1,0:T(8,128)S(1)} %fusion.2), channel_id=1, replica_groups=mesh['y'=4,'zh'=4,'zl'=2,'x'=4,'core'=2] {'core'}, dimensions={0} | all-to-all | bytes 8388608 | tf_op jit(solution)/shard_map/all_to_all | solution.py:75
  190.1 4.1 %reduce_sum.80 = f32[512,1024]{1,0:T(8,128)} reduce(f32[2,512,1024]{2,1,0:T(8,128)} %all_to_all.58, f32[]{:T(128)} %constant.39.clone.1), dimensions={0}, to_apply=%region_5.6 | reduce | flops 524288 | bytes 6291460 | tf_op jit(solution)/shard_map/reduce_sum | solution.py:75
  194.3 29.6 %all_to_all.59 = f32[4,128,1024]{2,1,0:T(8,128)} all-to-all(f32[4,128,1024]{2,1,0:T(8,128)} %bitcast.48), channel_id=1, replica_groups=mesh['y'=4,'zh'=4,'zl'=2,'x'=4,'core'=2] {'x'}, dimensions={0} | all-to-all | bytes 4194304 | tf_op jit(solution)/shard_map/all_to_all | solution.py:75
  223.9 2.6 %reduce_sum.81 = f32[128,1024]{1,0:T(8,128)} reduce(f32[4,128,1024]{2,1,0:T(8,128)} %all_to_all.59, f32[]{:T(128)} %constant.39.clone.1), dimensions={0}, to_apply=%region_6.7 | reduce | flops 393216 | bytes 2621444 | tf_op jit(solution)/shard_map/reduce_sum | solution.py:75
  226.5 3.5 %all-to-all-start.10 = ((f32[2,64,1024]{2,1,0:T(8,128)}), f32[2,64,1024]{2,1,0:T(8,128)S(1)}, u32[]{:S(2)}, u32[]{:S(2)}) async-start(f32[2,64,1024]{2,1,0:T(8,128)} %bitcast.17), calls=%async_computation.10 | async-start | bytes 1048576 | tf_op jit(solution)/shard_map/all_to_all | solution.py:75
  230.0 0.8 copy.82
  230.8 6.1 %all-to-all-done.10 = f32[2,64,1024]{2,1,0:T(8,128)S(1)} async-done(((f32[2,64,1024]{2,1,0:T(8,128)}), f32[2,64,1024]{2,1,0:T(8,128)S(1)}, u32[]{:S(2)}, u32[]{:S(2)}) %all-to-all-start.10) | async-done | bytes 524320 | tf_op jit(solution)/shard_map/all_to_all | solution.py:75
  236.9 1.6 add_convert_fusion
  (32 shorter events, 0.3 us)
Async XLA Ops:
  0.6 1.6 copy-start
  4.3 7.7 %copy-start.4 = (s32[384]{0:T(512)S(1)}, s32[384]{0:T(512)}, u32[]{:S(2)}) copy-start(s32[384]{0:T(512)} %param.15) | copy-start | bytes 4612
  5.5 21.4 %all-to-all-start = ((bf16[16,32,1024]{2,1,0:T(8,128)(2,1)}), bf16[16,32,1024]{2,1,0:T(8,128)(2,1)S(1)}, u32[]{:S(2)}, u32[]{:S(2)}) async-start(bf16[16,32,1024]{2,1,0:T(8,128)(2,1)} %select_select_fusion), calls=%async_computation | async-start | bytes 2097152 | tf_op jit(solution)/shard_map/all_to_all | solution.py:75
  12.0 4.9 %copy-start.3 = (f32[24,1024]{1,0:T(8,128)S(1)}, f32[24,1024]{1,0:T(8,128)}, u32[]{:S(2)}) copy-start(f32[24,1024]{1,0:T(8,128)} %param.10) | copy-start | bytes 294916
  12.0 4.9 %copy-start.6 = (s32[1024]{0:T(1024)S(1)}, s32[1024]{0:T(1024)}, u32[]{:S(2)}) copy-start(s32[1024]{0:T(1024)} %param.11) | copy-start | bytes 12292
  56.0 10.1 %copy-start.8 = (f32[384]{0:T(512)S(1)}, f32[384]{0:T(512)}, u32[]{:S(2)}) copy-start(f32[384]{0:T(512)} %param.14) | copy-start | bytes 4612
  56.0 10.1 %copy-start.2 = (f32[384,512]{1,0:T(8,128)S(1)}, f32[384,512]{1,0:T(8,128)}, u32[]{:S(2)}) copy-start(f32[384,512]{1,0:T(8,128)} %param.13) | copy-start | bytes 2359300
  58.7 29.6 %copy-start.5 = (s32[512]{0:T(512)S(1)}, s32[512]{0:T(512)}, u32[]{:S(2)}) copy-start(s32[512]{0:T(512)} %param.16) | copy-start | bytes 6148
  58.7 22.3 %all-to-all-start.2 = ((f32[4,64,416]{2,1,0:T(8,128)}), f32[4,64,416]{2,1,0:T(8,128)S(1)}, u32[]{:S(2)}, u32[]{:S(2)}) async-start(f32[4,64,416]{2,1,0:T(8,128)} %bitcast.1), calls=%async_computation.2 | async-start | bytes 1048576 | tf_op jit(solution)/shard_map/all_to_all | solution.py:75
  82.0 11.0 %all-to-all-start.3 = ((f32[16,1,2048]{2,1,0:T(1,128)}), f32[16,1,2048]{2,1,0:T(1,128)S(1)}, u32[]{:S(2)}, u32[]{:S(2)}) async-start(f32[16,1,2048]{2,1,0:T(1,128)} %reshape.109), calls=%async_computation.3 | async-start | bytes 262144 | tf_op jit(solution)/shard_map/all_to_all | solution.py:80
  116.8 19.0 %all-to-all-start.4 = ((f32[16,72,32]{1,2,0:T(8,128)}), f32[16,72,32]{1,2,0:T(8,128)S(1)}, u32[]{:S(2)}, u32[]{:S(2)}) async-start(f32[16,72,32]{1,2,0:T(8,128)} %maximum_bitcast_fusion), calls=%async_computation.4 | async-start | bytes 524288 | tf_op jit(solution)/shard_map/all_to_all | solution.py:145
  136.7 10.4 %all-to-all-start.5 = ((f32[16,1,2048]{2,1,0:T(1,128)}), f32[16,1,2048]{2,1,0:T(1,128)S(1)}, u32[]{:S(2)}, u32[]{:S(2)}) async-start(f32[16,1,2048]{2,1,0:T(1,128)} %reshape.111), calls=%async_computation.5 | async-start | bytes 262144 | tf_op jit(solution)/shard_map/all_to_all | solution.py:80
  177.0 1.1 copy-start.1
  223.9 13.0 %copy-start.7 = (f32[1024]{0:T(1024)S(1)}, f32[1024]{0:T(1024)}, u32[]{:S(2)}) copy-start(f32[1024]{0:T(1024)} %param.17) | copy-start | bytes 12292
  226.5 10.3 %all-to-all-start.10 = ((f32[2,64,1024]{2,1,0:T(8,128)}), f32[2,64,1024]{2,1,0:T(8,128)S(1)}, u32[]{:S(2)}, u32[]{:S(2)}) async-start(f32[2,64,1024]{2,1,0:T(8,128)} %bitcast.17), calls=%async_computation.10 | async-start | bytes 1048576 | tf_op jit(solution)/shard_map/all_to_all | solution.py:75

commit v13 on v7

--- a/solution.py
+++ b/solution.py
@@ -116,7 +116,14 @@
         jnp.take(ptdf, jnp.clip(rel_outages, 0, line_rows - 1), axis=0),
         jnp.zeros((), ptdf.dtype),
     )
-    my_outage_rows = exchange_sum(outage_rows, LINE, line_count)
+    staged_order = [lax.axis_size(name) for name in LINE]
+    my_outage_rows = (
+        outage_rows.reshape(staged_order + [outage_total // line_count, line_rows])
+        .transpose(2, 1, 0, 3, 4)
+        .reshape(outage_rows.shape)
+    )
+    for name in LINE[::-1]:
+        my_outage_rows = exchange_sum(my_outage_rows, name, lax.axis_size(name))
     monitored_rows = jnp.take(ptdf, local_monitored, axis=0)
     rows = jnp.concatenate([monitored_rows, my_outage_rows], axis=0)
 

time: 237 us -> 239 us (level)
  starting transfers between devices: 34.9 us -> 43 us
  waiting for transfers between devices: 31.1 us -> 23.2 us
    all_to_all x3 -> x4, waiting for transfers between devices: 25.2 us -> 17.1 us  [exchange_sum(): return jnp.sum(lax.all_to_all(blocks, axis, 0, 0, tiled=False), axis=0)]
    all_to_all x2, starting transfers between devices: 12.1 us -> 17.2 us  [gather_columns(): gathered = lax.all_to_all(copies, axis, 0, 0, tiled=False)]
    all_to_all x3 -> x4, starting transfers between devices: 17.3 us -> 20.3 us  [exchange_sum(): return jnp.sum(lax.all_to_all(blocks, axis, 0, 0, tiled=False), axis=0)]
    all_to_all x3 -> x4, blocking collectives: 66.3 us -> 68.1 us  [exchange_sum(): return jnp.sum(lax.all_to_all(blocks, axis, 0, 0, tiled=False), axis=0)]
    reduce_sum x6 -> x8, other arithmetic: 8.66 us -> 10.4 us  [exchange_sum(): return jnp.sum(lax.all_to_all(blocks, axis, 0, 0, tiled=False), axis=0)]
  transfers between devices with their start and end apart: 6 -> 7, of which waited for: 5 -> 5; matrix products, arithmetic and copies ran while one was open for 10% -> 9% of each run, Pallas kernels for 0% -> 0%
where the time goes in v13:
time: 239 us; the launch traced here: 235 us
  blocking collectives  95 us (40%)
  starting transfers between devices  43 us (18%)
  other arithmetic  27.4 us (11%)
  waiting for transfers between devices  23.2 us (10%)
  Pallas kernels  19.6 us (8%)
  local copies, waits for them, and re-layouts  16.4 us (7%)
  matrix products  9.28 us (4%)
    all_to_all x4, blocking collectives, exchange_sum(): return jnp.sum(lax.all_to_all(blocks, axis, 0, 0, tiled=False), axis=0)  68.1 us
    all_to_all x2, blocking collectives, gather_rows(): gathered = lax.all_to_all(copies, axis, 0, 0, tiled=False)  26.9 us
    all_to_all x4, starting transfers between devices, exchange_sum(): return jnp.sum(lax.all_to_all(blocks, axis, 0, 0, tiled=False), axis=0)  20.3 us
    pallas_call x1, Pallas kernels, penalty_slopes(): pl.pallas_call(kernel, grid=(blocks,), in_specs=[pl.BlockSpec((None, moni...  19.6 us
    all_to_all x2, starting transfers between devices, gather_columns(): gathered = lax.all_to_all(copies, axis, 0, 0, tiled=False)  17.2 us
    all_to_all x4, waiting for transfers between devices, exchange_sum(): return jnp.sum(lax.all_to_all(blocks, axis, 0, 0, tiled=False), axis=0)  17.1 us
    reduce_sum x8, other arithmetic, exchange_sum(): return jnp.sum(lax.all_to_all(blocks, axis, 0, 0, tiled=False), axis=0)  10.4 us
    reduce_sum x1, other arithmetic, penalty_slopes(): direct = jnp.sum(direct_lanes, axis=2) / (2.0 * outage_total)  7.89 us
  transfers between devices with their start and end apart: 7, of which 5 were waited for; matrix products, arithmetic and copies ran while one was open for 9% of the time, Pallas kernels for 0%

profile of v13, /device:TPU:7, one launch (start us, length us, event | category | flops | bytes accessed | tf_op | source)
XLA Modules:
  0.0 234.9 jit_solution(12615127242144219589)
XLA Ops:
  0.7 0.8 compare_and_fusion
  1.5 0.1 broadcast_in_dim.92
  1.6 0.1 broadcast_in_dim.94
  1.7 0.5 copy-done
  2.2 2.0 gather_fusion.1
  4.3 0.2 fusion.1
  4.5 4.9 %all_to_all.65 = bf16[2,256,1024]{2,1,0:T(8,128)(2,1)S(1)} all-to-all(bf16[2,256,1024]{2,1,0:T(8,128)(2,1)S(1)} %bitcast.52), channel_id=1, replica_groups=mesh['y'=4,'zh'=4,'zl'=2,'x'=4,'core'=2] {'core'}, dimensions={0} | all-to-all | bytes 2097152 | tf_op jit(solution)/shard_map/all_to_all | solution.py:71
  9.4 1.2 reduce_sum.108
  10.6 5.3 %all-to-all-start.1 = ((bf16[4,64,1024]{2,1,0:T(8,128)(2,1)}), bf16[4,64,1024]{2,1,0:T(8,128)(2,1)S(1)}, u32[]{:S(2)}, u32[]{:S(2)}) async-start(bf16[4,64,1024]{2,1,0:T(8,128)(2,1)} %bitcast.55), calls=%async_computation.1 | async-start | bytes 1048576 | tf_op jit(solution)/shard_map/all_to_all | solution.py:71
  16.0 2.7 %gather_fusion = bf16[384,1024]{1,0:T(8,128)(2,1)} fusion(bf16[1024,1024]{1,0:T(8,128)(2,1)S(1)} %copy-done, s32[1024]{0:T(1024)S(1)} %pad_clamp_fusion.1), kind=kCustom, calls=%fused_computation | custom fusion | bytes 1574400 | tf_op jit(solution)/shard_map/jit(_take)/gather | solution.py:127
  18.7 4.9 %subtract_convert_fusion = bf16[1024,1024]{1,0:T(8,128)(2,1)} fusion(bf16[1024,1024]{1,0:T(8,128)(2,1)} %param.9, f32[24,1024]{1,0:T(8,128)S(1)} %copy-done.4, s32[1024]{0:T(1024)S(1)} %copy-done.7), kind=kOutput, calls=%fused_computation.2 | convolution fusion | flops 305160192 | bytes 4296704 | tf_op jit(solution)/shard_map/dot_general | solution.py:102
  23.5 0.7 reduce_sum.109
  24.3 3.4 %all-to-all-start.2 = ((bf16[2,32,1024]{2,1,0:T(8,128)(2,1)}), bf16[2,32,1024]{2,1,0:T(8,128)(2,1)S(1)}, u32[]{:S(2)}, u32[]{:S(2)}) async-start(bf16[2,32,1024]{2,1,0:T(8,128)(2,1)} %bitcast.4), calls=%async_computation.2 | async-start | bytes 262144 | tf_op jit(solution)/shard_map/all_to_all | solution.py:71
  27.7 1.3 broadcast_select_fusion
  29.0 2.0 all-to-all-done.2
  31.0 2.7 %fusion.6 = f32[1024,416]{0,1:T(8,128)S(1)} fusion(bf16[1024,1024]{1,0:T(8,128)(2,1)} %subtract_convert_fusion, bf16[32,1024]{1,0:T(8,128)(2,1)S(1)} %reduce_sum.110, bf16[384,1024]{1,0:T(8,128)(2,1)S(1)} %broadcast_select_fusion), kind=kOutput, calls=%fused_computation.15 | convolution fusion | flops 874119168 | bytes 4653056 | tf_op jit(solution)/shard_map/dot_general | solution.py:130
  33.7 0.2 copy.106
  33.8 22.9 %all_to_all.66 = f32[4,256,416]{1,2,0:T(8,128)} all-to-all(f32[4,256,416]{1,2,0:T(8,128)S(1)} %bitcast.49), channel_id=1, replica_groups=mesh['y'=4,'zh'=4,'zl'=2,'x'=4,'core'=2] {'y'}, dimensions={0} | all-to-all | bytes 3407872 | tf_op jit(solution)/shard_map/all_to_all | solution.py:71
  56.8 1.7 reduce_sum.111
  58.5 1.0 copy.83
  59.5 8.1 %all-to-all-start.4 = ((f32[4,64,416]{2,1,0:T(8,128)}), f32[4,64,416]{2,1,0:T(8,128)S(1)}, u32[]{:S(2)}, u32[]{:S(2)}) async-start(f32[4,64,416]{2,1,0:T(8,128)} %bitcast.5), calls=%async_computation.4 | async-start | bytes 1048576 | tf_op jit(solution)/shard_map/all_to_all | solution.py:71
  67.6 1.0 broadcast_multiply_fusion.lodf_ref
  68.5 9.1 %all-to-all-done.4 = f32[4,64,416]{2,1,0:T(8,128)S(1)} async-done(((f32[4,64,416]{2,1,0:T(8,128)}), f32[4,64,416]{2,1,0:T(8,128)S(1)}, u32[]{:S(2)}, u32[]{:S(2)}) %all-to-all-start.4) | async-done | bytes 426016 | tf_op jit(solution)/shard_map/all_to_all | solution.py:71
  77.7 0.8 reshape.108
  78.6 11.4 %all-to-all-start.5 = ((f32[16,1,2048]{2,1,0:T(1,128)}), f32[16,1,2048]{2,1,0:T(1,128)S(1)}, u32[]{:S(2)}, u32[]{:S(2)}) async-start(f32[16,1,2048]{2,1,0:T(1,128)} %reshape.108), calls=%async_computation.5 | async-start | bytes 262144 | tf_op jit(solution)/shard_map/all_to_all | solution.py:76
  90.0 0.2 fusion.5
  90.3 0.8 reshape.106.lim_ref
  91.1 0.2 concatenate.19
  91.3 0.1 pad.4.clone
  91.4 1.7 copy.84
  93.0 1.7 all-to-all-done.5
  94.7 0.5 broadcast.43
  95.2 0.9 reduce.5
  96.2 0.1 reshape.109
  96.3 0.8 copy.86.out_ref
  97.0 19.6 %shard_map.112 = (f32[64,384,128]{2,1,0:T(8,128)}, f32[64,512]{1,0:T(8,128)}) custom-call(f32[8,384,8]{2,1,0:T(8,128)} %bitcast.50, f32[64,512]{1,0:T(8,128)} %copy.86.out_ref, f32[384,512]{1,0:T(8,128)} %broadcast_multiply_fusion.lodf_ref, f32[384,1]{1,0:T(8,128)} %reshape.106.lim_ref), custom_call_target="tpu_custom_call" | custom-call | tf_op jit(solution)/shard_map/pallas_call | solution.py:47
  116.6 0.9 broadcast_multiply_fusion.3
  117.6 0.1 copy.88
  117.7 0.9 maximum_bitcast_fusion
  118.5 5.5 %all-to-all-start.6 = ((f32[16,72,32]{1,2,0:T(8,128)}), f32[16,72,32]{1,2,0:T(8,128)S(1)}, u32[]{:S(2)}, u32[]{:S(2)}) async-start(f32[16,72,32]{1,2,0:T(8,128)} %maximum_bitcast_fusion), calls=%async_computation.6 | async-start | bytes 524288 | tf_op jit(solution)/shard_map/all_to_all | solution.py:148
  124.1 7.9 %reduce_sum.113 = f32[64,384]{1,0:T(8,128)S(1)} reduce(f32[64,384,128]{2,1,0:T(8,128)} %get-tuple-element.5, f32[]{:T(128)} %constant.41.clone.1), dimensions={2}, to_apply=%region_5.6 | reduce | flops 3121152 | bytes 12681220 | tf_op jit(solution)/shard_map/reduce_sum | solution.py:65
  132.0 0.8 reshape.110
  132.9 5.8 %all-to-all-start.7 = ((f32[16,1,2048]{2,1,0:T(1,128)}), f32[16,1,2048]{2,1,0:T(1,128)S(1)}, u32[]{:S(2)}, u32[]{:S(2)}) async-start(f32[16,1,2048]{2,1,0:T(1,128)} %reshape.110), calls=%async_computation.7 | async-start | bytes 262144 | tf_op jit(solution)/shard_map/all_to_all | solution.py:76
  138.6 0.2 fusion.11
  138.8 0.1 copy.100
  138.9 4.4 %all-to-all-done.7 = f32[16,1,2048]{2,1,0:T(1,128)S(1)} async-done(((f32[16,1,2048]{2,1,0:T(1,128)}), f32[16,1,2048]{2,1,0:T(1,128)S(1)}, u32[]{:S(2)}, u32[]{:S(2)}) %all-to-all-start.7) | async-done | bytes 131104 | tf_op jit(solution)/shard_map/all_to_all | solution.py:76
  143.3 0.9 reduce.6
  144.2 0.1 reshape.111
  144.4 0.5 fusion
  144.9 12.7 %all_to_all.67 = bf16[4,64,416]{2,1,0:T(8,128)(2,1)S(1)} all-to-all(bf16[4,64,416]{2,1,0:T(8,128)(2,1)S(1)} %broadcast_in_dim.105), channel_id=1, replica_groups=mesh['y'=4,'zh'=4,'zl'=2,'x'=4,'core'=2] {'zh'}, dimensions={0} | all-to-all | bytes 425984 | tf_op jit(solution)/shard_map/all_to_all | solution.py:83
  157.6 0.1 copy.92
  157.8 14.1 %all_to_all.68 = bf16[4,256,416]{1,2,0:T(8,128)(2,1)} all-to-all(bf16[4,256,416]{1,2,0:T(8,128)(2,1)S(1)} %broadcast_in_dim.107), channel_id=1, replica_groups=mesh['y'=4,'zh'=4,'zl'=2,'x'=4,'core'=2] {'y'}, dimensions={0} | all-to-all | bytes 1703936 | tf_op jit(solution)/shard_map/all_to_all | solution.py:83
  172.0 1.4 copy.93
  173.4 0.1 copy.94
  173.5 1.0 copy-done.2
  174.6 1.2 fusion.3
  175.8 10.7 %all_to_all.69 = f32[2,512,1024]{2,1,0:T(8,128)} all-to-all(f32[2,512,1024]{2,1,0:T(8,128)S(1)} %fusion.3), channel_id=1, replica_groups=mesh['y'=4,'zh'=4,'zl'=2,'x'=4,'core'=2] {'core'}, dimensions={0} | all-to-all | bytes 8388608 | tf_op jit(solution)/shard_map/all_to_all | solution.py:71
  186.5 4.1 %reduce_sum.116 = f32[512,1024]{1,0:T(8,128)} reduce(f32[2,512,1024]{2,1,0:T(8,128)} %all_to_all.69, f32[]{:T(128)} %constant.41.clone.1), dimensions={0}, to_apply=%region_8.9 | reduce | flops 524288 | bytes 6291460 | tf_op jit(solution)/shard_map/reduce_sum | solution.py:71
  190.7 29.6 %all_to_all.70 = f32[4,128,1024]{2,1,0:T(8,128)} all-to-all(f32[4,128,1024]{2,1,0:T(8,128)} %bitcast.48), channel_id=1, replica_groups=mesh['y'=4,'zh'=4,'zl'=2,'x'=4,'core'=2] {'x'}, dimensions={0} | all-to-all | bytes 4194304 | tf_op jit(solution)/shard_map/all_to_all | solution.py:71
  220.3 2.6 %reduce_sum.117 = f32[128,1024]{1,0:T(8,128)} reduce(f32[4,128,1024]{2,1,0:T(8,128)} %all_to_all.70, f32[]{:T(128)} %constant.41.clone.1), dimensions={0}, to_apply=%region_9.10 | reduce | flops 393216 | bytes 2621444 | tf_op jit(solution)/shard_map/reduce_sum | solution.py:71
  222.9 3.5 %all-to-all-start.12 = ((f32[2,64,1024]{2,1,0:T(8,128)}), f32[2,64,1024]{2,1,0:T(8,128)S(1)}, u32[]{:S(2)}, u32[]{:S(2)}) async-start(f32[2,64,1024]{2,1,0:T(8,128)} %bitcast.20), calls=%async_computation.12 | async-start | bytes 1048576 | tf_op jit(solution)/shard_map/all_to_all | solution.py:71
  226.4 0.8 copy.97
  227.2 6.1 %all-to-all-done.12 = f32[2,64,1024]{2,1,0:T(8,128)S(1)} async-done(((f32[2,64,1024]{2,1,0:T(8,128)}), f32[2,64,1024]{2,1,0:T(8,128)S(1)}, u32[]{:S(2)}, u32[]{:S(2)}) %all-to-all-start.12) | async-done | bytes 524320 | tf_op jit(solution)/shard_map/all_to_all | solution.py:71
  233.3 1.6 add_convert_fusion
  (41 shorter events, 0.5 us)
Async XLA Ops:
  0.6 1.6 copy-start
  4.5 11.4 %copy-start.5 = (s32[384]{0:T(512)S(1)}, s32[384]{0:T(512)}, u32[]{:S(2)}) copy-start(s32[384]{0:T(512)} %param.15) | copy-start | bytes 4612
  10.6 13.0 %all-to-all-start.1 = ((bf16[4,64,1024]{2,1,0:T(8,128)(2,1)}), bf16[4,64,1024]{2,1,0:T(8,128)(2,1)S(1)}, u32[]{:S(2)}, u32[]{:S(2)}) async-start(bf16[4,64,1024]{2,1,0:T(8,128)(2,1)} %bitcast.55), calls=%async_computation.1 | async-start | bytes 1048576 | tf_op jit(solution)/shard_map/all_to_all | solution.py:71
  15.9 2.7 %copy-start.4 = (f32[24,1024]{1,0:T(8,128)S(1)}, f32[24,1024]{1,0:T(8,128)}, u32[]{:S(2)}) copy-start(f32[24,1024]{1,0:T(8,128)} %param.10) | copy-start | bytes 294916
  15.9 2.7 %copy-start.7 = (s32[1024]{0:T(1024)S(1)}, s32[1024]{0:T(1024)}, u32[]{:S(2)}) copy-start(s32[1024]{0:T(1024)} %param.11) | copy-start | bytes 12292
  24.3 6.7 %all-to-all-start.2 = ((bf16[2,32,1024]{2,1,0:T(8,128)(2,1)}), bf16[2,32,1024]{2,1,0:T(8,128)(2,1)S(1)}, u32[]{:S(2)}, u32[]{:S(2)}) async-start(bf16[2,32,1024]{2,1,0:T(8,128)(2,1)} %bitcast.4), calls=%async_computation.2 | async-start | bytes 262144 | tf_op jit(solution)/shard_map/all_to_all | solution.py:71
  28.9 4.7 %copy-start.1 = (bf16[384,1024]{1,0:T(8,128)(2,1)}, bf16[384,1024]{1,0:T(8,128)(2,1)S(1)}, u32[]{:S(2)}) copy-start(bf16[384,1024]{1,0:T(8,128)(2,1)S(1)} %broadcast_select_fusion) | copy-start | bytes 2359300
  56.8 10.8 %copy-start.9 = (f32[384]{0:T(512)S(1)}, f32[384]{0:T(512)}, u32[]{:S(2)}) copy-start(f32[384]{0:T(512)} %param.14) | copy-start | bytes 4612
  56.8 10.8 %copy-start.3 = (f32[384,512]{1,0:T(8,128)S(1)}, f32[384,512]{1,0:T(8,128)}, u32[]{:S(2)}) copy-start(f32[384,512]{1,0:T(8,128)} %param.13) | copy-start | bytes 2359300
  59.4 30.6 %copy-start.6 = (s32[512]{0:T(512)S(1)}, s32[512]{0:T(512)}, u32[]{:S(2)}) copy-start(s32[512]{0:T(512)} %param.16) | copy-start | bytes 6148
  59.5 18.1 %all-to-all-start.4 = ((f32[4,64,416]{2,1,0:T(8,128)}), f32[4,64,416]{2,1,0:T(8,128)S(1)}, u32[]{:S(2)}, u32[]{:S(2)}) async-start(f32[4,64,416]{2,1,0:T(8,128)} %bitcast.5), calls=%async_computation.4 | async-start | bytes 1048576 | tf_op jit(solution)/shard_map/all_to_all | solution.py:71
  78.6 16.1 %all-to-all-start.5 = ((f32[16,1,2048]{2,1,0:T(1,128)}), f32[16,1,2048]{2,1,0:T(1,128)S(1)}, u32[]{:S(2)}, u32[]{:S(2)}) async-start(f32[16,1,2048]{2,1,0:T(1,128)} %reshape.108), calls=%async_computation.5 | async-start | bytes 262144 | tf_op jit(solution)/shard_map/all_to_all | solution.py:76
  118.5 13.4 %all-to-all-start.6 = ((f32[16,72,32]{1,2,0:T(8,128)}), f32[16,72,32]{1,2,0:T(8,128)S(1)}, u32[]{:S(2)}, u32[]{:S(2)}) async-start(f32[16,72,32]{1,2,0:T(8,128)} %maximum_bitcast_fusion), calls=%async_computation.6 | async-start | bytes 524288 | tf_op jit(solution)/shard_map/all_to_all | solution.py:148
  132.9 10.4 %all-to-all-start.7 = ((f32[16,1,2048]{2,1,0:T(1,128)}), f32[16,1,2048]{2,1,0:T(1,128)S(1)}, u32[]{:S(2)}, u32[]{:S(2)}) async-start(f32[16,1,2048]{2,1,0:T(1,128)} %reshape.110), calls=%async_computation.7 | async-start | bytes 262144 | tf_op jit(solution)/shard_map/all_to_all | solution.py:76
  173.4 1.1 copy-start.2
  220.3 13.0 %copy-start.8 = (f32[1024]{0:T(1024)S(1)}, f32[1024]{0:T(1024)}, u32[]{:S(2)}) copy-start(f32[1024]{0:T(1024)} %param.17) | copy-start | bytes 12292
  222.9 10.3 %all-to-all-start.12 = ((f32[2,64,1024]{2,1,0:T(8,128)}), f32[2,64,1024]{2,1,0:T(8,128)S(1)}, u32[]{:S(2)}, u32[]{:S(2)}) async-start(f32[2,64,1024]{2,1,0:T(8,128)} %bitcast.20), calls=%async_computation.12 | async-start | bytes 1048576 | tf_op jit(solution)/shard_map/all_to_all | solution.py:71

commit v14 on v7

--- a/solution.py
+++ b/solution.py
@@ -14,7 +14,7 @@
 def penalty_slopes(base, outflow, lodf, limits):
     scen_rows, monitor_count = base.shape
     outage_total = outflow.shape[1]
-    sb = 8
+    sb = 16
     ch = 16
     lanes = 128
     blocks = scen_rows // sb

time: 237 us -> 237 us (level)
  transfers between devices with their start and end apart: 6 -> 6, of which waited for: 5 -> 5; matrix products, arithmetic and copies ran while one was open for 10% -> 9% of each run, Pallas kernels for 0% -> 0%
where the time goes in v14:
time: 237 us; the launch traced here: 233 us
  blocking collectives  92.8 us (39%)
  starting transfers between devices  34.9 us (15%)
  waiting for transfers between devices  31.6 us (13%)
  other arithmetic  27.5 us (12%)
  Pallas kernels  19.7 us (8%)
  local copies, waits for them, and re-layouts  16 us (7%)
  matrix products  9.46 us (4%)
    all_to_all x3, blocking collectives, exchange_sum(): return jnp.sum(lax.all_to_all(blocks, axis, 0, 0, tiled=False), axis=0)  66.2 us
    all_to_all x2, blocking collectives, gather_rows(): gathered = lax.all_to_all(copies, axis, 0, 0, tiled=False)  26.6 us
    all_to_all x3, waiting for transfers between devices, exchange_sum(): return jnp.sum(lax.all_to_all(blocks, axis, 0, 0, tiled=False), axis=0)  25.1 us
    pallas_call x1, Pallas kernels, penalty_slopes(): pl.pallas_call(kernel, grid=(blocks,), in_specs=[pl.BlockSpec((None, moni...  19.7 us
    all_to_all x3, starting transfers between devices, exchange_sum(): return jnp.sum(lax.all_to_all(blocks, axis, 0, 0, tiled=False), axis=0)  17.3 us
    all_to_all x2, starting transfers between devices, gather_columns(): gathered = lax.all_to_all(copies, axis, 0, 0, tiled=False)  12.1 us
    reduce_sum x6, other arithmetic, exchange_sum(): return jnp.sum(lax.all_to_all(blocks, axis, 0, 0, tiled=False), axis=0)  8.66 us
    reduce_sum x1, other arithmetic, penalty_slopes(): direct = jnp.sum(direct_lanes, axis=2) / (2.0 * outage_total)  7.89 us
  transfers between devices with their start and end apart: 6, of which 5 were waited for; matrix products, arithmetic and copies ran while one was open for 9% of the time, Pallas kernels for 0%

profile of v14, /device:TPU:7, one launch (start us, length us, event | category | flops | bytes accessed | tf_op | source)
XLA Modules:
  0.0 232.9 jit_solution(2319802033972452219)
XLA Ops:
  0.6 0.0 copy-start
  0.7 0.8 compare_and_fusion
  1.5 0.1 broadcast_in_dim.92
  1.6 0.1 broadcast_in_dim.94
  1.7 0.6 copy-done
  2.2 2.0 gather_fusion.1
  4.3 1.2 select_select_fusion
  5.5 6.4 %all-to-all-start = ((bf16[16,32,1024]{2,1,0:T(8,128)(2,1)}), bf16[16,32,1024]{2,1,0:T(8,128)(2,1)S(1)}, u32[]{:S(2)}, u32[]{:S(2)}) async-start(bf16[16,32,1024]{2,1,0:T(8,128)(2,1)} %select_select_fusion), calls=%async_computation | async-start | bytes 2097152 | tf_op jit(solution)/shard_map/all_to_all | solution.py:71
  12.0 2.7 %gather_fusion = bf16[384,1024]{1,0:T(8,128)(2,1)} fusion(bf16[1024,1024]{1,0:T(8,128)(2,1)S(1)} %copy-done, s32[1024]{0:T(1024)S(1)} %pad_clamp_fusion.1), kind=kCustom, calls=%fused_computation | custom fusion | bytes 1574400 | tf_op jit(solution)/shard_map/jit(_take)/gather | solution.py:120
  14.7 2.1 broadcast_select_fusion
  16.9 4.9 %subtract_convert_fusion = bf16[1024,1024]{1,0:T(8,128)(2,1)} fusion(bf16[1024,1024]{1,0:T(8,128)(2,1)} %param.9, f32[24,1024]{1,0:T(8,128)S(1)} %copy-done.3, s32[1024]{0:T(1024)S(1)} %copy-done.6), kind=kOutput, calls=%fused_computation.2 | convolution fusion | flops 305160192 | bytes 4296704 | tf_op jit(solution)/shard_map/dot_general | solution.py:102
  21.7 5.2 %all-to-all-done = bf16[16,32,1024]{2,1,0:T(8,128)(2,1)S(1)} async-done(((bf16[16,32,1024]{2,1,0:T(8,128)(2,1)}), bf16[16,32,1024]{2,1,0:T(8,128)(2,1)S(1)}, u32[]{:S(2)}, u32[]{:S(2)}) %all-to-all-start) | async-done | bytes 1048608 | tf_op jit(solution)/shard_map/all_to_all | solution.py:71
  26.9 0.2 reduce_sum.84
  27.1 2.8 %fusion.5 = f32[1024,416]{0,1:T(8,128)S(1)} fusion(bf16[1024,1024]{1,0:T(8,128)(2,1)} %subtract_convert_fusion, bf16[32,1024]{1,0:T(8,128)(2,1)S(1)} %reduce_sum.84, bf16[384,1024]{1,0:T(8,128)(2,1)} %broadcast_select_fusion), kind=kOutput, calls=%fused_computation.14 | convolution fusion | flops 874119168 | bytes 4653056 | tf_op jit(solution)/shard_map/dot_general | solution.py:123
  29.9 0.2 copy.88
  30.1 25.9 %all_to_all.55 = f32[4,256,416]{1,2,0:T(8,128)} all-to-all(f32[4,256,416]{1,2,0:T(8,128)S(1)} %bitcast.43), channel_id=1, replica_groups=mesh['y'=4,'zh'=4,'zl'=2,'x'=4,'core'=2] {'y'}, dimensions={0} | all-to-all | bytes 3407872 | tf_op jit(solution)/shard_map/all_to_all | solution.py:71
  56.0 1.7 reduce_sum.85
  57.7 1.0 copy.68
  58.7 7.4 %all-to-all-start.2 = ((f32[4,64,416]{2,1,0:T(8,128)}), f32[4,64,416]{2,1,0:T(8,128)S(1)}, u32[]{:S(2)}, u32[]{:S(2)}) async-start(f32[4,64,416]{2,1,0:T(8,128)} %bitcast.1), calls=%async_computation.2 | async-start | bytes 1048576 | tf_op jit(solution)/shard_map/all_to_all | solution.py:71
  66.1 1.0 broadcast_multiply_fusion.lodf_ref
  67.1 13.9 %all-to-all-done.2 = f32[4,64,416]{2,1,0:T(8,128)S(1)} async-done(((f32[4,64,416]{2,1,0:T(8,128)}), f32[4,64,416]{2,1,0:T(8,128)S(1)}, u32[]{:S(2)}, u32[]{:S(2)}) %all-to-all-start.2) | async-done | bytes 426016 | tf_op jit(solution)/shard_map/all_to_all | solution.py:71
  81.1 0.1 copy.70
  81.2 0.8 reshape.100
  82.0 6.3 %all-to-all-start.3 = ((f32[16,1,2048]{2,1,0:T(1,128)}), f32[16,1,2048]{2,1,0:T(1,128)S(1)}, u32[]{:S(2)}, u32[]{:S(2)}) async-start(f32[16,1,2048]{2,1,0:T(1,128)} %reshape.100), calls=%async_computation.3 | async-start | bytes 262144 | tf_op jit(solution)/shard_map/all_to_all | solution.py:76
  88.3 0.2 fusion.4
  88.6 0.8 reshape.98.lim_ref
  89.4 0.2 concatenate.19
  89.6 0.1 pad.4.clone
  89.7 1.2 copy.69
  90.8 2.1 all-to-all-done.3
  93.0 0.5 broadcast.43
  93.5 0.9 reduce.3
  94.4 0.1 reshape.101
  94.6 0.8 copy.71.out_ref
  95.3 19.7 %shard_map.112 = (f32[64,384,128]{2,1,0:T(8,128)}, f32[64,512]{1,0:T(8,128)}) custom-call(f32[4,384,16]{2,1,0:T(8,128)} %bitcast.47, f32[64,512]{1,0:T(8,128)} %copy.71.out_ref, f32[384,512]{1,0:T(8,128)} %broadcast_multiply_fusion.lodf_ref, f32[384,1]{1,0:T(8,128)} %reshape.98.lim_ref), custom_call_target="tpu_custom_call" | custom-call | tf_op jit(solution)/shard_map/pallas_call | solution.py:47
  115.0 0.9 broadcast_multiply_fusion.3
  115.9 0.1 copy.73
  116.0 0.9 maximum_bitcast_fusion
  116.9 5.5 %all-to-all-start.4 = ((f32[16,72,32]{1,2,0:T(8,128)}), f32[16,72,32]{1,2,0:T(8,128)S(1)}, u32[]{:S(2)}, u32[]{:S(2)}) async-start(f32[16,72,32]{1,2,0:T(8,128)} %maximum_bitcast_fusion), calls=%async_computation.4 | async-start | bytes 524288 | tf_op jit(solution)/shard_map/all_to_all | solution.py:141
  122.4 7.9 %reduce_sum.87 = f32[64,384]{1,0:T(8,128)S(1)} reduce(f32[64,384,128]{2,1,0:T(8,128)} %get-tuple-element.5, f32[]{:T(128)} %constant.39.clone.1), dimensions={2}, to_apply=%region_3.4 | reduce | flops 3121152 | bytes 12681220 | tf_op jit(solution)/shard_map/reduce_sum | solution.py:65
  130.3 0.8 reshape.102
  131.2 5.8 %all-to-all-start.5 = ((f32[16,1,2048]{2,1,0:T(1,128)}), f32[16,1,2048]{2,1,0:T(1,128)S(1)}, u32[]{:S(2)}, u32[]{:S(2)}) async-start(f32[16,1,2048]{2,1,0:T(1,128)} %reshape.102), calls=%async_computation.5 | async-start | bytes 262144 | tf_op jit(solution)/shard_map/all_to_all | solution.py:76
  136.9 0.2 fusion.9
  137.1 0.1 copy.85
  137.2 4.4 %all-to-all-done.5 = f32[16,1,2048]{2,1,0:T(1,128)S(1)} async-done(((f32[16,1,2048]{2,1,0:T(1,128)}), f32[16,1,2048]{2,1,0:T(1,128)S(1)}, u32[]{:S(2)}, u32[]{:S(2)}) %all-to-all-start.5) | async-done | bytes 131104 | tf_op jit(solution)/shard_map/all_to_all | solution.py:76
  141.6 0.9 reduce.4
  142.5 0.1 reshape.103
  142.7 0.5 fusion
  143.2 12.4 %all_to_all.56 = bf16[4,64,416]{2,1,0:T(8,128)(2,1)S(1)} all-to-all(bf16[4,64,416]{2,1,0:T(8,128)(2,1)S(1)} %broadcast_in_dim.105), channel_id=1, replica_groups=mesh['y'=4,'zh'=4,'zl'=2,'x'=4,'core'=2] {'zh'}, dimensions={0} | all-to-all | bytes 425984 | tf_op jit(solution)/shard_map/all_to_all | solution.py:83
  155.7 0.1 copy.77
  155.8 0.1 broadcast_in_dim.107
  155.9 14.1 %all_to_all.57 = bf16[4,256,416]{1,2,0:T(8,128)(2,1)} all-to-all(bf16[4,256,416]{1,2,0:T(8,128)(2,1)S(1)} %broadcast_in_dim.107), channel_id=1, replica_groups=mesh['y'=4,'zh'=4,'zl'=2,'x'=4,'core'=2] {'y'}, dimensions={0} | all-to-all | bytes 1703936 | tf_op jit(solution)/shard_map/all_to_all | solution.py:83
  170.0 1.4 copy.78
  171.5 0.1 copy.79
  171.6 1.0 copy-done.1
  172.6 1.2 fusion.2
  173.9 10.7 %all_to_all.58 = f32[2,512,1024]{2,1,0:T(8,128)} all-to-all(f32[2,512,1024]{2,1,0:T(8,128)S(1)} %fusion.2), channel_id=1, replica_groups=mesh['y'=4,'zh'=4,'zl'=2,'x'=4,'core'=2] {'core'}, dimensions={0} | all-to-all | bytes 8388608 | tf_op jit(solution)/shard_map/all_to_all | solution.py:71
  184.6 4.1 %reduce_sum.90 = f32[512,1024]{1,0:T(8,128)} reduce(f32[2,512,1024]{2,1,0:T(8,128)} %all_to_all.58, f32[]{:T(128)} %constant.39.clone.1), dimensions={0}, to_apply=%region_6.7 | reduce | flops 524288 | bytes 6291460 | tf_op jit(solution)/shard_map/reduce_sum | solution.py:71
  188.7 29.6 %all_to_all.59 = f32[4,128,1024]{2,1,0:T(8,128)} all-to-all(f32[4,128,1024]{2,1,0:T(8,128)} %bitcast.42), channel_id=1, replica_groups=mesh['y'=4,'zh'=4,'zl'=2,'x'=4,'core'=2] {'x'}, dimensions={0} | all-to-all | bytes 4194304 | tf_op jit(solution)/shard_map/all_to_all | solution.py:71
  218.3 2.6 %reduce_sum.91 = f32[128,1024]{1,0:T(8,128)} reduce(f32[4,128,1024]{2,1,0:T(8,128)} %all_to_all.59, f32[]{:T(128)} %constant.39.clone.1), dimensions={0}, to_apply=%region_7.8 | reduce | flops 393216 | bytes 2621444 | tf_op jit(solution)/shard_map/reduce_sum | solution.py:71
  220.9 3.5 %all-to-all-start.10 = ((f32[2,64,1024]{2,1,0:T(8,128)}), f32[2,64,1024]{2,1,0:T(8,128)S(1)}, u32[]{:S(2)}, u32[]{:S(2)}) async-start(f32[2,64,1024]{2,1,0:T(8,128)} %bitcast.16), calls=%async_computation.10 | async-start | bytes 1048576 | tf_op jit(solution)/shard_map/all_to_all | solution.py:71
  224.4 0.8 copy.82
  225.2 6.1 %all-to-all-done.10 = f32[2,64,1024]{2,1,0:T(8,128)S(1)} async-done(((f32[2,64,1024]{2,1,0:T(8,128)}), f32[2,64,1024]{2,1,0:T(8,128)S(1)}, u32[]{:S(2)}, u32[]{:S(2)}) %all-to-all-start.10) | async-done | bytes 524320 | tf_op jit(solution)/shard_map/all_to_all | solution.py:71
  231.3 1.6 add_convert_fusion
  (32 shorter events, 0.3 us)
Async XLA Ops:
  0.6 1.6 copy-start
  4.3 7.7 %copy-start.4 = (s32[384]{0:T(512)S(1)}, s32[384]{0:T(512)}, u32[]{:S(2)}) copy-start(s32[384]{0:T(512)} %param.15) | copy-start | bytes 4612
  5.5 21.4 %all-to-all-start = ((bf16[16,32,1024]{2,1,0:T(8,128)(2,1)}), bf16[16,32,1024]{2,1,0:T(8,128)(2,1)S(1)}, u32[]{:S(2)}, u32[]{:S(2)}) async-start(bf16[16,32,1024]{2,1,0:T(8,128)(2,1)} %select_select_fusion), calls=%async_computation | async-start | bytes 2097152 | tf_op jit(solution)/shard_map/all_to_all | solution.py:71
  12.0 4.9 %copy-start.3 = (f32[24,1024]{1,0:T(8,128)S(1)}, f32[24,1024]{1,0:T(8,128)}, u32[]{:S(2)}) copy-start(f32[24,1024]{1,0:T(8,128)} %param.10) | copy-start | bytes 294916
  12.0 4.9 %copy-start.6 = (s32[1024]{0:T(1024)S(1)}, s32[1024]{0:T(1024)}, u32[]{:S(2)}) copy-start(s32[1024]{0:T(1024)} %param.11) | copy-start | bytes 12292
  56.0 10.1 %copy-start.8 = (f32[384]{0:T(512)S(1)}, f32[384]{0:T(512)}, u32[]{:S(2)}) copy-start(f32[384]{0:T(512)} %param.14) | copy-start | bytes 4612
  56.0 10.1 %copy-start.2 = (f32[384,512]{1,0:T(8,128)S(1)}, f32[384,512]{1,0:T(8,128)}, u32[]{:S(2)}) copy-start(f32[384,512]{1,0:T(8,128)} %param.13) | copy-start | bytes 2359300
  58.7 29.6 %copy-start.5 = (s32[512]{0:T(512)S(1)}, s32[512]{0:T(512)}, u32[]{:S(2)}) copy-start(s32[512]{0:T(512)} %param.16) | copy-start | bytes 6148
  58.7 22.3 %all-to-all-start.2 = ((f32[4,64,416]{2,1,0:T(8,128)}), f32[4,64,416]{2,1,0:T(8,128)S(1)}, u32[]{:S(2)}, u32[]{:S(2)}) async-start(f32[4,64,416]{2,1,0:T(8,128)} %bitcast.1), calls=%async_computation.2 | async-start | bytes 1048576 | tf_op jit(solution)/shard_map/all_to_all | solution.py:71
  82.0 11.0 %all-to-all-start.3 = ((f32[16,1,2048]{2,1,0:T(1,128)}), f32[16,1,2048]{2,1,0:T(1,128)S(1)}, u32[]{:S(2)}, u32[]{:S(2)}) async-start(f32[16,1,2048]{2,1,0:T(1,128)} %reshape.100), calls=%async_computation.3 | async-start | bytes 262144 | tf_op jit(solution)/shard_map/all_to_all | solution.py:76
  116.9 13.4 %all-to-all-start.4 = ((f32[16,72,32]{1,2,0:T(8,128)}), f32[16,72,32]{1,2,0:T(8,128)S(1)}, u32[]{:S(2)}, u32[]{:S(2)}) async-start(f32[16,72,32]{1,2,0:T(8,128)} %maximum_bitcast_fusion), calls=%async_computation.4 | async-start | bytes 524288 | tf_op jit(solution)/shard_map/all_to_all | solution.py:141
  131.2 10.4 %all-to-all-start.5 = ((f32[16,1,2048]{2,1,0:T(1,128)}), f32[16,1,2048]{2,1,0:T(1,128)S(1)}, u32[]{:S(2)}, u32[]{:S(2)}) async-start(f32[16,1,2048]{2,1,0:T(1,128)} %reshape.102), calls=%async_computation.5 | async-start | bytes 262144 | tf_op jit(solution)/shard_map/all_to_all | solution.py:76
  171.5 1.1 copy-start.1
  218.3 13.0 %copy-start.7 = (f32[1024]{0:T(1024)S(1)}, f32[1024]{0:T(1024)}, u32[]{:S(2)}) copy-start(f32[1024]{0:T(1024)} %param.17) | copy-start | bytes 12292
  220.9 10.3 %all-to-all-start.10 = ((f32[2,64,1024]{2,1,0:T(8,128)}), f32[2,64,1024]{2,1,0:T(8,128)S(1)}, u32[]{:S(2)}, u32[]{:S(2)}) async-start(f32[2,64,1024]{2,1,0:T(8,128)} %bitcast.16), calls=%async_computation.10 | async-start | bytes 1048576 | tf_op jit(solution)/shard_map/all_to_all | solution.py:71
